TPU v7x, 512 devices: a whole 4x8x8 slice. The times are simulated.
512 devices in a mesh: dp: 8 (over z), expert: 64 (over y, x, core).
Axes of the slice: x: 4, y: 8, z: 8, core: 2. Of those that a mesh axis runs over, the one named last changes fastest.
Arguments:
- tokens: bfloat16 [65536, 1024], P(('dp', 'expert')), may hold values from -6 to 6
- expert_ids: int32 [65536, 4], P(('dp', 'expert')), may hold values from 0 to 63, all different within a row; in each aligned block of 128 rows (0 to 127, 128 to 255, ...) at most 16 rows name the same one
- gate_probs: float32 [65536, 4], P(('dp', 'expert')), may hold values from 0.05 to 1
- gate_up: bfloat16 [64, 1024, 768], P('expert', 'dp'), may hold values from -0.1875 to 0.1875
- down_proj: bfloat16 [64, 384, 1024], P('expert', None, 'dp'), may hold values from -0.3125 to 0.3125
- cotangent: bfloat16 [65536, 1024], P(('dp', 'expert')), may hold values from -0.75 to 0.75
Outputs:
- moe_out: bfloat16 [65536, 1024], P(('dp', 'expert'))
- token_grads: bfloat16 [65536, 1024], P(('dp', 'expert'))
- gate_grads: float32 [65536, 4], P(('dp', 'expert'))
- gate_up_grads: float32 [64, 1024, 768], P('expert', 'dp')
- down_grads: float32 [64, 384, 1024], P('expert', None, 'dp')
Inputs may be any that keep to these rules, and one draw needn't show every extreme that they name: `expert_ids`: each row names 4 different experts. Among the rows of one device no expert is named more than 16 times, and in every draw some device names some expert exactly 16 times.
All inputs are finite; a program needn't handle non-finite values.
Results may differ from a plain program's by a relative error of at most 0.012.
Values may be sent and summed in bfloat16 or wider, within the bound.
No kernel may reach another device: no remote copies, remote signals or barrier semaphores. Data moves between devices by JAX's collectives and lax.ppermute only.
A program may use at most 64 MiB of HBM per device.

v0:
```python
import jax
import jax.numpy as jnp
from jax import lax
from jax.sharding import PartitionSpec as P


def forward_rows(rows_in, weight_in, weight_out):
    hidden_width = weight_out.shape[0]
    pre_act = jnp.dot(rows_in, weight_in, preferred_element_type=jnp.float32)
    hidden = (jax.nn.silu(pre_act[:, :hidden_width]) * pre_act[:, hidden_width:]).astype(
        jnp.bfloat16
    )
    expert_out = jnp.dot(hidden, weight_out, preferred_element_type=jnp.float32).astype(
        jnp.bfloat16
    )
    return (expert_out, pre_act, hidden)


def backward_rows(rows_in, grad_rows, pre_act, hidden, weight_in, weight_out):
    hidden_width = weight_out.shape[0]
    contract_last = (((1,), (1,)), ((), ()))
    contract_first = (((0,), (0,)), ((), ()))
    grad_hidden = lax.dot_general(
        grad_rows, weight_out, contract_last, preferred_element_type=jnp.float32
    )
    pre_gate = pre_act[:, :hidden_width]
    sigmoid_value = jax.nn.sigmoid(pre_gate)
    grad_gate = (
        grad_hidden
        * pre_act[:, hidden_width:]
        * sigmoid_value
        * (1.0 + pre_gate * (1.0 - sigmoid_value))
    )
    grad_up = grad_hidden * jax.nn.silu(pre_gate)
    grad_pre = jnp.concatenate([grad_gate, grad_up], axis=1).astype(jnp.bfloat16)
    grad_in = lax.dot_general(
        grad_pre, weight_in, contract_last, preferred_element_type=jnp.float32
    ).astype(jnp.bfloat16)
    weight_in_grad = lax.dot_general(
        rows_in, grad_pre, contract_first, preferred_element_type=jnp.float32
    )
    weight_out_grad = lax.dot_general(
        hidden, grad_rows, contract_first, preferred_element_type=jnp.float32
    )
    return (grad_in, weight_in_grad, weight_out_grad)


def live_slots(recv_counts, capacity):
    within = jnp.arange(capacity, dtype=jnp.int32)[None, :] < recv_counts[:, None]
    return within.reshape(-1)


def expert_forward(rows_in, filled, weight_in, weight_out):
    zero_row = jnp.zeros((), jnp.bfloat16)
    expert_out, pre_act, hidden = forward_rows(rows_in, weight_in, weight_out)
    expert_out = jnp.where(filled[:, None], expert_out, zero_row)
    stored = (rows_in, pre_act, hidden, None)
    return (expert_out, stored)


def expert_backward(grads_in, filled, stored, weight_in, weight_out):
    zero_row = jnp.zeros((), jnp.bfloat16)
    rows_in, pre_act, hidden, unused_plan = stored
    grad_back, in_grad, out_grad = backward_rows(
        rows_in, grads_in, pre_act, hidden, weight_in, weight_out
    )
    grad_back = jnp.where(filled[:, None], grad_back, zero_row)
    return (grad_back, in_grad, out_grad)


def local(tokens, expert_ids, gate_probs, gate_up, down_proj, cotangent):
    token_count, top_count = expert_ids.shape
    expert_count = lax.axis_size("expert")
    capacity = 2 * token_count * top_count // expert_count
    route_count = token_count * top_count
    slot_count = expert_count * capacity
    flat_ids = expert_ids.reshape(route_count)
    onehot = (flat_ids[:, None] == jnp.arange(expert_count, dtype=jnp.int32)[None, :]).astype(
        jnp.int32
    )
    slot_index = jnp.sum((jnp.cumsum(onehot, axis=0) - onehot) * onehot, axis=1)
    position = flat_ids * capacity + slot_index
    counts = jnp.sum(onehot, axis=0)
    slot_range = jnp.arange(slot_count, dtype=jnp.int32)
    matches = position[None, :] == slot_range[:, None]
    route_of_slot = jnp.sum(
        jnp.where(matches, jnp.arange(route_count, dtype=jnp.int32)[None, :], 0), axis=1
    )
    slot_filled = jnp.any(matches, axis=1)
    token_of_slot = route_of_slot // top_count
    zero_row = jnp.zeros((), jnp.bfloat16)
    send_tokens = jnp.where(slot_filled[:, None], tokens[token_of_slot], zero_row)
    slot_probs = jnp.where(slot_filled, gate_probs.reshape(route_count)[route_of_slot], 0.0)
    send_grads = (slot_probs[:, None] * cotangent[token_of_slot].astype(jnp.float32)).astype(
        jnp.bfloat16
    )
    weight_in, weight_out = (
        lax.all_gather(gate_up, "dp", axis=1, tiled=True),
        lax.all_gather(down_proj, "dp", axis=2, tiled=True),
    )
    weight_in = weight_in[0]
    weight_out = weight_out[0]
    rows_in, recv_counts = (
        lax.all_to_all(send_tokens, "expert", split_axis=0, concat_axis=0, tiled=True),
        lax.all_to_all(counts, "expert", split_axis=0, concat_axis=0, tiled=True),
    )
    filled = live_slots(recv_counts, capacity)
    expert_out, stored = expert_forward(rows_in, filled, weight_in, weight_out)
    back_out = lax.all_to_all(expert_out, "expert", split_axis=0, concat_axis=0, tiled=True)
    grads_in = lax.all_to_all(send_grads, "expert", split_axis=0, concat_axis=0, tiled=True)
    grad_back, in_grad, out_grad = expert_backward(grads_in, filled, stored, weight_in, weight_out)
    back_grad = lax.all_to_all(grad_back, "expert", split_axis=0, concat_axis=0, tiled=True)
    sum_in, sum_out = (
        lax.psum_scatter(
            in_grad[None].astype(jnp.bfloat16), "dp", scatter_dimension=1, tiled=True
        ).astype(jnp.float32),
        lax.psum_scatter(
            out_grad[None].astype(jnp.bfloat16), "dp", scatter_dimension=2, tiled=True
        ).astype(jnp.float32),
    )
    out_routes = back_out[position].reshape(token_count, top_count, -1).astype(jnp.float32)
    moe_out = jnp.sum(gate_probs[:, :, None] * out_routes, axis=1).astype(jnp.bfloat16)
    gate_grads = jnp.sum(cotangent.astype(jnp.float32)[:, None, :] * out_routes, axis=2)
    grad_routes = back_grad[position].reshape(token_count, top_count, -1).astype(jnp.float32)
    token_grads = jnp.sum(grad_routes, axis=1).astype(jnp.bfloat16)
    return (moe_out, token_grads, gate_grads, sum_in, sum_out)


def solution(mesh):
    return jax.shard_map(
        local,
        mesh=mesh,
        in_specs=(
            P(("dp", "expert"), None),
            P(("dp", "expert"), None),
            P(("dp", "expert"), None),
            P("expert", "dp", None),
            P("expert", None, "dp"),
            P(("dp", "expert"), None),
        ),
        out_specs=(
            P(("dp", "expert"), None),
            P(("dp", "expert"), None),
            P(("dp", "expert"), None),
            P("expert", "dp", None),
            P("expert", None, "dp"),
        ),
        check_vma=False,
    )
```

profile of v0, /device:TPU:6, one launch (start us, length us, event | category | flops | bytes accessed | tf_op | source)
XLA Modules:
  0.0 300.0 jit_solution(8653985739572995588)
XLA Ops:
  7.2 0.0 copy-start
  7.2 0.8 copy.35
  8.0 0.1 eq.42
  8.1 0.1 eq.38
  8.2 1.2 reduce-window.6
  9.5 0.2 slice_reduce_fusion
  9.7 0.2 fusion.12
  9.9 0.7 copy.36
  10.6 10.6 %all-to-all-start = ((s32[64,1,1]{2,1,0:T(1,128)}), s32[64,1,1]{2,1,0:T(1,128)S(1)}, u32[]{:S(2)}, u32[]{:S(2)}) async-start(s32[64,1,1]{2,1,0:T(1,128)} %copy.36), calls=%async_computation | async-start | bytes 65536 | tf_op jit(solution)/shard_map/all_to_all | solution.py:105
  21.2 0.3 select_reduce_fusion
  21.5 0.3 fusion.1
  21.9 0.1 broadcast_in_dim.60
  22.0 4.1 %gather_fusion = bf16[1024,1024]{1,0:T(8,128)(2,1)S(1)} fusion(bf16[128,1024]{1,0:T(8,128)(2,1)S(1)} %copy-done, s32[1024]{0:T(1024)S(1)} %broadcast_clamp_fusion.1), kind=kCustom, calls=%fused_computation | custom fusion | bytes 4198400 | tf_op jit(solution)/shard_map/gather | solution.py:92
  26.0 1.6 broadcast_select_fusion
  27.6 1.4 all-to-all-done
  29.1 9.2 %all-to-all-start.1 = ((bf16[64,16,1024]{2,1,0:T(8,128)(2,1)}), bf16[64,16,1024]{2,1,0:T(8,128)(2,1)}, u32[]{:S(2)}, u32[]{:S(2)}) async-start(bf16[64,16,1024]{2,1,0:T(8,128)(2,1)} %broadcast_select_fusion), calls=%async_computation.1 | async-start | bytes 4194304 | tf_op jit(solution)/shard_map/all_to_all | solution.py:104
  38.2 0.1 copy.34
  38.4 0.1 reshape.204
  38.5 0.0 copy-start.1
  38.5 6.9 %gather_fusion.2 = f32[1024]{0:T(1024)S(1)} fusion(f32[512]{0:T(512)S(1)} %reshape.204, s32[1024]{0:T(1024)S(1)} %broadcast_clamp_fusion), kind=kCustom, calls=%fused_computation.2 | custom fusion | bytes 12288 | tf_op jit(solution)/shard_map/gather | solution.py:93
  45.4 0.1 gather.23
  45.4 4.1 %gather_fusion.3 = bf16[1024,1024]{1,0:T(8,128)(2,1)S(1)} fusion(bf16[128,1024]{1,0:T(8,128)(2,1)S(1)} %copy-done.1, s32[1024]{0:T(1024)S(1)} %broadcast_clamp_fusion.1), kind=kCustom, calls=%fused_computation.3 | custom fusion | bytes 4198400 | tf_op jit(solution)/shard_map/gather | solution.py:94
  49.5 1.8 fusion
  51.3 38.1 %all-to-all-done.1 = bf16[64,16,1024]{2,1,0:T(8,128)(2,1)} async-done(((bf16[64,16,1024]{2,1,0:T(8,128)(2,1)}), bf16[64,16,1024]{2,1,0:T(8,128)(2,1)}, u32[]{:S(2)}, u32[]{:S(2)}) %all-to-all-start.1) | async-done | bytes 2097184 | tf_op jit(solution)/shard_map/all_to_all | solution.py:104
  89.4 5.4 %all-to-all-start.3 = ((bf16[64,16,1024]{2,1,0:T(8,128)(2,1)}), bf16[64,16,1024]{2,1,0:T(8,128)(2,1)S(1)}, u32[]{:S(2)}, u32[]{:S(2)}) async-start(bf16[64,16,1024]{2,1,0:T(8,128)(2,1)} %fusion), calls=%async_computation.3 | async-start | bytes 4194304 | tf_op jit(solution)/shard_map/all_to_all | solution.py:110
  94.8 0.0 all-gather.2.cloned.1.call-start
  94.9 0.7 all-gather.2.cloned.1.call-update
  95.6 34.6 %all_gather.7 = bf16[1,384,1024]{2,1,0:T(8,128)(2,1)S(1)} all-gather(bf16[1,384,128]{2,1,0:T(8,128)(2,1)} %param.10), channel_id=1, replica_groups=mesh['dp'=8,'expert'=64] {'dp'}, dimensions={2}, use_global_device_ids=true | all-gather | bytes 884736 | tf_op jit(solution)/shard_map/all_gather | solution.py:99
  130.2 1.2 reduce.5
  131.4 0.1 iota_compare_fusion.3
  131.5 0.1 lt.50
  131.6 15.3 %all-gather.2.cloned.1.call-done = bf16[1,1024,768]{2,1,0:T(8,128)(2,1)} async-done(((bf16[1,128,768]{2,1,0:T(8,128)(2,1)}), bf16[1,1024,768]{2,1,0:T(8,128)(2,1)}) %all-gather.2.cloned.1.call-update) | async-done | bytes 1572880 | tf_op jit(solution)/shard_map/all_gather | solution.py:98
  146.9 5.5 %fusion.3 = f32[1024,768]{0,1:T(8,128)} fusion(bf16[1024,1024]{1,0:T(8,128)(2,1)} %bitcast.5, bf16[1,1024,768]{2,1,0:T(8,128)(2,1)} %all-gather.2.cloned.1.call-done), kind=kOutput, calls=%fused_computation.18 | convolution fusion | flops 1610612736 | bytes 6815744 | tf_op jit(solution)/shard_map/dot_general | solution.py:9
  152.4 0.0 all-to-all-done.3
  152.4 5.1 %multiply_convert_fusion.1 = (bf16[1024,384]{0,1:T(8,128)(2,1)S(1)}, bf16[1024,384]{0,1:T(8,128)(2,1)S(1)}, bf16[1024,384]{0,1:T(8,128)(2,1)}) fusion(f32[1024,768]{0,1:T(8,128)} %fusion.3, bf16[1024,1024]{1,0:T(8,128)(2,1)S(1)} %bitcast.60, bf16[1,384,1024]{2,1,0:T(8,128)(2,1)S(1)} %all_gather.7), kind=kOutput, calls=%fused_computation.21 | convolution fusion | flops 811204608 | bytes 8388608 | tf_op jit(solution)/shard_map/dot_general | solution.py:23
  157.5 3.3 %convert_select_fusion = bf16[1024,1024]{1,0:T(8,128)(2,1)} fusion(pred[1024]{0:T(1024)(128)(4,1)S(1)} %lt.50, bf16[1,1024,768]{2,1,0:T(8,128)(2,1)S(1)} %copy-done.6, bf16[1024,384]{0,1:T(8,128)(2,1)S(1)} %get-tuple-element.25, bf16[1024,384]{0,1:T(8,128)(2,1)S(1)} %get-tuple-element.24), kind=kOutput, calls=%fused_computation.8 | convolution fusion | flops 1615855616 | bytes 5243904 | tf_op jit(solution)/shard_map/dot_general | solution.py:36
  160.9 10.3 %all-to-all-start.4 = ((bf16[64,16,1024]{2,1,0:T(8,128)(2,1)}), bf16[64,16,1024]{2,1,0:T(8,128)(2,1)S(1)}, u32[]{:S(2)}, u32[]{:S(2)}) async-start(bf16[64,16,1024]{2,1,0:T(8,128)(2,1)} %bitcast.62), calls=%async_computation.4 | async-start | bytes 4194304 | tf_op jit(solution)/shard_map/all_to_all | solution.py:112
  171.1 0.0 reduce-scatter.7.cloned.1.call-start
  171.2 3.7 %fusion.7 = bf16[1,384,1024]{2,1,0:T(8,128)(2,1)} fusion(bf16[1024,384]{0,1:T(8,128)(2,1)} %get-tuple-element.26, bf16[1024,1024]{1,0:T(8,128)(2,1)} %bitcast.61), kind=kOutput, calls=%fused_computation.27 | convolution fusion | flops 805699584 | bytes 3670016 | tf_op jit(solution)/shard_map/dot_general | solution.py:42
  174.9 4.8 %copy.42 = bf16[1,384,1024]{1,0,2:T(2,128)(2,1)} copy(bf16[1,384,1024]{2,1,0:T(8,128)(2,1)} %fusion.7) | data formatting | bytes 1572864
  179.7 2.5 copy.48
  182.2 0.0 reduce-scatter.7.cloned.1.call-update
  182.2 3.8 %convert_select_fusion.1 = bf16[1024,1024]{1,0:T(8,128)(2,1)} fusion(pred[1024]{0:T(1024)(128)(4,1)S(1)} %lt.50, bf16[1024,384]{0,1:T(8,128)(2,1)} %get-tuple-element.26, bf16[1,384,1024]{2,1,0:T(8,128)(2,1)S(1)} %all_gather.7), kind=kOutput, calls=%fused_computation.10 | convolution fusion | flops 807403520 | bytes 3671040 | tf_op jit(solution)/shard_map/dot_general | solution.py:13
  186.0 36.4 %all-to-all-done.4 = bf16[64,16,1024]{2,1,0:T(8,128)(2,1)S(1)} async-done(((bf16[64,16,1024]{2,1,0:T(8,128)(2,1)}), bf16[64,16,1024]{2,1,0:T(8,128)(2,1)S(1)}, u32[]{:S(2)}, u32[]{:S(2)}) %all-to-all-start.4) | async-done | bytes 2097184 | tf_op jit(solution)/shard_map/all_to_all | solution.py:112
  222.4 5.7 %all-to-all-start.2 = ((bf16[64,16,1024]{2,1,0:T(8,128)(2,1)}), bf16[64,16,1024]{2,1,0:T(8,128)(2,1)}, u32[]{:S(2)}, u32[]{:S(2)}) async-start(bf16[64,16,1024]{2,1,0:T(8,128)(2,1)} %bitcast.59), calls=%async_computation.2 | async-start | bytes 4194304 | tf_op jit(solution)/shard_map/all_to_all | solution.py:109
  228.1 0.3 reduce-scatter.5.cloned.1.call-start
  228.4 4.9 %fusion.6 = bf16[1,1024,768]{2,1,0:T(8,128)(2,1)} fusion(bf16[1024,1024]{1,0:T(8,128)(2,1)} %bitcast.5, bf16[1024,384]{0,1:T(8,128)(2,1)} %copy-done.9, bf16[1024,384]{0,1:T(8,128)(2,1)S(1)} %copy-done.8), kind=kOutput, calls=%fused_computation.25 | convolution fusion | flops 1614544896 | bytes 5242880 | tf_op jit(solution)/shard_map/dot_general | solution.py:39
  233.3 0.0 reduce-scatter.5.cloned.1.call-update
  233.3 0.8 convert_element_type.75
  234.1 0.1 copy.39
  234.2 0.1 mul.87
  234.4 0.0 reduce-scatter.7.cloned.1.call-done
  234.4 1.0 reshape_bitcast_fusion
  235.4 0.2 copy.43
  235.6 0.7 convert_element_type.81
  236.3 38.7 %reduce-scatter.5.cloned.1.call-done = bf16[1,128,768]{2,1,0:T(8,128)(2,1)} async-done(((bf16[1,1024,768]{2,1,0:T(8,128)(2,1)}), bf16[1,128,768]{2,1,0:T(8,128)(2,1)}) %reduce-scatter.5.cloned.1.call-update) | async-done | bytes 196624 | tf_op jit(solution)/shard_map/reduce_scatter | solution.py:114
  275.0 1.7 convert_element_type.78
  276.7 2.8 gather_fusion.4
  279.5 2.3 reshape.205
  281.7 4.6 %gather_fusion.1 = bf16[512,1024]{1,0:T(8,128)(2,1)S(1)} fusion(bf16[1024,1024]{1,0:T(8,128)(2,1)} %bitcast.9, s32[1024]{0:T(1024)S(1)} %pad_clamp_fusion), kind=kCustom, calls=%fused_computation.1 | custom fusion | bytes 2099200 | tf_op jit(solution)/shard_map/gather | solution.py:121
  286.3 0.7 reshape.206
  287.0 3.7 %multiply_reduce_fusion = (f32[128,4]{1,0:T(8,128)S(1)}, bf16[128,1024]{1,0:T(8,128)(2,1)}) fusion(f32[128,4,1024]{2,1,0:T(4,128)S(1)} %reshape.206, f32[128,1024]{1,0:T(8,128)} %convert_element_type.75, f32[128,4]{1,0:T(8,128)S(1)} %copy.34), kind=kLoop, calls=%fused_computation.7 | loop fusion | flops 1965568 | bytes 2887680 | tf_op jit(solution)/shard_map/reduce_sum | solution.py:123
  290.7 0.7 copy.41
  291.4 2.1 reduce_sum.67
  (30 shorter events, 0.2 us)
Async XLA Ops:
  7.2 14.8 %copy-start = (bf16[128,1024]{1,0:T(8,128)(2,1)S(1)}, bf16[128,1024]{1,0:T(8,128)(2,1)}, u32[]{:S(2)}) copy-start(bf16[128,1024]{1,0:T(8,128)(2,1)} %param.6) | copy-start | bytes 786436
  10.6 18.4 %all-to-all-start = ((s32[64,1,1]{2,1,0:T(1,128)}), s32[64,1,1]{2,1,0:T(1,128)S(1)}, u32[]{:S(2)}, u32[]{:S(2)}) async-start(s32[64,1,1]{2,1,0:T(1,128)} %copy.36), calls=%async_computation | async-start | bytes 65536 | tf_op jit(solution)/shard_map/all_to_all | solution.py:105
  27.6 10.6 %copy-start.5 = (f32[128,4]{0,1:T(4,128)S(1)}, f32[128,4]{0,1:T(4,128)}, u32[]{:S(2)}) copy-start(f32[128,4]{0,1:T(4,128)} %param.8) | copy-start | bytes 6148
  29.1 60.4 %all-to-all-start.1 = ((bf16[64,16,1024]{2,1,0:T(8,128)(2,1)}), bf16[64,16,1024]{2,1,0:T(8,128)(2,1)}, u32[]{:S(2)}, u32[]{:S(2)}) async-start(bf16[64,16,1024]{2,1,0:T(8,128)(2,1)} %broadcast_select_fusion), calls=%async_computation.1 | async-start | bytes 4194304 | tf_op jit(solution)/shard_map/all_to_all | solution.py:104
  38.5 7.0 %copy-start.1 = (bf16[128,1024]{1,0:T(8,128)(2,1)S(1)}, bf16[128,1024]{1,0:T(8,128)(2,1)}, u32[]{:S(2)}) copy-start(bf16[128,1024]{1,0:T(8,128)(2,1)} %param.11) | copy-start | bytes 786436
  89.4 63.0 %all-to-all-start.3 = ((bf16[64,16,1024]{2,1,0:T(8,128)(2,1)}), bf16[64,16,1024]{2,1,0:T(8,128)(2,1)S(1)}, u32[]{:S(2)}, u32[]{:S(2)}) async-start(bf16[64,16,1024]{2,1,0:T(8,128)(2,1)} %fusion), calls=%async_computation.3 | async-start | bytes 4194304 | tf_op jit(solution)/shard_map/all_to_all | solution.py:110
  94.8 52.0 %all-gather.2.cloned.1.call-start = ((), (), s32[]{:S(2)}) async-start(), calls=%async_computation.7 | async-start | bytes 1769472 | tf_op jit(solution)/shard_map/all_gather | solution.py:98
  152.4 5.1 %copy-start.3 = (bf16[64,16,1024]{2,1,0:T(8,128)(2,1)}, bf16[64,16,1024]{2,1,0:T(8,128)(2,1)S(1)}, u32[]{:S(2)}) copy-start(bf16[64,16,1024]{2,1,0:T(8,128)(2,1)S(1)} %all-to-all-done.3) | copy-start | bytes 6291460
  152.4 5.1 %copy-start.6 = (bf16[1,1024,768]{2,1,0:T(8,128)(2,1)S(1)}, bf16[1,1024,768]{2,1,0:T(8,128)(2,1)}, u32[]{:S(2)}) copy-start(bf16[1,1024,768]{2,1,0:T(8,128)(2,1)} %all-gather.2.cloned.1.call-done) | copy-start | bytes 4718596
  157.5 3.3 %copy-start.7 = (bf16[1024,384]{0,1:T(8,128)(2,1)}, bf16[1024,384]{0,1:T(8,128)(2,1)S(1)}, u32[]{:S(2)}) copy-start(bf16[1024,384]{0,1:T(8,128)(2,1)S(1)} %get-tuple-element.24) | copy-start | bytes 2359300
  157.5 3.3 %copy-start.9 = (bf16[1024,384]{0,1:T(8,128)(2,1)}, bf16[1024,384]{0,1:T(8,128)(2,1)S(1)}, u32[]{:S(2)}) copy-start(bf16[1024,384]{0,1:T(8,128)(2,1)S(1)} %get-tuple-element.25) | copy-start | bytes 2359300
  160.9 61.5 %all-to-all-start.4 = ((bf16[64,16,1024]{2,1,0:T(8,128)(2,1)}), bf16[64,16,1024]{2,1,0:T(8,128)(2,1)S(1)}, u32[]{:S(2)}, u32[]{:S(2)}) async-start(bf16[64,16,1024]{2,1,0:T(8,128)(2,1)} %bitcast.62), calls=%async_computation.4 | async-start | bytes 4194304 | tf_op jit(solution)/shard_map/all_to_all | solution.py:112
  171.1 63.3 %reduce-scatter.7.cloned.1.call-start = ((), (), s32[]{:S(2)}) async-start(), calls=%async_computation.9 | async-start | bytes 884736
  222.4 6.0 %copy-start.8 = (bf16[1024,384]{0,1:T(8,128)(2,1)S(1)}, bf16[1024,384]{0,1:T(8,128)(2,1)}, u32[]{:S(2)}) copy-start(bf16[1024,384]{0,1:T(8,128)(2,1)} %copy-done.7) | copy-start | bytes 2359300
  222.4 59.4 %all-to-all-start.2 = ((bf16[64,16,1024]{2,1,0:T(8,128)(2,1)}), bf16[64,16,1024]{2,1,0:T(8,128)(2,1)}, u32[]{:S(2)}, u32[]{:S(2)}) async-start(bf16[64,16,1024]{2,1,0:T(8,128)(2,1)} %bitcast.59), calls=%async_computation.2 | async-start | bytes 4194304 | tf_op jit(solution)/shard_map/all_to_all | solution.py:109
  228.1 46.9 %reduce-scatter.5.cloned.1.call-start = ((), (), s32[]{:S(2)}) async-start(), calls=%async_computation.8 | async-start | bytes 1769472 | tf_op jit(solution)/shard_map/reduce_scatter | solution.py:114
  233.3 0.9 copy-start.4
  287.0 4.4 %copy-start.2 = (bf16[128,4,1024]{2,1,0:T(4,128)(2,1)S(1)}, bf16[128,4,1024]{2,1,0:T(4,128)(2,1)}, u32[]{:S(2)}) copy-start(bf16[128,4,1024]{2,1,0:T(4,128)(2,1)} %reshape.205) | copy-start | bytes 3145732
Sparse Core Ops, SparseCore 0:
  97.7 49.0 all-gather.1
  182.3 39.2 reduce-scatter.6
  233.4 41.5 reduce-scatter.4
where the time goes:
time: 301 us; the launch traced here: 300 us
  waiting for transfers between devices  131 us (44%)
  starting transfers between devices  41.5 us (14%)
  local copies, waits for them, and re-layouts  37.2 us (12%)
  blocking collectives  34.6 us (11%)
  matrix products  26.3 us (9%)
  other arithmetic  15.8 us (5%)
  between operations  14 us (5%)
    reduce_scatter x1, waiting for transfers between devices, local(): lax.psum_scatter(in_grad[None].astype(jnp.bfloat16), 'dp', scatter_dimens...  38.7 us
    all_to_all x1, waiting for transfers between devices, local(): lax.all_to_all(send_tokens, 'expert', split_axis=0, concat_axis=0, tiled=...  38.1 us
    all_to_all x1, waiting for transfers between devices, local(): lax.all_to_all(grad_back, 'expert', split_axis=0, concat_axis=0, tiled=True)  36.4 us
    all_gather x1, blocking collectives, local(): lax.all_gather(down_proj, 'dp', axis=2, tiled=True)  34.6 us
    all_gather x1, waiting for transfers between devices, local(): lax.all_gather(gate_up, 'dp', axis=1, tiled=True)  15.3 us
    all_to_all x1, starting transfers between devices, local(): lax.all_to_all(counts, 'expert', split_axis=0, concat_axis=0, tiled=True)  10.6 us
    all_to_all x1, starting transfers between devices, local(): lax.all_to_all(grad_back, 'expert', split_axis=0, concat_axis=0, tiled=True)  10.3 us
    unnamed x27, local copies, waits for them, and re-layouts  10.1 us
  transfers between devices with their start and end apart: 8, of which 5 were waited for; matrix products, arithmetic and copies ran while one was open for 19% of the time, Pallas kernels for 0%

commit v1 on v0

v1 whole, which is shorter than its diff:
```python
import jax
import jax.numpy as jnp
from jax import lax
from jax.sharding import PartitionSpec as P


def expert_rows(rows_in, grad_rows, weight_in, weight_out_t):
    hidden_width = weight_out_t.shape[1]
    contract_last = (((1,), (1,)), ((), ()))
    contract_first = (((0,), (0,)), ((), ()))
    pre_act = jnp.dot(rows_in, weight_in, preferred_element_type=jnp.float32)
    pre_gate = pre_act[:, :hidden_width]
    up_value = pre_act[:, hidden_width:]
    act = jax.nn.silu(pre_gate)
    hidden = (act * up_value).astype(jnp.bfloat16)
    expert_out = lax.dot_general(
        hidden, weight_out_t, contract_last, preferred_element_type=jnp.float32
    ).astype(jnp.bfloat16)
    grad_hidden = jnp.dot(grad_rows, weight_out_t, preferred_element_type=jnp.float32)
    sigmoid_value = jax.nn.sigmoid(pre_gate)
    grad_gate = grad_hidden * up_value * sigmoid_value * (1.0 + pre_gate * (1.0 - sigmoid_value))
    grad_up = grad_hidden * act
    grad_pre = jnp.concatenate([grad_gate, grad_up], axis=1).astype(jnp.bfloat16)
    grad_in = lax.dot_general(
        grad_pre, weight_in, contract_last, preferred_element_type=jnp.float32
    ).astype(jnp.bfloat16)
    weight_in_grad = lax.dot_general(
        rows_in, grad_pre, contract_first, preferred_element_type=jnp.float32
    ).astype(jnp.bfloat16)
    weight_out_grad_t = lax.dot_general(
        grad_rows, hidden, contract_first, preferred_element_type=jnp.float32
    ).astype(jnp.bfloat16)
    return expert_out, grad_in, weight_in_grad, weight_out_grad_t


def local(tokens, expert_ids, gate_probs, gate_up, down_proj, cotangent):
    token_count, top_count = expert_ids.shape
    width = tokens.shape[1]
    expert_count = lax.axis_size("expert")
    capacity = 2 * token_count * top_count // expert_count
    route_count = token_count * top_count
    slot_count = expert_count * capacity
    gate_width = gate_up.shape[2]

    weights = jnp.concatenate([gate_up[0], down_proj[0].T], axis=1)
    weights = lax.all_gather(weights, "dp", axis=0, tiled=True)
    weight_in = weights[:, :gate_width]
    weight_out_t = weights[:, gate_width:]

    flat_ids = expert_ids.reshape(route_count)
    onehot = (flat_ids[:, None] == jnp.arange(expert_count, dtype=jnp.int32)[None, :]).astype(
        jnp.int32
    )
    slot_index = jnp.sum((jnp.cumsum(onehot, axis=0) - onehot) * onehot, axis=1)
    position = (flat_ids * capacity + slot_index).reshape(token_count, top_count)
    slot_range = jnp.arange(slot_count, dtype=jnp.int32)
    hits = position[None, :, :] == slot_range[:, None, None]
    select = jnp.any(hits, axis=2)
    weighted = jnp.sum(jnp.where(hits, gate_probs[None, :, :], 0.0), axis=2)
    slot_probs = jnp.sum(weighted, axis=1)
    select_rows = select.astype(jnp.bfloat16)

    both = jnp.concatenate([tokens, cotangent], axis=1)
    gathered = jnp.dot(select_rows, both, preferred_element_type=jnp.float32)
    send_tokens = gathered[:, :width].astype(jnp.bfloat16)
    slot_cot = gathered[:, width:]
    send_grads = (slot_probs[:, None] * slot_cot).astype(jnp.bfloat16)
    send = jnp.concatenate([send_tokens, send_grads], axis=1)

    recv = lax.all_to_all(send, "expert", split_axis=0, concat_axis=0, tiled=True)
    rows_in = recv[:, :width]
    grad_rows = recv[:, width:]
    expert_out, grad_in, weight_in_grad, weight_out_grad_t = expert_rows(
        rows_in, grad_rows, weight_in, weight_out_t
    )
    back = lax.all_to_all(
        jnp.concatenate([expert_out, grad_in], axis=1),
        "expert",
        split_axis=0,
        concat_axis=0,
        tiled=True,
    )
    grads = lax.psum_scatter(
        jnp.concatenate([weight_in_grad, weight_out_grad_t], axis=1),
        "dp",
        scatter_dimension=0,
        tiled=True,
    ).astype(jnp.float32)
    sum_in = grads[None, :, :gate_width]
    sum_out = grads[:, gate_width:].T[None]

    back_out = back[:, :width].astype(jnp.float32)
    back_grad = back[:, width:]
    moe_out = lax.dot_general(
        weighted,
        back_out,
        (((0,), (0,)), ((), ())),
        precision=lax.Precision.HIGHEST,
        preferred_element_type=jnp.float32,
    ).astype(jnp.bfloat16)
    token_grads = lax.dot_general(
        select_rows, back_grad, (((0,), (0,)), ((), ())), preferred_element_type=jnp.float32
    ).astype(jnp.bfloat16)
    slot_gate = jnp.sum(slot_cot * back_out, axis=1)
    gate_grads = slot_gate[position]
    return (moe_out, token_grads, gate_grads, sum_in, sum_out)


def solution(mesh):
    return jax.shard_map(
        local,
        mesh=mesh,
        in_specs=(
            P(("dp", "expert"), None),
            P(("dp", "expert"), None),
            P(("dp", "expert"), None),
            P("expert", "dp", None),
            P("expert", None, "dp"),
            P(("dp", "expert"), None),
        ),
        out_specs=(
            P(("dp", "expert"), None),
            P(("dp", "expert"), None),
            P(("dp", "expert"), None),
            P("expert", "dp", None),
            P("expert", None, "dp"),
        ),
        check_vma=False,
    )
```

time: 301 us -> 269 us (0.89)
  waiting for transfers between devices: 131 us -> 180 us
  blocking collectives: 34.6 us -> 0 us
  starting transfers between devices: 41.5 us -> 17 us
  local copies, waits for them, and re-layouts: 37.2 us -> 19.8 us
    unnamed x4 -> x3, waiting for transfers between devices: 0.73 us -> 50.9 us
    reduce_scatter x1 -> x0, waiting for transfers between devices: 38.7 us -> none  [local(): lax.psum_scatter(in_grad[None].astype(jnp.bfloat16), 'dp', scatter_dimens...]
    all_gather x1, waiting for transfers between devices: 15.3 us -> 51.1 us  [local(): weights = lax.all_gather(weights, 'dp', axis=0, tiled=True)]
    all_gather x1 -> x0, blocking collectives: 34.6 us -> none  [local(): lax.all_gather(down_proj, 'dp', axis=2, tiled=True)]
    all_to_all x5 -> x2, starting transfers between devices: 41.2 us -> 16.9 us  [the longest x1 11 us: local(): lax.all_to_all(send, 'expert', split_axis=0, concat_axis=0, tiled=True)]
    gather x6 -> x2, local copies, waits for them, and re-layouts: 22.4 us -> 2.38 us  [local(): gate_grads = slot_gate[position]]
    concatenate x0 -> x1, local copies, waits for them, and re-layouts: none -> 6.49 us  [local(): jnp.concatenate([expert_out, grad_in], axis=1)]
    concatenate x0 -> x4, other arithmetic: none -> 5.74 us  [the longest x1 2.4 us: local(): jnp.concatenate([expert_out, grad_in], axis=1)]
  transfers between devices with their start and end apart: 8 -> 4, of which waited for: 5 -> 4; matrix products, arithmetic and copies ran while one was open for 19% -> 5% of each run, Pallas kernels for 0% -> 0%
where the time goes in v1:
time: 269 us; the launch traced here: 268 us
  waiting for transfers between devices  180 us (67%)
  matrix products  24.8 us (9%)
  local copies, waits for them, and re-layouts  19.8 us (7%)
  starting transfers between devices  17 us (6%)
  between operations  14.2 us (5%)
  other arithmetic  12.9 us (5%)
    all_gather x1, waiting for transfers between devices, local(): weights = lax.all_gather(weights, 'dp', axis=0, tiled=True)  51.1 us
    unnamed x3, waiting for transfers between devices  50.9 us
    all_to_all x1, waiting for transfers between devices, local(): lax.all_to_all(send, 'expert', split_axis=0, concat_axis=0, tiled=True)  44.2 us
    all_to_all x1, waiting for transfers between devices, local(): lax.all_to_all(jnp.concatenate([expert_out, grad_in], axis=1), 'expert',...  33.4 us
    all_to_all x1, starting transfers between devices, local(): lax.all_to_all(send, 'expert', split_axis=0, concat_axis=0, tiled=True)  11 us
    unnamed x13, local copies, waits for them, and re-layouts  8.95 us
    concatenate x1, local copies, waits for them, and re-layouts, local(): jnp.concatenate([expert_out, grad_in], axis=1)  6.49 us
    all_to_all x1, starting transfers between devices, local(): lax.all_to_all(jnp.concatenate([expert_out, grad_in], axis=1), 'expert',...  5.89 us
  transfers between devices with their start and end apart: 4, of which 4 were waited for; matrix products, arithmetic and copies ran while one was open for 5% of the time, Pallas kernels for 0%

profile of v1, /device:TPU:6, one launch (start us, length us, event | category | flops | bytes accessed | tf_op | source)
XLA Modules:
  0.0 268.3 jit_solution(10926325315860447653)
XLA Ops:
  7.2 0.8 copy.46
  8.0 0.1 eq.42
  8.1 0.1 eq.38
  8.2 1.2 reduce-window.6
  9.4 0.2 slice_reduce_fusion
  9.7 0.1 fusion.36
  9.8 0.1 reduce_sum.39
  9.9 0.1 copy.49
  10.0 0.7 compare_select_fusion
  10.7 0.4 fusion.2
  11.0 1.0 select_reduce_fusion
  12.1 2.3 fusion.30
  14.3 0.0 copy-start
  14.3 0.3 slice.115
  14.7 2.9 %copy-done = f32[1024,2048]{1,0:T(8,128)} copy-done((f32[1024,2048]{1,0:T(8,128)}, f32[1024,2048]{1,0:T(8,128)S(1)}, u32[]{:S(2)}) %copy-start) | copy-done | bytes 8388632
  17.6 0.3 multiply_convert_fusion
  17.9 2.4 pad_maximum_fusion
  20.2 0.0 copy-start.2
  20.3 0.0 copy-start.1
  20.3 11.0 %all-to-all-start = ((bf16[64,16,2048]{2,1,0:T(8,128)(2,1)}), bf16[64,16,2048]{2,1,0:T(8,128)(2,1)}, u32[]{:S(2)}, u32[]{:S(2)}) async-start(bf16[64,16,2048]{2,1,0:T(8,128)(2,1)} %bitcast.40), calls=%async_computation | async-start | bytes 8388608 | tf_op jit(solution)/shard_map/all_to_all | solution.py:70
  31.3 0.0 all-gather.2.cloned.1.call-start
  31.3 0.0 copy-done.2
  31.3 0.1 copy.50
  31.5 0.0 copy-done.1
  31.5 0.7 pad_maximum_fusion.6
  32.2 0.0 all-gather.2.cloned.1.call-update
  32.2 51.1 %all-gather.2.cloned.1.call-done = bf16[1024,1152]{1,0:T(8,128)(2,1)} async-done(((bf16[128,1152]{1,0:T(8,128)(2,1)}), bf16[1024,1152]{1,0:T(8,128)(2,1)}) %all-gather.2.cloned.1.call-update) | async-done | bytes 2359312 | tf_op jit(solution)/shard_map/all_gather | solution.py:46
  83.3 44.2 %all-to-all-done = bf16[64,16,2048]{2,1,0:T(8,128)(2,1)} async-done(((bf16[64,16,2048]{2,1,0:T(8,128)(2,1)}), bf16[64,16,2048]{2,1,0:T(8,128)(2,1)}, u32[]{:S(2)}, u32[]{:S(2)}) %all-to-all-start) | async-done | bytes 4194336 | tf_op jit(solution)/shard_map/all_to_all | solution.py:70
  127.5 0.0 copy-start.3
  127.5 4.1 %fusion.11 = f32[1024,768]{0,1:T(8,128)S(1)} fusion(bf16[1024,2048]{1,0:T(8,128)(2,1)} %bitcast.2, bf16[1024,1152]{1,0:T(8,128)(2,1)} %all-gather.2.cloned.1.call-done), kind=kOutput, calls=%fused_computation.23 | convolution fusion | flops 1610612736 | bytes 6815744 | tf_op jit(solution)/shard_map/dot_general | solution.py:11
  131.6 0.0 copy-done.3
  131.6 3.3 %multiply_convert_fusion.2 = (bf16[1024,384]{0,1:T(8,128)(2,1)S(1)}, bf16[1024,384]{0,1:T(8,128)(2,1)S(1)}, bf16[1024,384]{0,1:T(8,128)(2,1)S(1)}) fusion(f32[1024,768]{0,1:T(8,128)S(1)} %fusion.11, bf16[1024,1152]{1,0:T(8,128)(2,1)S(1)} %copy-done.3, bf16[1024,2048]{1,0:T(8,128)(2,1)} %bitcast.2), kind=kOutput, calls=%fused_computation.28 | convolution fusion | flops 811204608 | bytes 8388608 | tf_op jit(solution)/shard_map/dot_general | solution.py:19
  134.8 1.3 convolution_convert_fusion
  136.1 1.8 convolution_convert_fusion.1
  137.9 2.4 pad_maximum_fusion.1
  140.3 6.5 %copy.51 = bf16[1024,2048]{1,0:T(8,128)(2,1)} copy(bf16[1024,2048]{0,1:T(8,128)(2,1)} %pad_maximum_fusion.1) | data formatting | bytes 8388608 | tf_op jit(solution)/shard_map/concatenate | solution.py:77
  146.8 5.9 %all-to-all-start.1 = ((bf16[64,16,2048]{2,1,0:T(8,128)(2,1)}), bf16[64,16,2048]{2,1,0:T(8,128)(2,1)}, u32[]{:S(2)}, u32[]{:S(2)}) async-start(bf16[64,16,2048]{2,1,0:T(8,128)(2,1)} %bitcast.39), calls=%async_computation.1 | async-start | bytes 8388608 | tf_op jit(solution)/shard_map/all_to_all | solution.py:76
  152.7 0.0 reduce-scatter.4.cloned.1.call-start
  152.7 2.6 fusion.17
  155.3 3.4 %fusion.13 = bf16[1024,768]{0,1:T(8,128)(2,1)S(1)} fusion(bf16[1024,2048]{1,0:T(8,128)(2,1)} %bitcast.2, bf16[1024,384]{0,1:T(8,128)(2,1)S(1)} %get-tuple-element.35, bf16[1024,384]{0,1:T(8,128)(2,1)S(1)} %get-tuple-element.34), kind=kOutput, calls=%fused_computation.25 | convolution fusion | flops 1614544896 | bytes 5242880 | tf_op jit(solution)/shard_map/dot_general | solution.py:27
  158.7 0.2 pad_maximum_fusion.2
  158.9 2.5 copy.55
  161.5 0.0 reduce-scatter.4.cloned.1.call-update
  161.5 0.1 copy.52
  161.6 0.1 reshape.45
  161.7 50.9 %reduce-scatter.4.cloned.1.call-done = bf16[128,1152]{1,0:T(8,128)(2,1)} async-done(((bf16[1024,1152]{1,0:T(8,128)(2,1)}), bf16[128,1152]{1,0:T(8,128)(2,1)}) %reduce-scatter.4.cloned.1.call-update) | async-done | bytes 294928
  212.6 1.2 copy.56
  213.9 0.9 copy.54
  214.8 0.7 slice_bitcast_fusion.1
  215.5 33.4 %all-to-all-done.1 = bf16[64,16,2048]{2,1,0:T(8,128)(2,1)} async-done(((bf16[64,16,2048]{2,1,0:T(8,128)(2,1)}), bf16[64,16,2048]{2,1,0:T(8,128)(2,1)}, u32[]{:S(2)}, u32[]{:S(2)}) %all-to-all-start.1) | async-done | bytes 4194336 | tf_op jit(solution)/shard_map/all_to_all | solution.py:76
  248.9 3.3 %multiply_reduce_fusion = f32[1024]{0:T(1024)S(1)} fusion(f32[1024,2048]{1,0:T(8,128)} %copy-done, bf16[1024,2048]{1,0:T(8,128)(2,1)} %bitcast.7), kind=kLoop, calls=%fused_computation.4 | loop fusion | flops 3144704 | bytes 6295552 | tf_op jit(solution)/shard_map/reduce_sum | solution.py:104
  252.2 2.8 %fusion.25 = bf16[128,1024]{1,0:T(8,128)(2,1)} fusion(pred[1024,128]{1,0:T(8,128)(4,1)S(1)} %fusion.2, bf16[1024,2048]{1,0:T(8,128)(2,1)} %bitcast.7), kind=kOutput, calls=%fused_computation.36 | convolution fusion | flops 268566528 | bytes 2490368 | tf_op jit(solution)/shard_map/dot_general | solution.py:101
  255.0 2.3 gather_fusion
  257.3 0.1 reshape.44
  257.4 0.7 copy.53
  258.1 3.4 %fusion.22 = bf16[128,1024]{1,0:T(8,128)(2,1)} fusion(f32[1024,128]{1,0:T(8,128)S(1)} %get-tuple-element.31, bf16[1024,2048]{1,0:T(8,128)(2,1)} %bitcast.7), kind=kOutput, calls=%fused_computation.35 | convolution fusion | flops 1610743808 | bytes 2883584 | tf_op jit(solution)/shard_map/dot_general | solution.py:94
  (6 shorter events, 0.1 us)
Async XLA Ops:
  14.3 3.2 %copy-start = (f32[1024,2048]{1,0:T(8,128)}, f32[1024,2048]{1,0:T(8,128)S(1)}, u32[]{:S(2)}) copy-start(f32[1024,2048]{1,0:T(8,128)S(1)} %fusion.30) | copy-start | bytes 25165828
  20.2 11.1 %copy-start.2 = (bf16[1,384,128]{2,1,0:T(8,128)(2,1)S(1)}, bf16[1,384,128]{2,1,0:T(8,128)(2,1)}, u32[]{:S(2)}) copy-start(bf16[1,384,128]{2,1,0:T(8,128)(2,1)} %param.10) | copy-start | bytes 294916
  20.3 11.2 %copy-start.1 = (bf16[1,128,768]{2,1,0:T(8,128)(2,1)S(1)}, bf16[1,128,768]{2,1,0:T(8,128)(2,1)}, u32[]{:S(2)}) copy-start(bf16[1,128,768]{2,1,0:T(8,128)(2,1)} %param.9) | copy-start | bytes 589828
  20.3 107.2 %all-to-all-start = ((bf16[64,16,2048]{2,1,0:T(8,128)(2,1)}), bf16[64,16,2048]{2,1,0:T(8,128)(2,1)}, u32[]{:S(2)}, u32[]{:S(2)}) async-start(bf16[64,16,2048]{2,1,0:T(8,128)(2,1)} %bitcast.40), calls=%async_computation | async-start | bytes 8388608 | tf_op jit(solution)/shard_map/all_to_all | solution.py:70
  31.3 52.0 %all-gather.2.cloned.1.call-start = ((), (), s32[]{:S(2)}) async-start(), calls=%async_computation.3 | async-start | bytes 2654208 | tf_op jit(solution)/shard_map/all_gather | solution.py:46
  127.5 4.1 %copy-start.3 = (bf16[1024,1152]{1,0:T(8,128)(2,1)S(1)}, bf16[1024,1152]{1,0:T(8,128)(2,1)}, u32[]{:S(2)}) copy-start(bf16[1024,1152]{1,0:T(8,128)(2,1)} %all-gather.2.cloned.1.call-done) | copy-start | bytes 7077892
  146.8 102.1 %all-to-all-start.1 = ((bf16[64,16,2048]{2,1,0:T(8,128)(2,1)}), bf16[64,16,2048]{2,1,0:T(8,128)(2,1)}, u32[]{:S(2)}, u32[]{:S(2)}) async-start(bf16[64,16,2048]{2,1,0:T(8,128)(2,1)} %bitcast.39), calls=%async_computation.1 | async-start | bytes 8388608 | tf_op jit(solution)/shard_map/all_to_all | solution.py:76
  152.7 59.9 %reduce-scatter.4.cloned.1.call-start = ((), (), s32[]{:S(2)}) async-start(), calls=%async_computation.4 | async-start | bytes 2654208
Sparse Core Ops, SparseCore 0:
  34.8 48.5 all-gather.1
  161.6 50.9 reduce-scatter.3

commit v2 on v1

--- a/solution.py
+++ b/solution.py
@@ -1,7 +1,12 @@
 import jax
 import jax.numpy as jnp
 from jax import lax
+from jax.experimental.layout import Layout, with_layout_constraint
 from jax.sharding import PartitionSpec as P
+
+
+def row_major(x):
+    return with_layout_constraint(x, Layout(major_to_minor=tuple(range(x.ndim))))
 
 
 def expert_rows(rows_in, grad_rows, weight_in, weight_out_t):
@@ -61,10 +66,10 @@
     select_rows = select.astype(jnp.bfloat16)
 
     both = jnp.concatenate([tokens, cotangent], axis=1)
-    gathered = jnp.dot(select_rows, both, preferred_element_type=jnp.float32)
-    send_tokens = gathered[:, :width].astype(jnp.bfloat16)
+    gathered = jnp.dot(select_rows, both, preferred_element_type=jnp.bfloat16)
+    send_tokens = gathered[:, :width]
     slot_cot = gathered[:, width:]
-    send_grads = (slot_probs[:, None] * slot_cot).astype(jnp.bfloat16)
+    send_grads = (slot_probs[:, None] * slot_cot.astype(jnp.float32)).astype(jnp.bfloat16)
     send = jnp.concatenate([send_tokens, send_grads], axis=1)
 
     recv = lax.all_to_all(send, "expert", split_axis=0, concat_axis=0, tiled=True)
@@ -74,7 +79,7 @@
         rows_in, grad_rows, weight_in, weight_out_t
     )
     back = lax.all_to_all(
-        jnp.concatenate([expert_out, grad_in], axis=1),
+        jnp.concatenate([row_major(expert_out), row_major(grad_in)], axis=1),
         "expert",
         split_axis=0,
         concat_axis=0,
@@ -101,8 +106,8 @@
     token_grads = lax.dot_general(
         select_rows, back_grad, (((0,), (0,)), ((), ())), preferred_element_type=jnp.float32
     ).astype(jnp.bfloat16)
-    slot_gate = jnp.sum(slot_cot * back_out, axis=1)
-    gate_grads = slot_gate[position]
+    slot_gate = jnp.sum(slot_cot.astype(jnp.float32) * back_out, axis=1)
+    gate_grads = jnp.sum(jnp.where(hits, slot_gate[:, None, None], 0.0), axis=0)
     return (moe_out, token_grads, gate_grads, sum_in, sum_out)
 
 

time: 269 us -> 259 us (0.963)
  local copies, waits for them, and re-layouts: 19.8 us -> 8.8 us
    concatenate x1 -> x0, local copies, waits for them, and re-layouts: 6.49 us -> none  [local(): jnp.concatenate([expert_out, grad_in], axis=1)]
    unnamed x13 -> x12, local copies, waits for them, and re-layouts: 8.95 us -> 7.13 us
where the time goes in v2:
time: 259 us; the launch traced here: 258 us
  waiting for transfers between devices  180 us (69%)
  matrix products  24.9 us (10%)
  starting transfers between devices  17 us (7%)
  between operations  14.2 us (5%)
  other arithmetic  13.4 us (5%)
  local copies, waits for them, and re-layouts  8.8 us (3%)
    unnamed x3, waiting for transfers between devices  51.1 us
    all_gather x1, waiting for transfers between devices, local(): weights = lax.all_gather(weights, 'dp', axis=0, tiled=True)  51.1 us
    all_to_all x1, waiting for transfers between devices, local(): lax.all_to_all(send, 'expert', split_axis=0, concat_axis=0, tiled=True)  44.2 us
    all_to_all x1, waiting for transfers between devices, local(): lax.all_to_all(jnp.concatenate([row_major(expert_out), row_major(grad_in)...  33.4 us
    all_to_all x1, starting transfers between devices, local(): lax.all_to_all(send, 'expert', split_axis=0, concat_axis=0, tiled=True)  11 us
    unnamed x12, local copies, waits for them, and re-layouts  7.13 us
    all_to_all x1, starting transfers between devices, local(): lax.all_to_all(jnp.concatenate([row_major(expert_out), row_major(grad_in)...  5.9 us
  transfers between devices with their start and end apart: 4, of which 4 were waited for; matrix products, arithmetic and copies ran while one was open for 5% of the time, Pallas kernels for 0%

profile of v2, /device:TPU:6, one launch (start us, length us, event | category | flops | bytes accessed | tf_op | source)
XLA Modules:
  0.0 258.1 jit_solution(1765834554842461727)
XLA Ops:
  7.2 0.8 copy.39
  8.0 0.1 eq.42
  8.1 0.1 eq.38
  8.2 1.2 reduce-window.6
  9.4 0.2 slice_reduce_fusion
  9.7 0.1 fusion.38
  9.8 0.1 reduce_sum.48
  9.9 0.1 copy.42
  10.0 0.7 multiply_add_fusion
  10.7 0.4 fusion.4
  11.0 1.0 select_reduce_fusion
  12.1 2.3 fusion.32
  14.3 0.0 copy-start
  14.4 0.2 slice.57
  14.6 1.7 copy-done
  16.3 0.4 fusion
  16.7 2.4 pad_maximum_fusion
  19.1 0.0 copy-start.2
  19.1 0.0 copy-start.1
  19.1 11.0 %all-to-all-start = ((bf16[64,16,2048]{2,1,0:T(8,128)(2,1)}), bf16[64,16,2048]{2,1,0:T(8,128)(2,1)}, u32[]{:S(2)}, u32[]{:S(2)}) async-start(bf16[64,16,2048]{2,1,0:T(8,128)(2,1)} %bitcast.40), calls=%async_computation | async-start | bytes 8388608 | tf_op jit(solution)/shard_map/all_to_all | solution.py:75
  30.1 0.0 all-gather.2.cloned.1.call-start
  30.2 0.0 copy-done.2
  30.2 0.1 copy.43
  30.3 0.0 copy-done.1
  30.3 0.7 pad_maximum_fusion.6
  31.0 0.0 all-gather.2.cloned.1.call-update
  31.1 51.1 %all-gather.2.cloned.1.call-done = bf16[1024,1152]{1,0:T(8,128)(2,1)} async-done(((bf16[128,1152]{1,0:T(8,128)(2,1)}), bf16[1024,1152]{1,0:T(8,128)(2,1)}) %all-gather.2.cloned.1.call-update) | async-done | bytes 2359312 | tf_op jit(solution)/shard_map/all_gather | solution.py:51
  82.1 44.2 %all-to-all-done = bf16[64,16,2048]{2,1,0:T(8,128)(2,1)} async-done(((bf16[64,16,2048]{2,1,0:T(8,128)(2,1)}), bf16[64,16,2048]{2,1,0:T(8,128)(2,1)}, u32[]{:S(2)}, u32[]{:S(2)}) %all-to-all-start) | async-done | bytes 4194336 | tf_op jit(solution)/shard_map/all_to_all | solution.py:75
  126.3 0.0 copy-start.3
  126.3 4.1 %fusion.13 = f32[1024,768]{0,1:T(8,128)S(1)} fusion(bf16[1024,2048]{1,0:T(8,128)(2,1)} %bitcast.2, bf16[1024,1152]{1,0:T(8,128)(2,1)} %all-gather.2.cloned.1.call-done), kind=kOutput, calls=%fused_computation.24 | convolution fusion | flops 1610612736 | bytes 6815744 | tf_op jit(solution)/shard_map/dot_general | solution.py:16
  130.4 0.0 copy-done.3
  130.4 3.3 %multiply_convert_fusion.1 = (bf16[1024,384]{0,1:T(8,128)(2,1)S(1)}, bf16[1024,384]{0,1:T(8,128)(2,1)S(1)}, bf16[1024,384]{0,1:T(8,128)(2,1)S(1)}) fusion(f32[1024,768]{0,1:T(8,128)S(1)} %fusion.13, bf16[1024,1152]{1,0:T(8,128)(2,1)S(1)} %copy-done.3, bf16[1024,2048]{1,0:T(8,128)(2,1)} %bitcast.2), kind=kOutput, calls=%fused_computation.29 | convolution fusion | flops 811204608 | bytes 8388608 | tf_op jit(solution)/shard_map/dot_general | solution.py:24
  133.7 1.3 convolution_convert_fusion
  135.0 1.9 convolution_convert_fusion.1
  136.8 2.4 pad_maximum_fusion.1
  139.2 5.9 %all-to-all-start.1 = ((bf16[64,16,2048]{2,1,0:T(8,128)(2,1)}), bf16[64,16,2048]{2,1,0:T(8,128)(2,1)}, u32[]{:S(2)}, u32[]{:S(2)}) async-start(bf16[64,16,2048]{2,1,0:T(8,128)(2,1)} %bitcast.39), calls=%async_computation.1 | async-start | bytes 8388608 | tf_op jit(solution)/shard_map/all_to_all | solution.py:81
  145.2 0.0 reduce-scatter.4.cloned.1.call-start
  145.2 2.6 fusion.19
  147.8 3.4 %fusion.15 = bf16[1024,768]{0,1:T(8,128)(2,1)S(1)} fusion(bf16[1024,2048]{1,0:T(8,128)(2,1)} %bitcast.2, bf16[1024,384]{0,1:T(8,128)(2,1)S(1)} %get-tuple-element.33, bf16[1024,384]{0,1:T(8,128)(2,1)S(1)} %get-tuple-element.32), kind=kOutput, calls=%fused_computation.26 | convolution fusion | flops 1614544896 | bytes 5242880 | tf_op jit(solution)/shard_map/dot_general | solution.py:32
  151.2 0.2 pad_maximum_fusion.2
  151.4 2.6 copy.45
  153.9 0.0 reduce-scatter.4.cloned.1.call-update
  154.0 51.1 %reduce-scatter.4.cloned.1.call-done = bf16[128,1152]{1,0:T(8,128)(2,1)} async-done(((bf16[1024,1152]{1,0:T(8,128)(2,1)}), bf16[128,1152]{1,0:T(8,128)(2,1)}) %reduce-scatter.4.cloned.1.call-update) | async-done | bytes 294928
  205.1 1.2 copy.46
  206.3 0.9 copy.44
  207.2 0.7 slice_bitcast_fusion.1
  207.9 33.4 %all-to-all-done.1 = bf16[64,16,2048]{2,1,0:T(8,128)(2,1)} async-done(((bf16[64,16,2048]{2,1,0:T(8,128)(2,1)}), bf16[64,16,2048]{2,1,0:T(8,128)(2,1)}, u32[]{:S(2)}, u32[]{:S(2)}) %all-to-all-start.1) | async-done | bytes 4194336 | tf_op jit(solution)/shard_map/all_to_all | solution.py:81
  241.4 2.8 %fusion.1 = f32[1024]{0:T(1024)S(1)} fusion(bf16[1024,2048]{1,0:T(8,128)(2,1)} %bitcast.7, bf16[1024,2048]{1,0:T(8,128)(2,1)} %copy-done), kind=kLoop, calls=%fused_computation.3 | loop fusion | flops 4193280 | bytes 4198400 | tf_op jit(solution)/shard_map/reduce_sum | solution.py:109
  244.2 2.8 %fusion.27 = bf16[128,1024]{1,0:T(8,128)(2,1)} fusion(pred[1024,128]{1,0:T(8,128)(4,1)S(1)} %fusion.4, bf16[1024,2048]{1,0:T(8,128)(2,1)} %bitcast.7), kind=kOutput, calls=%fused_computation.37 | convolution fusion | flops 268566528 | bytes 2490368 | tf_op jit(solution)/shard_map/dot_general | solution.py:106
  247.0 3.4 %fusion.24 = bf16[128,1024]{1,0:T(8,128)(2,1)} fusion(f32[1024,128]{1,0:T(8,128)S(1)} %get-tuple-element.31, bf16[1024,2048]{1,0:T(8,128)(2,1)} %bitcast.7), kind=kOutput, calls=%fused_computation.36 | convolution fusion | flops 1610743808 | bytes 2883584 | tf_op jit(solution)/shard_map/dot_general | solution.py:99
  250.4 0.9 select_reduce_fusion.2
  (5 shorter events, 0.1 us)
Async XLA Ops:
  14.3 1.9 copy-start
  19.1 11.1 %copy-start.2 = (bf16[1,384,128]{2,1,0:T(8,128)(2,1)S(1)}, bf16[1,384,128]{2,1,0:T(8,128)(2,1)}, u32[]{:S(2)}) copy-start(bf16[1,384,128]{2,1,0:T(8,128)(2,1)} %param.10) | copy-start | bytes 294916
  19.1 11.2 %copy-start.1 = (bf16[1,128,768]{2,1,0:T(8,128)(2,1)S(1)}, bf16[1,128,768]{2,1,0:T(8,128)(2,1)}, u32[]{:S(2)}) copy-start(bf16[1,128,768]{2,1,0:T(8,128)(2,1)} %param.9) | copy-start | bytes 589828
  19.1 107.2 %all-to-all-start = ((bf16[64,16,2048]{2,1,0:T(8,128)(2,1)}), bf16[64,16,2048]{2,1,0:T(8,128)(2,1)}, u32[]{:S(2)}, u32[]{:S(2)}) async-start(bf16[64,16,2048]{2,1,0:T(8,128)(2,1)} %bitcast.40), calls=%async_computation | async-start | bytes 8388608 | tf_op jit(solution)/shard_map/all_to_all | solution.py:75
  30.1 52.0 %all-gather.2.cloned.1.call-start = ((), (), s32[]{:S(2)}) async-start(), calls=%async_computation.3 | async-start | bytes 2654208 | tf_op jit(solution)/shard_map/all_gather | solution.py:51
  126.3 4.1 %copy-start.3 = (bf16[1024,1152]{1,0:T(8,128)(2,1)S(1)}, bf16[1024,1152]{1,0:T(8,128)(2,1)}, u32[]{:S(2)}) copy-start(bf16[1024,1152]{1,0:T(8,128)(2,1)} %all-gather.2.cloned.1.call-done) | copy-start | bytes 7077892
  139.2 102.1 %all-to-all-start.1 = ((bf16[64,16,2048]{2,1,0:T(8,128)(2,1)}), bf16[64,16,2048]{2,1,0:T(8,128)(2,1)}, u32[]{:S(2)}, u32[]{:S(2)}) async-start(bf16[64,16,2048]{2,1,0:T(8,128)(2,1)} %bitcast.39), calls=%async_computation.1 | async-start | bytes 8388608 | tf_op jit(solution)/shard_map/all_to_all | solution.py:81
  145.2 59.9 %reduce-scatter.4.cloned.1.call-start = ((), (), s32[]{:S(2)}) async-start(), calls=%async_computation.4 | async-start | bytes 2654208
Sparse Core Ops, SparseCore 0:
  33.6 48.5 all-gather.1
  154.1 50.9 reduce-scatter.3

commit v3 on v2

--- a/solution.py
+++ b/solution.py
@@ -38,6 +38,32 @@
     return expert_out, grad_in, weight_in_grad, weight_out_grad_t
 
 
+def gather_dp(block):
+    size = lax.axis_size("dp")
+    me = lax.axis_index("dp")
+    pieces = [block]
+    for shift in range(1, size):
+        pairs = [(i, (i + shift) % size) for i in range(size)]
+        pieces.append(lax.ppermute(block, "dp", pairs))
+    stacked = jnp.stack(pieces[::-1] + pieces[::-1])
+    return lax.dynamic_slice_in_dim(stacked, size - 1 - me, size, axis=0).reshape(
+        size * block.shape[0], block.shape[1]
+    )
+
+
+def scatter_dp(full):
+    size = lax.axis_size("dp")
+    me = lax.axis_index("dp")
+    rows = full.shape[0] // size
+    blocks = full.reshape(size, rows, full.shape[1])
+    total = lax.dynamic_index_in_dim(blocks, me, axis=0, keepdims=False).astype(jnp.float32)
+    for shift in range(1, size):
+        pairs = [(i, (i + shift) % size) for i in range(size)]
+        part = lax.dynamic_index_in_dim(blocks, (me + shift) % size, axis=0, keepdims=False)
+        total = total + lax.ppermute(part, "dp", pairs).astype(jnp.float32)
+    return total
+
+
 def local(tokens, expert_ids, gate_probs, gate_up, down_proj, cotangent):
     token_count, top_count = expert_ids.shape
     width = tokens.shape[1]
@@ -47,8 +73,7 @@
     slot_count = expert_count * capacity
     gate_width = gate_up.shape[2]
 
-    weights = jnp.concatenate([gate_up[0], down_proj[0].T], axis=1)
-    weights = lax.all_gather(weights, "dp", axis=0, tiled=True)
+    weights = gather_dp(jnp.concatenate([gate_up[0], down_proj[0].T], axis=1))
     weight_in = weights[:, :gate_width]
     weight_out_t = weights[:, gate_width:]
 
@@ -66,11 +91,9 @@
     select_rows = select.astype(jnp.bfloat16)
 
     both = jnp.concatenate([tokens, cotangent], axis=1)
-    gathered = jnp.dot(select_rows, both, preferred_element_type=jnp.bfloat16)
-    send_tokens = gathered[:, :width]
-    slot_cot = gathered[:, width:]
-    send_grads = (slot_probs[:, None] * slot_cot.astype(jnp.float32)).astype(jnp.bfloat16)
-    send = jnp.concatenate([send_tokens, send_grads], axis=1)
+    gathered = jnp.dot(select_rows, both, preferred_element_type=jnp.float32)
+    column = lax.broadcasted_iota(jnp.int32, gathered.shape, 1)
+    send = (gathered * jnp.where(column < width, 1.0, slot_probs[:, None])).astype(jnp.bfloat16)
 
     recv = lax.all_to_all(send, "expert", split_axis=0, concat_axis=0, tiled=True)
     rows_in = recv[:, :width]
@@ -85,12 +108,7 @@
         concat_axis=0,
         tiled=True,
     )
-    grads = lax.psum_scatter(
-        jnp.concatenate([weight_in_grad, weight_out_grad_t], axis=1),
-        "dp",
-        scatter_dimension=0,
-        tiled=True,
-    ).astype(jnp.float32)
+    grads = scatter_dp(jnp.concatenate([weight_in_grad, weight_out_grad_t], axis=1))
     sum_in = grads[None, :, :gate_width]
     sum_out = grads[:, gate_width:].T[None]
 
@@ -106,8 +124,10 @@
     token_grads = lax.dot_general(
         select_rows, back_grad, (((0,), (0,)), ((), ())), preferred_element_type=jnp.float32
     ).astype(jnp.bfloat16)
-    slot_gate = jnp.sum(slot_cot.astype(jnp.float32) * back_out, axis=1)
-    gate_grads = jnp.sum(jnp.where(hits, slot_gate[:, None, None], 0.0), axis=0)
+    token_slot = lax.dot_general(
+        cotangent, back[:, :width], (((1,), (1,)), ((), ())), preferred_element_type=jnp.float32
+    )
+    gate_grads = jnp.sum(jnp.where(hits, token_slot.T[:, :, None], 0.0), axis=0)
     return (moe_out, token_grads, gate_grads, sum_in, sum_out)
 
 

time: 259 us -> 242 us (0.934)
  waiting for transfers between devices: 180 us -> 109 us
  starting transfers between devices: 17 us -> 83.1 us
  between operations: 14.2 us -> 1.24 us
  matrix products: 24.9 us -> 28.7 us
  other arithmetic: 13.4 us -> 10.3 us
    ppermute x0 -> x14, waiting for transfers between devices: none -> 79 us  [the longest x7 43.5 us: gather_dp(): pieces.append(lax.ppermute(block, 'dp', pairs))]
    ppermute x0 -> x14, starting transfers between devices: none -> 66 us  [the longest x7 35.8 us: scatter_dp(): total = total + lax.ppermute(part, 'dp', pairs).astype(jnp.float32)]
    unnamed x3 -> x0, waiting for transfers between devices: 51.1 us -> none
    all_gather x1 -> x0, waiting for transfers between devices: 51.1 us -> none  [local(): weights = lax.all_gather(weights, 'dp', axis=0, tiled=True)]
    all_to_all x1, waiting for transfers between devices: 33.4 us -> 8.73 us  [local(): lax.all_to_all(jnp.concatenate([row_major(expert_out), row_major(grad_in)...]
    all_to_all x1, waiting for transfers between devices: 44.2 us -> 21.4 us  [local(): lax.all_to_all(send, 'expert', split_axis=0, concat_axis=0, tiled=True)]
    unnamed x12 -> x40, local copies, waits for them, and re-layouts: 7.13 us -> 2.82 us
    dot_general x1 -> x2, matrix products: 2.27 us -> 6.53 us  [the longest x1 4.23 us: local(): gathered = jnp.dot(select_rows, both, preferred_element_type=jnp.float32)]
  transfers between devices with their start and end apart: 4 -> 16, of which waited for: 4 -> 11; matrix products, arithmetic and copies ran while one was open for 5% -> 7% of each run, Pallas kernels for 0% -> 0%
where the time goes in v3:
time: 242 us; the launch traced here: 241 us
  waiting for transfers between devices  109 us (45%)
  starting transfers between devices  83.1 us (34%)
  matrix products  28.7 us (12%)
  other arithmetic  10.3 us (4%)
  local copies, waits for them, and re-layouts  8.59 us (4%)
    ppermute x7, waiting for transfers between devices, gather_dp(): pieces.append(lax.ppermute(block, 'dp', pairs))  43.5 us
    ppermute x7, starting transfers between devices, scatter_dp(): total = total + lax.ppermute(part, 'dp', pairs).astype(jnp.float32)  35.8 us
    ppermute x7, waiting for transfers between devices, scatter_dp(): total = total + lax.ppermute(part, 'dp', pairs).astype(jnp.float32)  35.5 us
    ppermute x7, starting transfers between devices, gather_dp(): pieces.append(lax.ppermute(block, 'dp', pairs))  30.3 us
    all_to_all x1, waiting for transfers between devices, local(): lax.all_to_all(send, 'expert', split_axis=0, concat_axis=0, tiled=True)  21.4 us
    all_to_all x1, starting transfers between devices, local(): lax.all_to_all(send, 'expert', split_axis=0, concat_axis=0, tiled=True)  11 us
    all_to_all x1, waiting for transfers between devices, local(): lax.all_to_all(jnp.concatenate([row_major(expert_out), row_major(grad_in)...  8.73 us
    all_to_all x1, starting transfers between devices, local(): lax.all_to_all(jnp.concatenate([row_major(expert_out), row_major(grad_in)...  6.02 us
  transfers between devices with their start and end apart: 16, of which 11 were waited for; matrix products, arithmetic and copies ran while one was open for 7% of the time, Pallas kernels for 0%

profile of v3, /device:TPU:6, one launch (start us, length us, event | category | flops | bytes accessed | tf_op | source)
XLA Modules:
  0.0 241.0 jit_solution(16396720179078775445)
XLA Ops:
  0.6 0.8 copy.47
  1.4 0.1 eq.50
  1.5 0.1 eq.46
  1.7 1.2 reduce-window.6
  2.9 0.2 slice_reduce_fusion
  3.1 0.1 fusion.43
  3.3 0.1 reduce_sum.39
  3.4 0.1 copy.50
  3.5 0.7 multiply_add_fusion
  4.2 0.4 fusion.2
  4.5 0.0 copy-start.3
  4.5 1.0 select_reduce_fusion
  5.6 4.2 %multiply_convert_fusion = bf16[1024,2048]{1,0:T(8,128)(2,1)} fusion(pred[1024,128]{1,0:T(8,128)(4,1)S(1)} %fusion.2, f32[1024]{0:T(1024)S(1)} %get-tuple-element.20, pred[2048]{0:T(1024)(128)(4,1)S(1)} %iota_compare_fusion.3, bf16[128,1024]{1,0:T(8,128)(2,1)} %param.11, bf16[128,1024]{1,0:T(8,128)(2,1)} %param.6), kind=kOutput, calls=%fused_computation | convolution fusion | flops 544210944 | bytes 4855808 | tf_op jit(solution)/shard_map/dot_general | solution.py:94
  9.8 11.0 %all-to-all-start = ((bf16[64,16,2048]{2,1,0:T(8,128)(2,1)}), bf16[64,16,2048]{2,1,0:T(8,128)(2,1)}, u32[]{:S(2)}, u32[]{:S(2)}) async-start(bf16[64,16,2048]{2,1,0:T(8,128)(2,1)} %bitcast.85), calls=%async_computation | async-start | bytes 8388608 | tf_op jit(solution)/shard_map/all_to_all | solution.py:98
  20.8 0.1 copy.51
  21.0 10.9 %collective-permute-start = (bf16[128,1152]{1,0:T(8,128)(2,1)S(1)}, bf16[128,1152]{1,0:T(8,128)(2,1)S(1)}, u32[]{:S(2)}, u32[]{:S(2)}) collective-permute-start(bf16[128,1152]{1,0:T(8,128)(2,1)S(1)} %pad_maximum_fusion.5), channel_id=1, source_target_pairs={{0,448},{64,0},{128,64},{192,128},{256,192},{320,256},{384,320},{4... | collective-permute-start | bytes 884744 | tf_op jit(solution)/shard_map/ppermute | solution.py:47
  31.9 2.5 %collective-permute-start.1 = (bf16[128,1152]{1,0:T(8,128)(2,1)S(1)}, bf16[128,1152]{1,0:T(8,128)(2,1)S(1)}, u32[]{:S(2)}, u32[]{:S(2)}) collective-permute-start(bf16[128,1152]{1,0:T(8,128)(2,1)S(1)} %pad_maximum_fusion.5), channel_id=1, source_target_pairs={{0,384},{64,448},{128,0},{192,64},{256,128},{320,192},{384,256},{4... | collective-permute-start | bytes 884744 | tf_op jit(solution)/shard_map/ppermute | solution.py:47
  34.3 1.9 collective-permute-start.2
  36.3 7.8 %collective-permute-start.3 = (bf16[128,1152]{1,0:T(8,128)(2,1)S(1)}, bf16[128,1152]{1,0:T(8,128)(2,1)S(1)}, u32[]{:S(2)}, u32[]{:S(2)}) collective-permute-start(bf16[128,1152]{1,0:T(8,128)(2,1)S(1)} %pad_maximum_fusion.5), channel_id=1, source_target_pairs={{0,256},{64,320},{128,384},{192,448},{256,0},{320,64},{384,128},{4... | collective-permute-start | bytes 884744 | tf_op jit(solution)/shard_map/ppermute | solution.py:47
  44.1 1.9 collective-permute-start.4
  46.1 3.4 %collective-permute-start.5 = (bf16[128,1152]{1,0:T(8,128)(2,1)S(1)}, bf16[128,1152]{1,0:T(8,128)(2,1)S(1)}, u32[]{:S(2)}, u32[]{:S(2)}) collective-permute-start(bf16[128,1152]{1,0:T(8,128)(2,1)S(1)} %pad_maximum_fusion.5), channel_id=1, source_target_pairs={{0,128},{64,192},{128,256},{192,320},{256,384},{320,448},{384,0},{... | collective-permute-start | bytes 884744 | tf_op jit(solution)/shard_map/ppermute | solution.py:47
  49.5 5.6 %collective-permute-done.1 = bf16[128,1152]{1,0:T(8,128)(2,1)S(1)} collective-permute-done((bf16[128,1152]{1,0:T(8,128)(2,1)S(1)}, bf16[128,1152]{1,0:T(8,128)(2,1)S(1)}, u32[]{:S(2)}, u32[]{:S(2)}) %collective-permute-start.1) | collective-permute-done | bytes 294944 | tf_op jit(solution)/shard_map/ppermute | solution.py:47
  55.1 1.9 collective-permute-start.6
  57.0 25.6 %collective-permute-done.2 = bf16[128,1152]{1,0:T(8,128)(2,1)S(1)} collective-permute-done((bf16[128,1152]{1,0:T(8,128)(2,1)S(1)}, bf16[128,1152]{1,0:T(8,128)(2,1)S(1)}, u32[]{:S(2)}, u32[]{:S(2)}) %collective-permute-start.2) | collective-permute-done | bytes 294944 | tf_op jit(solution)/shard_map/ppermute | solution.py:47
  82.7 0.0 collective-permute-done.3
  82.7 0.7 collective-permute-done.4
  83.4 4.6 %collective-permute-done.5 = bf16[128,1152]{1,0:T(8,128)(2,1)S(1)} collective-permute-done((bf16[128,1152]{1,0:T(8,128)(2,1)S(1)}, bf16[128,1152]{1,0:T(8,128)(2,1)S(1)}, u32[]{:S(2)}, u32[]{:S(2)}) %collective-permute-start.5) | collective-permute-done | bytes 294944 | tf_op jit(solution)/shard_map/ppermute | solution.py:47
  88.0 7.0 %collective-permute-done.6 = bf16[128,1152]{1,0:T(8,128)(2,1)S(1)} collective-permute-done((bf16[128,1152]{1,0:T(8,128)(2,1)S(1)}, bf16[128,1152]{1,0:T(8,128)(2,1)S(1)}, u32[]{:S(2)}, u32[]{:S(2)}) %collective-permute-start.6) | collective-permute-done | bytes 294944 | tf_op jit(solution)/shard_map/ppermute | solution.py:47
  95.4 0.2 constant_dynamic-slice_fusion
  95.7 21.4 %all-to-all-done = bf16[64,16,2048]{2,1,0:T(8,128)(2,1)} async-done(((bf16[64,16,2048]{2,1,0:T(8,128)(2,1)}), bf16[64,16,2048]{2,1,0:T(8,128)(2,1)}, u32[]{:S(2)}, u32[]{:S(2)}) %all-to-all-start) | async-done | bytes 4194336 | tf_op jit(solution)/shard_map/all_to_all | solution.py:98
  117.0 3.5 %fusion.13 = f32[1024,768]{0,1:T(8,128)S(1)} fusion(bf16[1024,2048]{1,0:T(8,128)(2,1)} %bitcast.2, bf16[1024,1152]{1,0:T(8,128)(2,1)S(1)} %bitcast.86), kind=kOutput, calls=%fused_computation.22 | convolution fusion | flops 1610612736 | bytes 6815744 | tf_op jit(solution)/shard_map/dot_general | solution.py:16
  120.5 3.3 %multiply_convert_fusion.2 = (bf16[1024,384]{0,1:T(8,128)(2,1)S(1)}, bf16[1024,384]{0,1:T(8,128)(2,1)S(1)}, bf16[1024,384]{0,1:T(8,128)(2,1)S(1)}) fusion(f32[1024,768]{0,1:T(8,128)S(1)} %fusion.13, bf16[1024,1152]{1,0:T(8,128)(2,1)S(1)} %bitcast.87, bf16[1024,2048]{1,0:T(8,128)(2,1)} %bitcast.2), kind=kOutput, calls=%fused_computation.27 | convolution fusion | flops 811204608 | bytes 8388608 | tf_op jit(solution)/shard_map/dot_general | solution.py:24
  123.8 1.3 convolution_convert_fusion
  125.1 0.0 copy-done.10
  125.2 1.9 convolution_convert_fusion.1
  127.0 2.4 %pad_maximum_fusion = bf16[1024,2048]{1,0:T(8,128)(2,1)} fusion(bf16[1024,1024]{1,0:T(8,128)(2,1)S(1)} %convolution_convert_fusion.1, bf16[1024,1024]{1,0:T(8,128)(2,1)S(1)} %convolution_convert_fusion), kind=kLoop, calls=%fused_computation.1 | loop fusion | flops 8388608 | bytes 8388608 | tf_op jit(solution)/shard_map/concatenate | solution.py:105
  129.4 6.0 %all-to-all-start.1 = ((bf16[64,16,2048]{2,1,0:T(8,128)(2,1)}), bf16[64,16,2048]{2,1,0:T(8,128)(2,1)}, u32[]{:S(2)}, u32[]{:S(2)}) async-start(bf16[64,16,2048]{2,1,0:T(8,128)(2,1)} %bitcast.82), calls=%async_computation.1 | async-start | bytes 8388608 | tf_op jit(solution)/shard_map/all_to_all | solution.py:104
  135.6 2.7 %fusion.19 = bf16[1024,384]{0,1:T(8,128)(2,1)S(1)} fusion(bf16[1024,384]{0,1:T(8,128)(2,1)S(1)} %copy-done.7, bf16[1024,2048]{1,0:T(8,128)(2,1)} %bitcast.2), kind=kOutput, calls=%fused_computation.31 | convolution fusion | flops 805699584 | bytes 3670016 | tf_op jit(solution)/shard_map/dot_general | solution.py:35
  138.3 3.4 %fusion.15 = bf16[1024,768]{0,1:T(8,128)(2,1)S(1)} fusion(bf16[1024,2048]{1,0:T(8,128)(2,1)} %bitcast.2, bf16[1024,384]{0,1:T(8,128)(2,1)S(1)} %copy-done.11, bf16[1024,384]{0,1:T(8,128)(2,1)S(1)} %copy-done.9), kind=kOutput, calls=%fused_computation.24 | convolution fusion | flops 1614544896 | bytes 5242880 | tf_op jit(solution)/shard_map/dot_general | solution.py:32
  141.7 1.7 pad_maximum_fusion.1
  143.4 3.0 %copy.61 = bf16[1024,1152]{1,0:T(8,128)(2,1)S(1)} copy(bf16[1024,1152]{0,1:T(8,128)(2,1)} %pad_maximum_fusion.1) | data formatting | bytes 4718592 | tf_op jit(solution)/shard_map/reshape | solution.py:58
  146.4 1.0 dynamic-slice_bitcast_fusion.6
  147.4 10.7 %collective-permute-start.10 = (bf16[128,1152]{1,0:T(8,128)(2,1)S(1)}, bf16[128,1152]{1,0:T(8,128)(2,1)S(1)}, u32[]{:S(2)}, u32[]{:S(2)}) collective-permute-start(bf16[128,1152]{1,0:T(8,128)(2,1)S(1)} %get-tuple-element.29), channel_id=1, source_target_pairs={{0,256},{64,320},{128,384},{192,448},{256,0},{320,64},{384,128},{4... | collective-permute-start | bytes 884744 | tf_op jit(solution)/shard_map/ppermute | solution.py:63
  158.2 1.9 collective-permute-start.11
  160.1 7.8 %collective-permute-start.12 = (bf16[128,1152]{1,0:T(8,128)(2,1)}, bf16[128,1152]{1,0:T(8,128)(2,1)}, u32[]{:S(2)}, u32[]{:S(2)}) collective-permute-start(bf16[128,1152]{1,0:T(8,128)(2,1)} %get-tuple-element.27), channel_id=1, source_target_pairs={{0,384},{64,448},{128,0},{192,64},{256,128},{320,192},{384,256},{4... | collective-permute-start | bytes 884744 | tf_op jit(solution)/shard_map/ppermute | solution.py:63
  168.0 2.5 %collective-permute-start.13 = (bf16[128,1152]{1,0:T(8,128)(2,1)}, bf16[128,1152]{1,0:T(8,128)(2,1)}, u32[]{:S(2)}, u32[]{:S(2)}) collective-permute-start(bf16[128,1152]{1,0:T(8,128)(2,1)} %get-tuple-element.26), channel_id=1, source_target_pairs={{0,448},{64,0},{128,64},{192,128},{256,192},{320,256},{384,320},{4... | collective-permute-start | bytes 884744 | tf_op jit(solution)/shard_map/ppermute | solution.py:63
  170.5 3.4 %collective-permute-start.7 = (bf16[128,1152]{1,0:T(8,128)(2,1)}, bf16[128,1152]{1,0:T(8,128)(2,1)}, u32[]{:S(2)}, u32[]{:S(2)}) collective-permute-start(bf16[128,1152]{1,0:T(8,128)(2,1)} %get-tuple-element.25), channel_id=1, source_target_pairs={{0,64},{64,128},{128,192},{192,256},{256,320},{320,384},{384,448},... | collective-permute-start | bytes 884744 | tf_op jit(solution)/shard_map/ppermute | solution.py:63
  173.9 2.3 collective-permute-start.8
  176.2 16.8 %collective-permute-done.11 = bf16[128,1152]{1,0:T(8,128)(2,1)S(1)} collective-permute-done((bf16[128,1152]{1,0:T(8,128)(2,1)S(1)}, bf16[128,1152]{1,0:T(8,128)(2,1)S(1)}, u32[]{:S(2)}, u32[]{:S(2)}) %collective-permute-start.11) | collective-permute-done | bytes 294944 | tf_op jit(solution)/shard_map/ppermute | solution.py:63
  192.9 0.7 copy-done.2
  193.6 7.1 %collective-permute-start.9 = (bf16[128,1152]{1,0:T(8,128)(2,1)S(1)}, bf16[128,1152]{1,0:T(8,128)(2,1)}, u32[]{:S(2)}, u32[]{:S(2)}) collective-permute-start(bf16[128,1152]{1,0:T(8,128)(2,1)S(1)} %get-tuple-element.30), channel_id=1, source_target_pairs={{0,192},{64,256},{128,320},{192,384},{256,448},{320,0},{384,64},{4... | collective-permute-start | bytes 884744 | tf_op jit(solution)/shard_map/ppermute | solution.py:63
  200.8 3.4 %collective-permute-done.12 = bf16[128,1152]{1,0:T(8,128)(2,1)} collective-permute-done((bf16[128,1152]{1,0:T(8,128)(2,1)}, bf16[128,1152]{1,0:T(8,128)(2,1)}, u32[]{:S(2)}, u32[]{:S(2)}) %collective-permute-start.12) | collective-permute-done | bytes 294944 | tf_op jit(solution)/shard_map/ppermute | solution.py:63
  204.2 6.9 %collective-permute-done.13 = bf16[128,1152]{1,0:T(8,128)(2,1)} collective-permute-done((bf16[128,1152]{1,0:T(8,128)(2,1)}, bf16[128,1152]{1,0:T(8,128)(2,1)}, u32[]{:S(2)}, u32[]{:S(2)}) %collective-permute-start.13) | collective-permute-done | bytes 294944 | tf_op jit(solution)/shard_map/ppermute | solution.py:63
  211.1 0.0 collective-permute-done.7
  211.1 8.5 %collective-permute-done.9 = bf16[128,1152]{1,0:T(8,128)(2,1)} collective-permute-done((bf16[128,1152]{1,0:T(8,128)(2,1)S(1)}, bf16[128,1152]{1,0:T(8,128)(2,1)}, u32[]{:S(2)}, u32[]{:S(2)}) %collective-permute-start.9) | collective-permute-done | bytes 294944 | tf_op jit(solution)/shard_map/ppermute | solution.py:63
  219.5 1.8 fusion.37
  221.3 0.0 copy-start.4
  221.4 0.8 copy.60
  222.2 0.8 slice_bitcast_fusion
  222.9 8.7 %all-to-all-done.1 = bf16[64,16,2048]{2,1,0:T(8,128)(2,1)} async-done(((bf16[64,16,2048]{2,1,0:T(8,128)(2,1)}), bf16[64,16,2048]{2,1,0:T(8,128)(2,1)}, u32[]{:S(2)}, u32[]{:S(2)}) %all-to-all-start.1) | async-done | bytes 4194336 | tf_op jit(solution)/shard_map/all_to_all | solution.py:104
  231.7 2.3 fusion.3
  234.0 2.8 %fusion.27 = bf16[128,1024]{1,0:T(8,128)(2,1)} fusion(pred[1024,128]{1,0:T(8,128)(4,1)S(1)} %copy-done.4, bf16[1024,2048]{1,0:T(8,128)(2,1)} %bitcast.16), kind=kOutput, calls=%fused_computation.35 | convolution fusion | flops 268566528 | bytes 2490368 | tf_op jit(solution)/shard_map/dot_general | solution.py:124
  236.8 0.8 select_reduce_fusion.2
  237.6 3.4 %fusion.24 = bf16[128,1024]{1,0:T(8,128)(2,1)} fusion(f32[1024,128]{1,0:T(8,128)S(1)} %get-tuple-element.21, bf16[1024,2048]{1,0:T(8,128)(2,1)} %bitcast.16), kind=kOutput, calls=%fused_computation.34 | convolution fusion | flops 1610743808 | bytes 2883584 | tf_op jit(solution)/shard_map/dot_general | solution.py:117
  (45 shorter events, 0.6 us)
Async XLA Ops:
  4.5 5.3 %copy-start.3 = (pred[1024,128]{1,0:T(8,128)(4,1)}, pred[1024,128]{1,0:T(8,128)(4,1)S(1)}, u32[]{:S(2)}) copy-start(pred[1024,128]{1,0:T(8,128)(4,1)S(1)} %fusion.2) | copy-start | bytes 393220
  9.8 11.0 %copy-start.5 = (bf16[1,384,128]{2,1,0:T(8,128)(2,1)S(1)}, bf16[1,384,128]{2,1,0:T(8,128)(2,1)}, u32[]{:S(2)}) copy-start(bf16[1,384,128]{2,1,0:T(8,128)(2,1)} %param.10) | copy-start | bytes 294916
  9.8 11.2 %copy-start = (bf16[1,128,768]{2,1,0:T(8,128)(2,1)S(1)}, bf16[1,128,768]{2,1,0:T(8,128)(2,1)}, u32[]{:S(2)}) copy-start(bf16[1,128,768]{2,1,0:T(8,128)(2,1)} %param.9) | copy-start | bytes 589828
  9.8 107.2 %all-to-all-start = ((bf16[64,16,2048]{2,1,0:T(8,128)(2,1)}), bf16[64,16,2048]{2,1,0:T(8,128)(2,1)}, u32[]{:S(2)}, u32[]{:S(2)}) async-start(bf16[64,16,2048]{2,1,0:T(8,128)(2,1)} %bitcast.85), calls=%async_computation | async-start | bytes 8388608 | tf_op jit(solution)/shard_map/all_to_all | solution.py:98
  21.0 25.0 %collective-permute-start = (bf16[128,1152]{1,0:T(8,128)(2,1)S(1)}, bf16[128,1152]{1,0:T(8,128)(2,1)S(1)}, u32[]{:S(2)}, u32[]{:S(2)}) collective-permute-start(bf16[128,1152]{1,0:T(8,128)(2,1)S(1)} %pad_maximum_fusion.5), channel_id=1, source_target_pairs={{0,448},{64,0},{128,64},{192,128},{256,192},{320,256},{384,320},{4... | collective-permute-start | bytes 884744 | tf_op jit(solution)/shard_map/ppermute | solution.py:47
  31.9 23.2 %collective-permute-start.1 = (bf16[128,1152]{1,0:T(8,128)(2,1)S(1)}, bf16[128,1152]{1,0:T(8,128)(2,1)S(1)}, u32[]{:S(2)}, u32[]{:S(2)}) collective-permute-start(bf16[128,1152]{1,0:T(8,128)(2,1)S(1)} %pad_maximum_fusion.5), channel_id=1, source_target_pairs={{0,384},{64,448},{128,0},{192,64},{256,128},{320,192},{384,256},{4... | collective-permute-start | bytes 884744 | tf_op jit(solution)/shard_map/ppermute | solution.py:47
  34.3 48.3 %collective-permute-start.2 = (bf16[128,1152]{1,0:T(8,128)(2,1)S(1)}, bf16[128,1152]{1,0:T(8,128)(2,1)S(1)}, u32[]{:S(2)}, u32[]{:S(2)}) collective-permute-start(bf16[128,1152]{1,0:T(8,128)(2,1)S(1)} %pad_maximum_fusion.5), channel_id=1, source_target_pairs={{0,320},{64,384},{128,448},{192,0},{256,64},{320,128},{384,192},{4... | collective-permute-start | bytes 884744 | tf_op jit(solution)/shard_map/ppermute | solution.py:47
  36.3 46.4 %collective-permute-start.3 = (bf16[128,1152]{1,0:T(8,128)(2,1)S(1)}, bf16[128,1152]{1,0:T(8,128)(2,1)S(1)}, u32[]{:S(2)}, u32[]{:S(2)}) collective-permute-start(bf16[128,1152]{1,0:T(8,128)(2,1)S(1)} %pad_maximum_fusion.5), channel_id=1, source_target_pairs={{0,256},{64,320},{128,384},{192,448},{256,0},{320,64},{384,128},{4... | collective-permute-start | bytes 884744 | tf_op jit(solution)/shard_map/ppermute | solution.py:47
  44.1 39.3 %collective-permute-start.4 = (bf16[128,1152]{1,0:T(8,128)(2,1)S(1)}, bf16[128,1152]{1,0:T(8,128)(2,1)S(1)}, u32[]{:S(2)}, u32[]{:S(2)}) collective-permute-start(bf16[128,1152]{1,0:T(8,128)(2,1)S(1)} %pad_maximum_fusion.5), channel_id=1, source_target_pairs={{0,192},{64,256},{128,320},{192,384},{256,448},{320,0},{384,64},{4... | collective-permute-start | bytes 884744 | tf_op jit(solution)/shard_map/ppermute | solution.py:47
  46.1 42.0 %collective-permute-start.5 = (bf16[128,1152]{1,0:T(8,128)(2,1)S(1)}, bf16[128,1152]{1,0:T(8,128)(2,1)S(1)}, u32[]{:S(2)}, u32[]{:S(2)}) collective-permute-start(bf16[128,1152]{1,0:T(8,128)(2,1)S(1)} %pad_maximum_fusion.5), channel_id=1, source_target_pairs={{0,128},{64,192},{128,256},{192,320},{256,384},{320,448},{384,0},{... | collective-permute-start | bytes 884744 | tf_op jit(solution)/shard_map/ppermute | solution.py:47
  55.1 40.0 %collective-permute-start.6 = (bf16[128,1152]{1,0:T(8,128)(2,1)S(1)}, bf16[128,1152]{1,0:T(8,128)(2,1)S(1)}, u32[]{:S(2)}, u32[]{:S(2)}) collective-permute-start(bf16[128,1152]{1,0:T(8,128)(2,1)S(1)} %pad_maximum_fusion.5), channel_id=1, source_target_pairs={{0,64},{64,128},{128,192},{192,256},{256,320},{320,384},{384,448},... | collective-permute-start | bytes 884744 | tf_op jit(solution)/shard_map/ppermute | solution.py:47
  123.8 1.3 copy-start.6
  123.8 1.3 copy-start.8
  123.8 1.4 copy-start.10
  129.4 6.1 %copy-start.7 = (bf16[1024,384]{0,1:T(8,128)(2,1)S(1)}, bf16[1024,384]{0,1:T(8,128)(2,1)}, u32[]{:S(2)}) copy-start(bf16[1024,384]{0,1:T(8,128)(2,1)} %copy-done.6) | copy-start | bytes 2359300
  129.4 102.2 %all-to-all-start.1 = ((bf16[64,16,2048]{2,1,0:T(8,128)(2,1)}), bf16[64,16,2048]{2,1,0:T(8,128)(2,1)}, u32[]{:S(2)}, u32[]{:S(2)}) async-start(bf16[64,16,2048]{2,1,0:T(8,128)(2,1)} %bitcast.82), calls=%async_computation.1 | async-start | bytes 8388608 | tf_op jit(solution)/shard_map/all_to_all | solution.py:104
  135.6 2.7 %copy-start.9 = (bf16[1024,384]{0,1:T(8,128)(2,1)S(1)}, bf16[1024,384]{0,1:T(8,128)(2,1)}, u32[]{:S(2)}) copy-start(bf16[1024,384]{0,1:T(8,128)(2,1)} %copy-done.8) | copy-start | bytes 2359300
  135.6 2.7 %copy-start.11 = (bf16[1024,384]{0,1:T(8,128)(2,1)S(1)}, bf16[1024,384]{0,1:T(8,128)(2,1)}, u32[]{:S(2)}) copy-start(bf16[1024,384]{0,1:T(8,128)(2,1)} %copy-done.10) | copy-start | bytes 2359300
  147.4 26.4 %collective-permute-start.10 = (bf16[128,1152]{1,0:T(8,128)(2,1)S(1)}, bf16[128,1152]{1,0:T(8,128)(2,1)S(1)}, u32[]{:S(2)}, u32[]{:S(2)}) collective-permute-start(bf16[128,1152]{1,0:T(8,128)(2,1)S(1)} %get-tuple-element.29), channel_id=1, source_target_pairs={{0,256},{64,320},{128,384},{192,448},{256,0},{320,64},{384,128},{4... | collective-permute-start | bytes 884744 | tf_op jit(solution)/shard_map/ppermute | solution.py:63
  158.2 34.7 %collective-permute-start.11 = (bf16[128,1152]{1,0:T(8,128)(2,1)S(1)}, bf16[128,1152]{1,0:T(8,128)(2,1)S(1)}, u32[]{:S(2)}, u32[]{:S(2)}) collective-permute-start(bf16[128,1152]{1,0:T(8,128)(2,1)S(1)} %get-tuple-element.28), channel_id=1, source_target_pairs={{0,320},{64,384},{128,448},{192,0},{256,64},{320,128},{384,192},{4... | collective-permute-start | bytes 884744 | tf_op jit(solution)/shard_map/ppermute | solution.py:63
  160.1 44.1 %collective-permute-start.12 = (bf16[128,1152]{1,0:T(8,128)(2,1)}, bf16[128,1152]{1,0:T(8,128)(2,1)}, u32[]{:S(2)}, u32[]{:S(2)}) collective-permute-start(bf16[128,1152]{1,0:T(8,128)(2,1)} %get-tuple-element.27), channel_id=1, source_target_pairs={{0,384},{64,448},{128,0},{192,64},{256,128},{320,192},{384,256},{4... | collective-permute-start | bytes 884744 | tf_op jit(solution)/shard_map/ppermute | solution.py:63
  168.0 43.1 %collective-permute-start.13 = (bf16[128,1152]{1,0:T(8,128)(2,1)}, bf16[128,1152]{1,0:T(8,128)(2,1)}, u32[]{:S(2)}, u32[]{:S(2)}) collective-permute-start(bf16[128,1152]{1,0:T(8,128)(2,1)} %get-tuple-element.26), channel_id=1, source_target_pairs={{0,448},{64,0},{128,64},{192,128},{256,192},{320,256},{384,320},{4... | collective-permute-start | bytes 884744 | tf_op jit(solution)/shard_map/ppermute | solution.py:63
  170.5 40.6 %collective-permute-start.7 = (bf16[128,1152]{1,0:T(8,128)(2,1)}, bf16[128,1152]{1,0:T(8,128)(2,1)}, u32[]{:S(2)}, u32[]{:S(2)}) collective-permute-start(bf16[128,1152]{1,0:T(8,128)(2,1)} %get-tuple-element.25), channel_id=1, source_target_pairs={{0,64},{64,128},{128,192},{192,256},{256,320},{320,384},{384,448},... | collective-permute-start | bytes 884744 | tf_op jit(solution)/shard_map/ppermute | solution.py:63
  173.8 19.1 %copy-start.1 = (bf16[128,1152]{1,0:T(8,128)(2,1)}, bf16[128,1152]{1,0:T(8,128)(2,1)S(1)}, u32[]{:S(2)}) copy-start(bf16[128,1152]{1,0:T(8,128)(2,1)S(1)} %collective-permute-done.10) | copy-start | bytes 884740
  173.9 37.2 %collective-permute-start.8 = (bf16[128,1152]{1,0:T(8,128)(2,1)S(1)}, bf16[128,1152]{1,0:T(8,128)(2,1)}, u32[]{:S(2)}, u32[]{:S(2)}) collective-permute-start(bf16[128,1152]{1,0:T(8,128)(2,1)S(1)} %get-tuple-element.31), channel_id=1, source_target_pairs={{0,128},{64,192},{128,256},{192,320},{256,384},{320,448},{384,0},{... | collective-permute-start | bytes 884744 | tf_op jit(solution)/shard_map/ppermute | solution.py:63
  192.9 0.7 copy-start.2
  193.6 25.9 %collective-permute-start.9 = (bf16[128,1152]{1,0:T(8,128)(2,1)S(1)}, bf16[128,1152]{1,0:T(8,128)(2,1)}, u32[]{:S(2)}, u32[]{:S(2)}) collective-permute-start(bf16[128,1152]{1,0:T(8,128)(2,1)S(1)} %get-tuple-element.30), channel_id=1, source_target_pairs={{0,192},{64,256},{128,320},{192,384},{256,448},{320,0},{384,64},{4... | collective-permute-start | bytes 884744 | tf_op jit(solution)/shard_map/ppermute | solution.py:63
  221.3 12.7 %copy-start.4 = (pred[1024,128]{1,0:T(8,128)(4,1)S(1)}, pred[1024,128]{1,0:T(8,128)(4,1)}, u32[]{:S(2)}) copy-start(pred[1024,128]{1,0:T(8,128)(4,1)} %copy-done.3) | copy-start | bytes 393220

commit v4 on v3

--- a/solution.py
+++ b/solution.py
@@ -112,18 +112,21 @@
     sum_in = grads[None, :, :gate_width]
     sum_out = grads[:, gate_width:].T[None]
 
-    back_out = back[:, :width].astype(jnp.float32)
-    back_grad = back[:, width:]
-    moe_out = lax.dot_general(
-        weighted,
-        back_out,
-        (((0,), (0,)), ((), ())),
-        precision=lax.Precision.HIGHEST,
-        preferred_element_type=jnp.float32,
+    high = lax.reduce_precision(weighted, exponent_bits=8, mantissa_bits=7)
+    rest = weighted - high
+    middle = lax.reduce_precision(rest, exponent_bits=8, mantissa_bits=7)
+    low = rest - middle
+    parts = [part.astype(jnp.bfloat16) for part in (high, middle, low)]
+    combine = jnp.concatenate(parts + [select_rows], axis=1)
+    summed = lax.dot_general(
+        combine, back, (((0,), (0,)), ((), ())), preferred_element_type=jnp.float32
+    )
+    moe_out = (
+        summed[:token_count, :width]
+        + summed[token_count : 2 * token_count, :width]
+        + summed[2 * token_count : 3 * token_count, :width]
     ).astype(jnp.bfloat16)
-    token_grads = lax.dot_general(
-        select_rows, back_grad, (((0,), (0,)), ((), ())), preferred_element_type=jnp.float32
-    ).astype(jnp.bfloat16)
+    token_grads = summed[3 * token_count :, width:].astype(jnp.bfloat16)
     token_slot = lax.dot_general(
         cotangent, back[:, :width], (((1,), (1,)), ((), ())), preferred_element_type=jnp.float32
     )

time: 242 us -> 242 us (level)
  other arithmetic: 10.3 us -> 12.8 us
    convert_element_type x0 -> x3, other arithmetic: none -> 2.53 us  [the longest x1 0.97 us: local(): parts = [part.astype(jnp.bfloat16) for part in (high, middle, low)]]
    dot_general x2 -> x1, matrix products: 6.19 us -> 4.84 us  [local(): lax.dot_general(combine, back, (((0,), (0,)), ((), ())), preferred_elemen...]
where the time goes in v4:
time: 242 us; the launch traced here: 241 us
  waiting for transfers between devices  107 us (44%)
  starting transfers between devices  83.1 us (34%)
  matrix products  27.3 us (11%)
  other arithmetic  12.8 us (5%)
  local copies, waits for them, and re-layouts  9.4 us (4%)
    ppermute x7, waiting for transfers between devices, gather_dp(): pieces.append(lax.ppermute(block, 'dp', pairs))  43.5 us
    ppermute x7, starting transfers between devices, scatter_dp(): total = total + lax.ppermute(part, 'dp', pairs).astype(jnp.float32)  35.8 us
    ppermute x7, waiting for transfers between devices, scatter_dp(): total = total + lax.ppermute(part, 'dp', pairs).astype(jnp.float32)  33.8 us
    ppermute x7, starting transfers between devices, gather_dp(): pieces.append(lax.ppermute(block, 'dp', pairs))  30.3 us
    all_to_all x1, waiting for transfers between devices, local(): lax.all_to_all(send, 'expert', split_axis=0, concat_axis=0, tiled=True)  21.4 us
    all_to_all x1, starting transfers between devices, local(): lax.all_to_all(send, 'expert', split_axis=0, concat_axis=0, tiled=True)  11 us
    all_to_all x1, waiting for transfers between devices, local(): lax.all_to_all(jnp.concatenate([row_major(expert_out), row_major(grad_in)...  8.62 us
    all_to_all x1, starting transfers between devices, local(): lax.all_to_all(jnp.concatenate([row_major(expert_out), row_major(grad_in)...  6.02 us
  transfers between devices with their start and end apart: 16, of which 11 were waited for; matrix products, arithmetic and copies ran while one was open for 7% of the time, Pallas kernels for 0%

profile of v4, /device:TPU:6, one launch (start us, length us, event | category | flops | bytes accessed | tf_op | source)
XLA Modules:
  0.0 241.1 jit_solution(17061691347265732292)
XLA Ops:
  0.6 0.8 copy.47
  1.4 0.1 eq.50
  1.5 0.1 eq.46
  1.7 1.2 reduce-window.6
  2.9 0.2 slice_reduce_fusion
  3.1 0.1 fusion.43
  3.3 0.1 reduce_sum.39
  3.4 0.1 copy.50
  3.5 0.7 multiply_add_fusion
  4.2 0.4 fusion.2
  4.5 1.0 select_reduce_fusion.1
  5.5 4.2 %multiply_convert_fusion = bf16[1024,2048]{1,0:T(8,128)(2,1)} fusion(pred[1024,128]{1,0:T(8,128)(4,1)S(1)} %fusion.2, f32[1024]{0:T(1024)S(1)} %get-tuple-element.21, pred[2048]{0:T(1024)(128)(4,1)S(1)} %iota_compare_fusion.3, bf16[128,1024]{1,0:T(8,128)(2,1)} %param.11, bf16[128,1024]{1,0:T(8,128)(2,1)} %param.6), kind=kOutput, calls=%fused_computation | convolution fusion | flops 544210944 | bytes 4855808 | tf_op jit(solution)/shard_map/dot_general | solution.py:94
  9.8 11.0 %all-to-all-start = ((bf16[64,16,2048]{2,1,0:T(8,128)(2,1)}), bf16[64,16,2048]{2,1,0:T(8,128)(2,1)}, u32[]{:S(2)}, u32[]{:S(2)}) async-start(bf16[64,16,2048]{2,1,0:T(8,128)(2,1)} %bitcast.84), calls=%async_computation | async-start | bytes 8388608 | tf_op jit(solution)/shard_map/all_to_all | solution.py:98
  20.8 0.1 copy.51
  21.0 10.9 %collective-permute-start = (bf16[128,1152]{1,0:T(8,128)(2,1)S(1)}, bf16[128,1152]{1,0:T(8,128)(2,1)S(1)}, u32[]{:S(2)}, u32[]{:S(2)}) collective-permute-start(bf16[128,1152]{1,0:T(8,128)(2,1)S(1)} %pad_maximum_fusion.5), channel_id=1, source_target_pairs={{0,448},{64,0},{128,64},{192,128},{256,192},{320,256},{384,320},{4... | collective-permute-start | bytes 884744 | tf_op jit(solution)/shard_map/ppermute | solution.py:47
  31.8 2.5 %collective-permute-start.1 = (bf16[128,1152]{1,0:T(8,128)(2,1)S(1)}, bf16[128,1152]{1,0:T(8,128)(2,1)S(1)}, u32[]{:S(2)}, u32[]{:S(2)}) collective-permute-start(bf16[128,1152]{1,0:T(8,128)(2,1)S(1)} %pad_maximum_fusion.5), channel_id=1, source_target_pairs={{0,384},{64,448},{128,0},{192,64},{256,128},{320,192},{384,256},{4... | collective-permute-start | bytes 884744 | tf_op jit(solution)/shard_map/ppermute | solution.py:47
  34.3 1.9 collective-permute-start.2
  36.2 7.8 %collective-permute-start.3 = (bf16[128,1152]{1,0:T(8,128)(2,1)S(1)}, bf16[128,1152]{1,0:T(8,128)(2,1)S(1)}, u32[]{:S(2)}, u32[]{:S(2)}) collective-permute-start(bf16[128,1152]{1,0:T(8,128)(2,1)S(1)} %pad_maximum_fusion.5), channel_id=1, source_target_pairs={{0,256},{64,320},{128,384},{192,448},{256,0},{320,64},{384,128},{4... | collective-permute-start | bytes 884744 | tf_op jit(solution)/shard_map/ppermute | solution.py:47
  44.1 1.9 collective-permute-start.4
  46.0 3.4 %collective-permute-start.5 = (bf16[128,1152]{1,0:T(8,128)(2,1)S(1)}, bf16[128,1152]{1,0:T(8,128)(2,1)S(1)}, u32[]{:S(2)}, u32[]{:S(2)}) collective-permute-start(bf16[128,1152]{1,0:T(8,128)(2,1)S(1)} %pad_maximum_fusion.5), channel_id=1, source_target_pairs={{0,128},{64,192},{128,256},{192,320},{256,384},{320,448},{384,0},{... | collective-permute-start | bytes 884744 | tf_op jit(solution)/shard_map/ppermute | solution.py:47
  49.4 5.6 %collective-permute-done.1 = bf16[128,1152]{1,0:T(8,128)(2,1)S(1)} collective-permute-done((bf16[128,1152]{1,0:T(8,128)(2,1)S(1)}, bf16[128,1152]{1,0:T(8,128)(2,1)S(1)}, u32[]{:S(2)}, u32[]{:S(2)}) %collective-permute-start.1) | collective-permute-done | bytes 294944 | tf_op jit(solution)/shard_map/ppermute | solution.py:47
  55.1 1.9 collective-permute-start.6
  57.0 25.6 %collective-permute-done.2 = bf16[128,1152]{1,0:T(8,128)(2,1)S(1)} collective-permute-done((bf16[128,1152]{1,0:T(8,128)(2,1)S(1)}, bf16[128,1152]{1,0:T(8,128)(2,1)S(1)}, u32[]{:S(2)}, u32[]{:S(2)}) %collective-permute-start.2) | collective-permute-done | bytes 294944 | tf_op jit(solution)/shard_map/ppermute | solution.py:47
  82.6 0.0 collective-permute-done.3
  82.7 0.7 collective-permute-done.4
  83.4 4.6 %collective-permute-done.5 = bf16[128,1152]{1,0:T(8,128)(2,1)S(1)} collective-permute-done((bf16[128,1152]{1,0:T(8,128)(2,1)S(1)}, bf16[128,1152]{1,0:T(8,128)(2,1)S(1)}, u32[]{:S(2)}, u32[]{:S(2)}) %collective-permute-start.5) | collective-permute-done | bytes 294944 | tf_op jit(solution)/shard_map/ppermute | solution.py:47
  88.0 7.0 %collective-permute-done.6 = bf16[128,1152]{1,0:T(8,128)(2,1)S(1)} collective-permute-done((bf16[128,1152]{1,0:T(8,128)(2,1)S(1)}, bf16[128,1152]{1,0:T(8,128)(2,1)S(1)}, u32[]{:S(2)}, u32[]{:S(2)}) %collective-permute-start.6) | collective-permute-done | bytes 294944 | tf_op jit(solution)/shard_map/ppermute | solution.py:47
  95.4 0.2 constant_dynamic-slice_fusion
  95.6 21.4 %all-to-all-done = bf16[64,16,2048]{2,1,0:T(8,128)(2,1)} async-done(((bf16[64,16,2048]{2,1,0:T(8,128)(2,1)}), bf16[64,16,2048]{2,1,0:T(8,128)(2,1)}, u32[]{:S(2)}, u32[]{:S(2)}) %all-to-all-start) | async-done | bytes 4194336 | tf_op jit(solution)/shard_map/all_to_all | solution.py:98
  117.0 3.5 %fusion.9 = f32[1024,768]{0,1:T(8,128)S(1)} fusion(bf16[1024,2048]{1,0:T(8,128)(2,1)} %bitcast.2, bf16[1024,1152]{1,0:T(8,128)(2,1)S(1)} %bitcast.85), kind=kOutput, calls=%fused_computation.18 | convolution fusion | flops 1610612736 | bytes 6815744 | tf_op jit(solution)/shard_map/dot_general | solution.py:16
  120.5 3.3 %multiply_convert_fusion.2 = (bf16[1024,384]{0,1:T(8,128)(2,1)S(1)}, bf16[1024,384]{0,1:T(8,128)(2,1)S(1)}, bf16[1024,384]{0,1:T(8,128)(2,1)S(1)}) fusion(f32[1024,768]{0,1:T(8,128)S(1)} %fusion.9, bf16[1024,1152]{1,0:T(8,128)(2,1)S(1)} %bitcast.86, bf16[1024,2048]{1,0:T(8,128)(2,1)} %bitcast.2), kind=kOutput, calls=%fused_computation.23 | convolution fusion | flops 811204608 | bytes 8388608 | tf_op jit(solution)/shard_map/dot_general | solution.py:24
  123.8 1.3 convolution_convert_fusion
  125.1 0.0 copy-done.11
  125.1 1.9 convolution_convert_fusion.1
  127.0 2.4 pad_maximum_fusion
  129.4 6.0 %all-to-all-start.1 = ((bf16[64,16,2048]{2,1,0:T(8,128)(2,1)}), bf16[64,16,2048]{2,1,0:T(8,128)(2,1)}, u32[]{:S(2)}, u32[]{:S(2)}) async-start(bf16[64,16,2048]{2,1,0:T(8,128)(2,1)} %bitcast.81), calls=%async_computation.1 | async-start | bytes 8388608 | tf_op jit(solution)/shard_map/all_to_all | solution.py:104
  135.6 2.7 %fusion.15 = bf16[1024,384]{0,1:T(8,128)(2,1)S(1)} fusion(bf16[1024,384]{0,1:T(8,128)(2,1)S(1)} %copy-done.8, bf16[1024,2048]{1,0:T(8,128)(2,1)} %bitcast.2), kind=kOutput, calls=%fused_computation.27 | convolution fusion | flops 805699584 | bytes 3670016 | tf_op jit(solution)/shard_map/dot_general | solution.py:35
  138.3 3.4 %fusion.11 = bf16[1024,768]{0,1:T(8,128)(2,1)S(1)} fusion(bf16[1024,2048]{1,0:T(8,128)(2,1)} %bitcast.2, bf16[1024,384]{0,1:T(8,128)(2,1)S(1)} %copy-done.12, bf16[1024,384]{0,1:T(8,128)(2,1)S(1)} %copy-done.10), kind=kOutput, calls=%fused_computation.20 | convolution fusion | flops 1614544896 | bytes 5242880 | tf_op jit(solution)/shard_map/dot_general | solution.py:32
  141.7 1.7 pad_maximum_fusion.1
  143.3 3.0 %copy.61 = bf16[1024,1152]{1,0:T(8,128)(2,1)S(1)} copy(bf16[1024,1152]{0,1:T(8,128)(2,1)} %pad_maximum_fusion.1) | data formatting | bytes 4718592 | tf_op jit(solution)/shard_map/reshape | solution.py:58
  146.4 1.1 dynamic-slice_bitcast_fusion.6
  147.5 10.7 %collective-permute-start.10 = (bf16[128,1152]{1,0:T(8,128)(2,1)S(1)}, bf16[128,1152]{1,0:T(8,128)(2,1)S(1)}, u32[]{:S(2)}, u32[]{:S(2)}) collective-permute-start(bf16[128,1152]{1,0:T(8,128)(2,1)S(1)} %get-tuple-element.29), channel_id=1, source_target_pairs={{0,256},{64,320},{128,384},{192,448},{256,0},{320,64},{384,128},{4... | collective-permute-start | bytes 884744 | tf_op jit(solution)/shard_map/ppermute | solution.py:63
  158.2 1.9 collective-permute-start.11
  160.2 7.8 %collective-permute-start.12 = (bf16[128,1152]{1,0:T(8,128)(2,1)}, bf16[128,1152]{1,0:T(8,128)(2,1)}, u32[]{:S(2)}, u32[]{:S(2)}) collective-permute-start(bf16[128,1152]{1,0:T(8,128)(2,1)} %get-tuple-element.27), channel_id=1, source_target_pairs={{0,384},{64,448},{128,0},{192,64},{256,128},{320,192},{384,256},{4... | collective-permute-start | bytes 884744 | tf_op jit(solution)/shard_map/ppermute | solution.py:63
  168.0 2.5 %collective-permute-start.13 = (bf16[128,1152]{1,0:T(8,128)(2,1)}, bf16[128,1152]{1,0:T(8,128)(2,1)}, u32[]{:S(2)}, u32[]{:S(2)}) collective-permute-start(bf16[128,1152]{1,0:T(8,128)(2,1)} %get-tuple-element.26), channel_id=1, source_target_pairs={{0,448},{64,0},{128,64},{192,128},{256,192},{320,256},{384,320},{4... | collective-permute-start | bytes 884744 | tf_op jit(solution)/shard_map/ppermute | solution.py:63
  170.5 3.4 %collective-permute-start.7 = (bf16[128,1152]{1,0:T(8,128)(2,1)}, bf16[128,1152]{1,0:T(8,128)(2,1)}, u32[]{:S(2)}, u32[]{:S(2)}) collective-permute-start(bf16[128,1152]{1,0:T(8,128)(2,1)} %get-tuple-element.25), channel_id=1, source_target_pairs={{0,64},{64,128},{128,192},{192,256},{256,320},{320,384},{384,448},... | collective-permute-start | bytes 884744 | tf_op jit(solution)/shard_map/ppermute | solution.py:63
  173.9 2.3 collective-permute-start.8
  176.2 16.8 %collective-permute-done.11 = bf16[128,1152]{1,0:T(8,128)(2,1)S(1)} collective-permute-done((bf16[128,1152]{1,0:T(8,128)(2,1)S(1)}, bf16[128,1152]{1,0:T(8,128)(2,1)S(1)}, u32[]{:S(2)}, u32[]{:S(2)}) %collective-permute-start.11) | collective-permute-done | bytes 294944 | tf_op jit(solution)/shard_map/ppermute | solution.py:63
  193.0 0.7 copy-done.2
  193.7 7.1 %collective-permute-start.9 = (bf16[128,1152]{1,0:T(8,128)(2,1)S(1)}, bf16[128,1152]{1,0:T(8,128)(2,1)}, u32[]{:S(2)}, u32[]{:S(2)}) collective-permute-start(bf16[128,1152]{1,0:T(8,128)(2,1)S(1)} %get-tuple-element.30), channel_id=1, source_target_pairs={{0,192},{64,256},{128,320},{192,384},{256,448},{320,0},{384,64},{4... | collective-permute-start | bytes 884744 | tf_op jit(solution)/shard_map/ppermute | solution.py:63
  200.8 0.8 convert_element_type.74
  201.6 1.0 reduce-precision_convert_fusion.1
  202.5 1.7 collective-permute-done.12
  204.2 6.9 %collective-permute-done.13 = bf16[128,1152]{1,0:T(8,128)(2,1)} collective-permute-done((bf16[128,1152]{1,0:T(8,128)(2,1)}, bf16[128,1152]{1,0:T(8,128)(2,1)}, u32[]{:S(2)}, u32[]{:S(2)}) %collective-permute-start.13) | collective-permute-done | bytes 294944 | tf_op jit(solution)/shard_map/ppermute | solution.py:63
  211.1 8.5 %collective-permute-done.9 = bf16[128,1152]{1,0:T(8,128)(2,1)} collective-permute-done((bf16[128,1152]{1,0:T(8,128)(2,1)S(1)}, bf16[128,1152]{1,0:T(8,128)(2,1)}, u32[]{:S(2)}, u32[]{:S(2)}) %collective-permute-start.9) | collective-permute-done | bytes 294944 | tf_op jit(solution)/shard_map/ppermute | solution.py:63
  219.6 1.8 fusion.35
  221.4 0.8 copy.60
  222.2 0.8 slice_bitcast_fusion
  223.0 8.6 %all-to-all-done.1 = bf16[64,16,2048]{2,1,0:T(8,128)(2,1)} async-done(((bf16[64,16,2048]{2,1,0:T(8,128)(2,1)}), bf16[64,16,2048]{2,1,0:T(8,128)(2,1)}, u32[]{:S(2)}, u32[]{:S(2)}) %all-to-all-start.1) | async-done | bytes 4194336 | tf_op jit(solution)/shard_map/all_to_all | solution.py:104
  231.6 4.8 %fusion.20 = f32[512,2048]{1,0:T(8,128)S(1)} fusion(bf16[1024,2048]{1,0:T(8,128)(2,1)} %bitcast.16, bf16[1024,128]{1,0:T(8,128)(2,1)} %convert_element_type.74, bf16[1024,128]{1,0:T(8,128)(2,1)S(1)} %copy-done.4, bf16[1024,128]{1,0:T(8,128)(2,1)} %get-tuple-element.34, bf16[1024,128]{1,0:T(8,128)(2,1)S(1)} %copy-done.3), kind=kOutput, calls=%fused_computation.30 | convolution fusion | flops 2151677952 | bytes 9437184 | tf_op jit(solution)/shard_map/dot_general | solution.py:121
  236.5 0.8 fusion.37
  237.3 0.7 slice.116
  238.0 2.3 fusion
  240.3 0.8 select_reduce_fusion.2
  (50 shorter events, 0.6 us)
Async XLA Ops:
  9.8 11.0 %copy-start.5 = (bf16[1,384,128]{2,1,0:T(8,128)(2,1)S(1)}, bf16[1,384,128]{2,1,0:T(8,128)(2,1)}, u32[]{:S(2)}) copy-start(bf16[1,384,128]{2,1,0:T(8,128)(2,1)} %param.10) | copy-start | bytes 294916
  9.8 11.2 %copy-start = (bf16[1,128,768]{2,1,0:T(8,128)(2,1)S(1)}, bf16[1,128,768]{2,1,0:T(8,128)(2,1)}, u32[]{:S(2)}) copy-start(bf16[1,128,768]{2,1,0:T(8,128)(2,1)} %param.9) | copy-start | bytes 589828
  9.8 107.2 %all-to-all-start = ((bf16[64,16,2048]{2,1,0:T(8,128)(2,1)}), bf16[64,16,2048]{2,1,0:T(8,128)(2,1)}, u32[]{:S(2)}, u32[]{:S(2)}) async-start(bf16[64,16,2048]{2,1,0:T(8,128)(2,1)} %bitcast.84), calls=%async_computation | async-start | bytes 8388608 | tf_op jit(solution)/shard_map/all_to_all | solution.py:98
  21.0 25.0 %collective-permute-start = (bf16[128,1152]{1,0:T(8,128)(2,1)S(1)}, bf16[128,1152]{1,0:T(8,128)(2,1)S(1)}, u32[]{:S(2)}, u32[]{:S(2)}) collective-permute-start(bf16[128,1152]{1,0:T(8,128)(2,1)S(1)} %pad_maximum_fusion.5), channel_id=1, source_target_pairs={{0,448},{64,0},{128,64},{192,128},{256,192},{320,256},{384,320},{4... | collective-permute-start | bytes 884744 | tf_op jit(solution)/shard_map/ppermute | solution.py:47
  31.8 23.2 %collective-permute-start.1 = (bf16[128,1152]{1,0:T(8,128)(2,1)S(1)}, bf16[128,1152]{1,0:T(8,128)(2,1)S(1)}, u32[]{:S(2)}, u32[]{:S(2)}) collective-permute-start(bf16[128,1152]{1,0:T(8,128)(2,1)S(1)} %pad_maximum_fusion.5), channel_id=1, source_target_pairs={{0,384},{64,448},{128,0},{192,64},{256,128},{320,192},{384,256},{4... | collective-permute-start | bytes 884744 | tf_op jit(solution)/shard_map/ppermute | solution.py:47
  34.3 48.3 %collective-permute-start.2 = (bf16[128,1152]{1,0:T(8,128)(2,1)S(1)}, bf16[128,1152]{1,0:T(8,128)(2,1)S(1)}, u32[]{:S(2)}, u32[]{:S(2)}) collective-permute-start(bf16[128,1152]{1,0:T(8,128)(2,1)S(1)} %pad_maximum_fusion.5), channel_id=1, source_target_pairs={{0,320},{64,384},{128,448},{192,0},{256,64},{320,128},{384,192},{4... | collective-permute-start | bytes 884744 | tf_op jit(solution)/shard_map/ppermute | solution.py:47
  36.2 46.4 %collective-permute-start.3 = (bf16[128,1152]{1,0:T(8,128)(2,1)S(1)}, bf16[128,1152]{1,0:T(8,128)(2,1)S(1)}, u32[]{:S(2)}, u32[]{:S(2)}) collective-permute-start(bf16[128,1152]{1,0:T(8,128)(2,1)S(1)} %pad_maximum_fusion.5), channel_id=1, source_target_pairs={{0,256},{64,320},{128,384},{192,448},{256,0},{320,64},{384,128},{4... | collective-permute-start | bytes 884744 | tf_op jit(solution)/shard_map/ppermute | solution.py:47
  44.1 39.3 %collective-permute-start.4 = (bf16[128,1152]{1,0:T(8,128)(2,1)S(1)}, bf16[128,1152]{1,0:T(8,128)(2,1)S(1)}, u32[]{:S(2)}, u32[]{:S(2)}) collective-permute-start(bf16[128,1152]{1,0:T(8,128)(2,1)S(1)} %pad_maximum_fusion.5), channel_id=1, source_target_pairs={{0,192},{64,256},{128,320},{192,384},{256,448},{320,0},{384,64},{4... | collective-permute-start | bytes 884744 | tf_op jit(solution)/shard_map/ppermute | solution.py:47
  46.0 42.0 %collective-permute-start.5 = (bf16[128,1152]{1,0:T(8,128)(2,1)S(1)}, bf16[128,1152]{1,0:T(8,128)(2,1)S(1)}, u32[]{:S(2)}, u32[]{:S(2)}) collective-permute-start(bf16[128,1152]{1,0:T(8,128)(2,1)S(1)} %pad_maximum_fusion.5), channel_id=1, source_target_pairs={{0,128},{64,192},{128,256},{192,320},{256,384},{320,448},{384,0},{... | collective-permute-start | bytes 884744 | tf_op jit(solution)/shard_map/ppermute | solution.py:47
  55.1 40.0 %collective-permute-start.6 = (bf16[128,1152]{1,0:T(8,128)(2,1)S(1)}, bf16[128,1152]{1,0:T(8,128)(2,1)S(1)}, u32[]{:S(2)}, u32[]{:S(2)}) collective-permute-start(bf16[128,1152]{1,0:T(8,128)(2,1)S(1)} %pad_maximum_fusion.5), channel_id=1, source_target_pairs={{0,64},{64,128},{128,192},{192,256},{256,320},{320,384},{384,448},... | collective-permute-start | bytes 884744 | tf_op jit(solution)/shard_map/ppermute | solution.py:47
  123.7 1.3 copy-start.7
  123.7 1.3 copy-start.9
  123.7 1.4 copy-start.11
  129.4 6.1 %copy-start.8 = (bf16[1024,384]{0,1:T(8,128)(2,1)S(1)}, bf16[1024,384]{0,1:T(8,128)(2,1)}, u32[]{:S(2)}) copy-start(bf16[1024,384]{0,1:T(8,128)(2,1)} %copy-done.7) | copy-start | bytes 2359300
  129.4 102.2 %all-to-all-start.1 = ((bf16[64,16,2048]{2,1,0:T(8,128)(2,1)}), bf16[64,16,2048]{2,1,0:T(8,128)(2,1)}, u32[]{:S(2)}, u32[]{:S(2)}) async-start(bf16[64,16,2048]{2,1,0:T(8,128)(2,1)} %bitcast.81), calls=%async_computation.1 | async-start | bytes 8388608 | tf_op jit(solution)/shard_map/all_to_all | solution.py:104
  135.5 2.7 %copy-start.10 = (bf16[1024,384]{0,1:T(8,128)(2,1)S(1)}, bf16[1024,384]{0,1:T(8,128)(2,1)}, u32[]{:S(2)}) copy-start(bf16[1024,384]{0,1:T(8,128)(2,1)} %copy-done.9) | copy-start | bytes 2359300
  135.5 2.7 %copy-start.12 = (bf16[1024,384]{0,1:T(8,128)(2,1)S(1)}, bf16[1024,384]{0,1:T(8,128)(2,1)}, u32[]{:S(2)}) copy-start(bf16[1024,384]{0,1:T(8,128)(2,1)} %copy-done.11) | copy-start | bytes 2359300
  147.5 26.4 %collective-permute-start.10 = (bf16[128,1152]{1,0:T(8,128)(2,1)S(1)}, bf16[128,1152]{1,0:T(8,128)(2,1)S(1)}, u32[]{:S(2)}, u32[]{:S(2)}) collective-permute-start(bf16[128,1152]{1,0:T(8,128)(2,1)S(1)} %get-tuple-element.29), channel_id=1, source_target_pairs={{0,256},{64,320},{128,384},{192,448},{256,0},{320,64},{384,128},{4... | collective-permute-start | bytes 884744 | tf_op jit(solution)/shard_map/ppermute | solution.py:63
  158.2 34.7 %collective-permute-start.11 = (bf16[128,1152]{1,0:T(8,128)(2,1)S(1)}, bf16[128,1152]{1,0:T(8,128)(2,1)S(1)}, u32[]{:S(2)}, u32[]{:S(2)}) collective-permute-start(bf16[128,1152]{1,0:T(8,128)(2,1)S(1)} %get-tuple-element.28), channel_id=1, source_target_pairs={{0,320},{64,384},{128,448},{192,0},{256,64},{320,128},{384,192},{4... | collective-permute-start | bytes 884744 | tf_op jit(solution)/shard_map/ppermute | solution.py:63
  160.2 44.1 %collective-permute-start.12 = (bf16[128,1152]{1,0:T(8,128)(2,1)}, bf16[128,1152]{1,0:T(8,128)(2,1)}, u32[]{:S(2)}, u32[]{:S(2)}) collective-permute-start(bf16[128,1152]{1,0:T(8,128)(2,1)} %get-tuple-element.27), channel_id=1, source_target_pairs={{0,384},{64,448},{128,0},{192,64},{256,128},{320,192},{384,256},{4... | collective-permute-start | bytes 884744 | tf_op jit(solution)/shard_map/ppermute | solution.py:63
  168.0 43.1 %collective-permute-start.13 = (bf16[128,1152]{1,0:T(8,128)(2,1)}, bf16[128,1152]{1,0:T(8,128)(2,1)}, u32[]{:S(2)}, u32[]{:S(2)}) collective-permute-start(bf16[128,1152]{1,0:T(8,128)(2,1)} %get-tuple-element.26), channel_id=1, source_target_pairs={{0,448},{64,0},{128,64},{192,128},{256,192},{320,256},{384,320},{4... | collective-permute-start | bytes 884744 | tf_op jit(solution)/shard_map/ppermute | solution.py:63
  170.5 40.6 %collective-permute-start.7 = (bf16[128,1152]{1,0:T(8,128)(2,1)}, bf16[128,1152]{1,0:T(8,128)(2,1)}, u32[]{:S(2)}, u32[]{:S(2)}) collective-permute-start(bf16[128,1152]{1,0:T(8,128)(2,1)} %get-tuple-element.25), channel_id=1, source_target_pairs={{0,64},{64,128},{128,192},{192,256},{256,320},{320,384},{384,448},... | collective-permute-start | bytes 884744 | tf_op jit(solution)/shard_map/ppermute | solution.py:63
  173.9 19.1 %copy-start.1 = (bf16[128,1152]{1,0:T(8,128)(2,1)}, bf16[128,1152]{1,0:T(8,128)(2,1)S(1)}, u32[]{:S(2)}) copy-start(bf16[128,1152]{1,0:T(8,128)(2,1)S(1)} %collective-permute-done.10) | copy-start | bytes 884740
  173.9 37.2 %collective-permute-start.8 = (bf16[128,1152]{1,0:T(8,128)(2,1)}, bf16[128,1152]{1,0:T(8,128)(2,1)}, u32[]{:S(2)}, u32[]{:S(2)}) collective-permute-start(bf16[128,1152]{1,0:T(8,128)(2,1)} %get-tuple-element.31), channel_id=1, source_target_pairs={{0,128},{64,192},{128,256},{192,320},{256,384},{320,448},{384,0},{... | collective-permute-start | bytes 884744 | tf_op jit(solution)/shard_map/ppermute | solution.py:63
  193.0 0.7 copy-start.2
  193.7 25.9 %collective-permute-start.9 = (bf16[128,1152]{1,0:T(8,128)(2,1)S(1)}, bf16[128,1152]{1,0:T(8,128)(2,1)}, u32[]{:S(2)}, u32[]{:S(2)}) collective-permute-start(bf16[128,1152]{1,0:T(8,128)(2,1)S(1)} %get-tuple-element.30), channel_id=1, source_target_pairs={{0,192},{64,256},{128,320},{192,384},{256,448},{320,0},{384,64},{4... | collective-permute-start | bytes 884744 | tf_op jit(solution)/shard_map/ppermute | solution.py:63
  219.6 12.1 %copy-start.3 = (bf16[1024,128]{1,0:T(8,128)(2,1)S(1)}, bf16[1024,128]{1,0:T(8,128)(2,1)}, u32[]{:S(2)}) copy-start(bf16[1024,128]{1,0:T(8,128)(2,1)} %get-tuple-element.32) | copy-start | bytes 786436
  219.6 12.1 %copy-start.4 = (bf16[1024,128]{1,0:T(8,128)(2,1)S(1)}, bf16[1024,128]{1,0:T(8,128)(2,1)}, u32[]{:S(2)}) copy-start(bf16[1024,128]{1,0:T(8,128)(2,1)} %get-tuple-element.33) | copy-start | bytes 786436
  231.6 6.4 %copy-start.6 = (bf16[128,1024]{1,0:T(8,128)(2,1)S(1)}, bf16[128,1024]{1,0:T(8,128)(2,1)}, u32[]{:S(2)}) copy-start(bf16[128,1024]{1,0:T(8,128)(2,1)} %param.11) | copy-start | bytes 786436

commit v5 on v4

--- a/solution.py
+++ b/solution.py
@@ -13,7 +13,7 @@
     hidden_width = weight_out_t.shape[1]
     contract_last = (((1,), (1,)), ((), ()))
     contract_first = (((0,), (0,)), ((), ()))
-    pre_act = jnp.dot(rows_in, weight_in, preferred_element_type=jnp.float32)
+    pre_act = row_major(jnp.dot(rows_in, weight_in, preferred_element_type=jnp.float32))
     pre_gate = pre_act[:, :hidden_width]
     up_value = pre_act[:, hidden_width:]
     act = jax.nn.silu(pre_gate)

time: 242 us -> 242 us (level)
  no operation moved by 1% of the time
where the time goes in v5:
time: 242 us; the launch traced here: 241 us
  waiting for transfers between devices  107 us (44%)
  starting transfers between devices  82.9 us (34%)
  matrix products  27.5 us (11%)
  other arithmetic  12.8 us (5%)
  local copies, waits for them, and re-layouts  9.43 us (4%)
    ppermute x7, waiting for transfers between devices, gather_dp(): pieces.append(lax.ppermute(block, 'dp', pairs))  43.5 us
    ppermute x7, starting transfers between devices, scatter_dp(): total = total + lax.ppermute(part, 'dp', pairs).astype(jnp.float32)  35.8 us
    ppermute x7, waiting for transfers between devices, scatter_dp(): total = total + lax.ppermute(part, 'dp', pairs).astype(jnp.float32)  33.8 us
    ppermute x7, starting transfers between devices, gather_dp(): pieces.append(lax.ppermute(block, 'dp', pairs))  30.3 us
    all_to_all x1, waiting for transfers between devices, local(): lax.all_to_all(send, 'expert', split_axis=0, concat_axis=0, tiled=True)  21.4 us
    all_to_all x1, starting transfers between devices, local(): lax.all_to_all(send, 'expert', split_axis=0, concat_axis=0, tiled=True)  11 us
    all_to_all x1, waiting for transfers between devices, local(): lax.all_to_all(jnp.concatenate([row_major(expert_out), row_major(grad_in)...  8.48 us
    all_to_all x1, starting transfers between devices, local(): lax.all_to_all(jnp.concatenate([row_major(expert_out), row_major(grad_in)...  5.85 us
  transfers between devices with their start and end apart: 16, of which 11 were waited for; matrix products, arithmetic and copies ran while one was open for 7% of the time, Pallas kernels for 0%

profile of v5, /device:TPU:6, one launch (start us, length us, event | category | flops | bytes accessed | tf_op | source)
XLA Modules:
  0.0 241.1 jit_solution(13106915896679685020)
XLA Ops:
  0.6 0.8 copy.53
  1.4 0.1 eq.50
  1.5 0.1 eq.46
  1.7 1.2 reduce-window.6
  2.9 0.2 slice_reduce_fusion
  3.1 0.1 fusion.43
  3.3 0.1 reduce_sum.39
  3.4 0.1 copy.56
  3.5 0.7 multiply_add_fusion
  4.2 0.4 fusion.2
  4.5 1.0 select_reduce_fusion.1
  5.5 4.2 %multiply_convert_fusion = bf16[1024,2048]{1,0:T(8,128)(2,1)} fusion(pred[1024,128]{1,0:T(8,128)(4,1)S(1)} %fusion.2, f32[1024]{0:T(1024)S(1)} %get-tuple-element.21, pred[2048]{0:T(1024)(128)(4,1)S(1)} %iota_compare_fusion.3, bf16[128,1024]{1,0:T(8,128)(2,1)} %param.11, bf16[128,1024]{1,0:T(8,128)(2,1)} %param.6), kind=kOutput, calls=%fused_computation | convolution fusion | flops 544210944 | bytes 4855808 | tf_op jit(solution)/shard_map/dot_general | solution.py:94
  9.8 11.0 %all-to-all-start = ((bf16[64,16,2048]{2,1,0:T(8,128)(2,1)}), bf16[64,16,2048]{2,1,0:T(8,128)(2,1)}, u32[]{:S(2)}, u32[]{:S(2)}) async-start(bf16[64,16,2048]{2,1,0:T(8,128)(2,1)} %bitcast.84), calls=%async_computation | async-start | bytes 8388608 | tf_op jit(solution)/shard_map/all_to_all | solution.py:98
  20.8 0.1 copy.57
  21.0 10.9 %collective-permute-start = (bf16[128,1152]{1,0:T(8,128)(2,1)S(1)}, bf16[128,1152]{1,0:T(8,128)(2,1)S(1)}, u32[]{:S(2)}, u32[]{:S(2)}) collective-permute-start(bf16[128,1152]{1,0:T(8,128)(2,1)S(1)} %pad_maximum_fusion.5), channel_id=1, source_target_pairs={{0,448},{64,0},{128,64},{192,128},{256,192},{320,256},{384,320},{4... | collective-permute-start | bytes 884744 | tf_op jit(solution)/shard_map/ppermute | solution.py:47
  31.8 2.5 %collective-permute-start.1 = (bf16[128,1152]{1,0:T(8,128)(2,1)S(1)}, bf16[128,1152]{1,0:T(8,128)(2,1)S(1)}, u32[]{:S(2)}, u32[]{:S(2)}) collective-permute-start(bf16[128,1152]{1,0:T(8,128)(2,1)S(1)} %pad_maximum_fusion.5), channel_id=1, source_target_pairs={{0,384},{64,448},{128,0},{192,64},{256,128},{320,192},{384,256},{4... | collective-permute-start | bytes 884744 | tf_op jit(solution)/shard_map/ppermute | solution.py:47
  34.3 1.9 collective-permute-start.2
  36.2 7.8 %collective-permute-start.3 = (bf16[128,1152]{1,0:T(8,128)(2,1)S(1)}, bf16[128,1152]{1,0:T(8,128)(2,1)S(1)}, u32[]{:S(2)}, u32[]{:S(2)}) collective-permute-start(bf16[128,1152]{1,0:T(8,128)(2,1)S(1)} %pad_maximum_fusion.5), channel_id=1, source_target_pairs={{0,256},{64,320},{128,384},{192,448},{256,0},{320,64},{384,128},{4... | collective-permute-start | bytes 884744 | tf_op jit(solution)/shard_map/ppermute | solution.py:47
  44.1 1.9 collective-permute-start.4
  46.0 3.4 %collective-permute-start.5 = (bf16[128,1152]{1,0:T(8,128)(2,1)S(1)}, bf16[128,1152]{1,0:T(8,128)(2,1)S(1)}, u32[]{:S(2)}, u32[]{:S(2)}) collective-permute-start(bf16[128,1152]{1,0:T(8,128)(2,1)S(1)} %pad_maximum_fusion.5), channel_id=1, source_target_pairs={{0,128},{64,192},{128,256},{192,320},{256,384},{320,448},{384,0},{... | collective-permute-start | bytes 884744 | tf_op jit(solution)/shard_map/ppermute | solution.py:47
  49.4 5.6 %collective-permute-done.1 = bf16[128,1152]{1,0:T(8,128)(2,1)S(1)} collective-permute-done((bf16[128,1152]{1,0:T(8,128)(2,1)S(1)}, bf16[128,1152]{1,0:T(8,128)(2,1)S(1)}, u32[]{:S(2)}, u32[]{:S(2)}) %collective-permute-start.1) | collective-permute-done | bytes 294944 | tf_op jit(solution)/shard_map/ppermute | solution.py:47
  55.1 1.9 collective-permute-start.6
  57.0 25.6 %collective-permute-done.2 = bf16[128,1152]{1,0:T(8,128)(2,1)S(1)} collective-permute-done((bf16[128,1152]{1,0:T(8,128)(2,1)S(1)}, bf16[128,1152]{1,0:T(8,128)(2,1)S(1)}, u32[]{:S(2)}, u32[]{:S(2)}) %collective-permute-start.2) | collective-permute-done | bytes 294944 | tf_op jit(solution)/shard_map/ppermute | solution.py:47
  82.6 0.0 collective-permute-done.3
  82.7 0.7 collective-permute-done.4
  83.4 4.6 %collective-permute-done.5 = bf16[128,1152]{1,0:T(8,128)(2,1)S(1)} collective-permute-done((bf16[128,1152]{1,0:T(8,128)(2,1)S(1)}, bf16[128,1152]{1,0:T(8,128)(2,1)S(1)}, u32[]{:S(2)}, u32[]{:S(2)}) %collective-permute-start.5) | collective-permute-done | bytes 294944 | tf_op jit(solution)/shard_map/ppermute | solution.py:47
  88.0 7.0 %collective-permute-done.6 = bf16[128,1152]{1,0:T(8,128)(2,1)S(1)} collective-permute-done((bf16[128,1152]{1,0:T(8,128)(2,1)S(1)}, bf16[128,1152]{1,0:T(8,128)(2,1)S(1)}, u32[]{:S(2)}, u32[]{:S(2)}) %collective-permute-start.6) | collective-permute-done | bytes 294944 | tf_op jit(solution)/shard_map/ppermute | solution.py:47
  95.4 0.2 constant_dynamic-slice_fusion
  95.6 21.4 %all-to-all-done = bf16[64,16,2048]{2,1,0:T(8,128)(2,1)} async-done(((bf16[64,16,2048]{2,1,0:T(8,128)(2,1)}), bf16[64,16,2048]{2,1,0:T(8,128)(2,1)}, u32[]{:S(2)}, u32[]{:S(2)}) %all-to-all-start) | async-done | bytes 4194336 | tf_op jit(solution)/shard_map/all_to_all | solution.py:98
  117.0 3.4 %fusion.9 = f32[1024,768]{1,0:T(8,128)S(1)} fusion(bf16[1024,2048]{1,0:T(8,128)(2,1)} %bitcast.2, bf16[1024,1152]{1,0:T(8,128)(2,1)S(1)} %bitcast.85), kind=kOutput, calls=%fused_computation.18 | convolution fusion | flops 1610612736 | bytes 6815744 | tf_op jit(solution)/shard_map/dot_general | solution.py:16
  120.4 3.5 %multiply_convert_fusion.2 = (bf16[1024,384]{1,0:T(8,128)(2,1)S(1)}, bf16[1024,384]{1,0:T(8,128)(2,1)S(1)}, bf16[1024,384]{1,0:T(8,128)(2,1)S(1)}) fusion(f32[1024,768]{1,0:T(8,128)S(1)} %fusion.9, bf16[1024,1152]{1,0:T(8,128)(2,1)S(1)} %bitcast.86, bf16[1024,2048]{1,0:T(8,128)(2,1)} %bitcast.2), kind=kOutput, calls=%fused_computation.23 | convolution fusion | flops 811204608 | bytes 8388608 | tf_op jit(solution)/shard_map/dot_general | solution.py:24
  123.9 1.3 convolution_convert_fusion
  125.2 0.1 copy-done.11
  125.3 1.8 convolution_convert_fusion.1
  127.1 2.4 pad_maximum_fusion
  129.5 5.8 %all-to-all-start.1 = ((bf16[64,16,2048]{2,1,0:T(8,128)(2,1)}), bf16[64,16,2048]{2,1,0:T(8,128)(2,1)}, u32[]{:S(2)}, u32[]{:S(2)}) async-start(bf16[64,16,2048]{2,1,0:T(8,128)(2,1)} %bitcast.81), calls=%async_computation.1 | async-start | bytes 8388608 | tf_op jit(solution)/shard_map/all_to_all | solution.py:104
  135.5 2.7 %fusion.15 = bf16[1024,384]{0,1:T(8,128)(2,1)S(1)} fusion(bf16[1024,384]{1,0:T(8,128)(2,1)S(1)} %copy-done.8, bf16[1024,2048]{1,0:T(8,128)(2,1)} %bitcast.2), kind=kOutput, calls=%fused_computation.27 | convolution fusion | flops 805699584 | bytes 3670016 | tf_op jit(solution)/shard_map/dot_general | solution.py:35
  138.2 3.5 %fusion.11 = bf16[1024,768]{0,1:T(8,128)(2,1)S(1)} fusion(bf16[1024,2048]{1,0:T(8,128)(2,1)} %bitcast.2, bf16[1024,384]{1,0:T(8,128)(2,1)S(1)} %copy-done.12, bf16[1024,384]{1,0:T(8,128)(2,1)S(1)} %copy-done.10), kind=kOutput, calls=%fused_computation.20 | convolution fusion | flops 1614544896 | bytes 5242880 | tf_op jit(solution)/shard_map/dot_general | solution.py:32
  141.7 1.7 pad_maximum_fusion.1
  143.4 3.0 %copy.70 = bf16[1024,1152]{1,0:T(8,128)(2,1)S(1)} copy(bf16[1024,1152]{0,1:T(8,128)(2,1)} %pad_maximum_fusion.1) | data formatting | bytes 4718592 | tf_op jit(solution)/shard_map/reshape | solution.py:58
  146.4 1.1 dynamic-slice_bitcast_fusion.6
  147.5 10.7 %collective-permute-start.10 = (bf16[128,1152]{1,0:T(8,128)(2,1)S(1)}, bf16[128,1152]{1,0:T(8,128)(2,1)S(1)}, u32[]{:S(2)}, u32[]{:S(2)}) collective-permute-start(bf16[128,1152]{1,0:T(8,128)(2,1)S(1)} %get-tuple-element.29), channel_id=1, source_target_pairs={{0,256},{64,320},{128,384},{192,448},{256,0},{320,64},{384,128},{4... | collective-permute-start | bytes 884744 | tf_op jit(solution)/shard_map/ppermute | solution.py:63
  158.3 1.9 collective-permute-start.11
  160.2 7.8 %collective-permute-start.12 = (bf16[128,1152]{1,0:T(8,128)(2,1)}, bf16[128,1152]{1,0:T(8,128)(2,1)}, u32[]{:S(2)}, u32[]{:S(2)}) collective-permute-start(bf16[128,1152]{1,0:T(8,128)(2,1)} %get-tuple-element.27), channel_id=1, source_target_pairs={{0,384},{64,448},{128,0},{192,64},{256,128},{320,192},{384,256},{4... | collective-permute-start | bytes 884744 | tf_op jit(solution)/shard_map/ppermute | solution.py:63
  168.1 2.5 %collective-permute-start.13 = (bf16[128,1152]{1,0:T(8,128)(2,1)}, bf16[128,1152]{1,0:T(8,128)(2,1)}, u32[]{:S(2)}, u32[]{:S(2)}) collective-permute-start(bf16[128,1152]{1,0:T(8,128)(2,1)} %get-tuple-element.26), channel_id=1, source_target_pairs={{0,448},{64,0},{128,64},{192,128},{256,192},{320,256},{384,320},{4... | collective-permute-start | bytes 884744 | tf_op jit(solution)/shard_map/ppermute | solution.py:63
  170.5 3.4 %collective-permute-start.7 = (bf16[128,1152]{1,0:T(8,128)(2,1)}, bf16[128,1152]{1,0:T(8,128)(2,1)}, u32[]{:S(2)}, u32[]{:S(2)}) collective-permute-start(bf16[128,1152]{1,0:T(8,128)(2,1)} %get-tuple-element.25), channel_id=1, source_target_pairs={{0,64},{64,128},{128,192},{192,256},{256,320},{320,384},{384,448},... | collective-permute-start | bytes 884744 | tf_op jit(solution)/shard_map/ppermute | solution.py:63
  173.9 2.3 collective-permute-start.8
  176.2 16.8 %collective-permute-done.11 = bf16[128,1152]{1,0:T(8,128)(2,1)S(1)} collective-permute-done((bf16[128,1152]{1,0:T(8,128)(2,1)S(1)}, bf16[128,1152]{1,0:T(8,128)(2,1)S(1)}, u32[]{:S(2)}, u32[]{:S(2)}) %collective-permute-start.11) | collective-permute-done | bytes 294944 | tf_op jit(solution)/shard_map/ppermute | solution.py:63
  193.0 0.7 copy-done.2
  193.7 7.1 %collective-permute-start.9 = (bf16[128,1152]{1,0:T(8,128)(2,1)S(1)}, bf16[128,1152]{1,0:T(8,128)(2,1)}, u32[]{:S(2)}, u32[]{:S(2)}) collective-permute-start(bf16[128,1152]{1,0:T(8,128)(2,1)S(1)} %get-tuple-element.30), channel_id=1, source_target_pairs={{0,192},{64,256},{128,320},{192,384},{256,448},{320,0},{384,64},{4... | collective-permute-start | bytes 884744 | tf_op jit(solution)/shard_map/ppermute | solution.py:63
  200.9 0.8 convert_element_type.74
  201.6 1.0 reduce-precision_convert_fusion.1
  202.6 1.7 collective-permute-done.12
  204.3 6.9 %collective-permute-done.13 = bf16[128,1152]{1,0:T(8,128)(2,1)} collective-permute-done((bf16[128,1152]{1,0:T(8,128)(2,1)}, bf16[128,1152]{1,0:T(8,128)(2,1)}, u32[]{:S(2)}, u32[]{:S(2)}) %collective-permute-start.13) | collective-permute-done | bytes 294944 | tf_op jit(solution)/shard_map/ppermute | solution.py:63
  211.2 8.5 %collective-permute-done.9 = bf16[128,1152]{1,0:T(8,128)(2,1)} collective-permute-done((bf16[128,1152]{1,0:T(8,128)(2,1)S(1)}, bf16[128,1152]{1,0:T(8,128)(2,1)}, u32[]{:S(2)}, u32[]{:S(2)}) %collective-permute-start.9) | collective-permute-done | bytes 294944 | tf_op jit(solution)/shard_map/ppermute | solution.py:63
  219.6 1.8 fusion.35
  221.5 0.8 copy.68
  222.3 0.8 slice_bitcast_fusion
  223.1 8.5 %all-to-all-done.1 = bf16[64,16,2048]{2,1,0:T(8,128)(2,1)} async-done(((bf16[64,16,2048]{2,1,0:T(8,128)(2,1)}), bf16[64,16,2048]{2,1,0:T(8,128)(2,1)}, u32[]{:S(2)}, u32[]{:S(2)}) %all-to-all-start.1) | async-done | bytes 4194336 | tf_op jit(solution)/shard_map/all_to_all | solution.py:104
  231.6 4.8 %fusion.20 = f32[512,2048]{1,0:T(8,128)S(1)} fusion(bf16[1024,2048]{1,0:T(8,128)(2,1)} %bitcast.16, bf16[1024,128]{1,0:T(8,128)(2,1)} %convert_element_type.74, bf16[1024,128]{1,0:T(8,128)(2,1)S(1)} %copy-done.4, bf16[1024,128]{1,0:T(8,128)(2,1)} %get-tuple-element.34, bf16[1024,128]{1,0:T(8,128)(2,1)S(1)} %copy-done.3), kind=kOutput, calls=%fused_computation.30 | convolution fusion | flops 2151677952 | bytes 9437184 | tf_op jit(solution)/shard_map/dot_general | solution.py:121
  236.4 0.8 fusion.37
  237.2 0.7 slice.116
  237.9 2.3 fusion
  240.2 0.8 select_reduce_fusion.2
  (50 shorter events, 0.6 us)
Async XLA Ops:
  9.8 11.0 %copy-start.5 = (bf16[1,384,128]{2,1,0:T(8,128)(2,1)S(1)}, bf16[1,384,128]{2,1,0:T(8,128)(2,1)}, u32[]{:S(2)}) copy-start(bf16[1,384,128]{2,1,0:T(8,128)(2,1)} %param.10) | copy-start | bytes 294916
  9.8 11.2 %copy-start = (bf16[1,128,768]{2,1,0:T(8,128)(2,1)S(1)}, bf16[1,128,768]{2,1,0:T(8,128)(2,1)}, u32[]{:S(2)}) copy-start(bf16[1,128,768]{2,1,0:T(8,128)(2,1)} %param.9) | copy-start | bytes 589828
  9.8 107.2 %all-to-all-start = ((bf16[64,16,2048]{2,1,0:T(8,128)(2,1)}), bf16[64,16,2048]{2,1,0:T(8,128)(2,1)}, u32[]{:S(2)}, u32[]{:S(2)}) async-start(bf16[64,16,2048]{2,1,0:T(8,128)(2,1)} %bitcast.84), calls=%async_computation | async-start | bytes 8388608 | tf_op jit(solution)/shard_map/all_to_all | solution.py:98
  21.0 25.0 %collective-permute-start = (bf16[128,1152]{1,0:T(8,128)(2,1)S(1)}, bf16[128,1152]{1,0:T(8,128)(2,1)S(1)}, u32[]{:S(2)}, u32[]{:S(2)}) collective-permute-start(bf16[128,1152]{1,0:T(8,128)(2,1)S(1)} %pad_maximum_fusion.5), channel_id=1, source_target_pairs={{0,448},{64,0},{128,64},{192,128},{256,192},{320,256},{384,320},{4... | collective-permute-start | bytes 884744 | tf_op jit(solution)/shard_map/ppermute | solution.py:47
  31.8 23.2 %collective-permute-start.1 = (bf16[128,1152]{1,0:T(8,128)(2,1)S(1)}, bf16[128,1152]{1,0:T(8,128)(2,1)S(1)}, u32[]{:S(2)}, u32[]{:S(2)}) collective-permute-start(bf16[128,1152]{1,0:T(8,128)(2,1)S(1)} %pad_maximum_fusion.5), channel_id=1, source_target_pairs={{0,384},{64,448},{128,0},{192,64},{256,128},{320,192},{384,256},{4... | collective-permute-start | bytes 884744 | tf_op jit(solution)/shard_map/ppermute | solution.py:47
  34.3 48.3 %collective-permute-start.2 = (bf16[128,1152]{1,0:T(8,128)(2,1)S(1)}, bf16[128,1152]{1,0:T(8,128)(2,1)S(1)}, u32[]{:S(2)}, u32[]{:S(2)}) collective-permute-start(bf16[128,1152]{1,0:T(8,128)(2,1)S(1)} %pad_maximum_fusion.5), channel_id=1, source_target_pairs={{0,320},{64,384},{128,448},{192,0},{256,64},{320,128},{384,192},{4... | collective-permute-start | bytes 884744 | tf_op jit(solution)/shard_map/ppermute | solution.py:47
  36.2 46.4 %collective-permute-start.3 = (bf16[128,1152]{1,0:T(8,128)(2,1)S(1)}, bf16[128,1152]{1,0:T(8,128)(2,1)S(1)}, u32[]{:S(2)}, u32[]{:S(2)}) collective-permute-start(bf16[128,1152]{1,0:T(8,128)(2,1)S(1)} %pad_maximum_fusion.5), channel_id=1, source_target_pairs={{0,256},{64,320},{128,384},{192,448},{256,0},{320,64},{384,128},{4... | collective-permute-start | bytes 884744 | tf_op jit(solution)/shard_map/ppermute | solution.py:47
  44.1 39.3 %collective-permute-start.4 = (bf16[128,1152]{1,0:T(8,128)(2,1)S(1)}, bf16[128,1152]{1,0:T(8,128)(2,1)S(1)}, u32[]{:S(2)}, u32[]{:S(2)}) collective-permute-start(bf16[128,1152]{1,0:T(8,128)(2,1)S(1)} %pad_maximum_fusion.5), channel_id=1, source_target_pairs={{0,192},{64,256},{128,320},{192,384},{256,448},{320,0},{384,64},{4... | collective-permute-start | bytes 884744 | tf_op jit(solution)/shard_map/ppermute | solution.py:47
  46.0 42.0 %collective-permute-start.5 = (bf16[128,1152]{1,0:T(8,128)(2,1)S(1)}, bf16[128,1152]{1,0:T(8,128)(2,1)S(1)}, u32[]{:S(2)}, u32[]{:S(2)}) collective-permute-start(bf16[128,1152]{1,0:T(8,128)(2,1)S(1)} %pad_maximum_fusion.5), channel_id=1, source_target_pairs={{0,128},{64,192},{128,256},{192,320},{256,384},{320,448},{384,0},{... | collective-permute-start | bytes 884744 | tf_op jit(solution)/shard_map/ppermute | solution.py:47
  55.1 40.0 %collective-permute-start.6 = (bf16[128,1152]{1,0:T(8,128)(2,1)S(1)}, bf16[128,1152]{1,0:T(8,128)(2,1)S(1)}, u32[]{:S(2)}, u32[]{:S(2)}) collective-permute-start(bf16[128,1152]{1,0:T(8,128)(2,1)S(1)} %pad_maximum_fusion.5), channel_id=1, source_target_pairs={{0,64},{64,128},{128,192},{192,256},{256,320},{320,384},{384,448},... | collective-permute-start | bytes 884744 | tf_op jit(solution)/shard_map/ppermute | solution.py:47
  123.9 1.3 copy-start.7
  123.9 1.3 copy-start.9
  123.9 1.4 copy-start.11
  129.5 6.0 %copy-start.8 = (bf16[1024,384]{1,0:T(8,128)(2,1)S(1)}, bf16[1024,384]{1,0:T(8,128)(2,1)}, u32[]{:S(2)}) copy-start(bf16[1024,384]{1,0:T(8,128)(2,1)} %copy-done.7) | copy-start | bytes 2359300
  129.5 102.0 %all-to-all-start.1 = ((bf16[64,16,2048]{2,1,0:T(8,128)(2,1)}), bf16[64,16,2048]{2,1,0:T(8,128)(2,1)}, u32[]{:S(2)}, u32[]{:S(2)}) async-start(bf16[64,16,2048]{2,1,0:T(8,128)(2,1)} %bitcast.81), calls=%async_computation.1 | async-start | bytes 8388608 | tf_op jit(solution)/shard_map/all_to_all | solution.py:104
  135.5 2.8 %copy-start.10 = (bf16[1024,384]{1,0:T(8,128)(2,1)S(1)}, bf16[1024,384]{1,0:T(8,128)(2,1)}, u32[]{:S(2)}) copy-start(bf16[1024,384]{1,0:T(8,128)(2,1)} %copy-done.9) | copy-start | bytes 2359300
  135.5 2.8 %copy-start.12 = (bf16[1024,384]{1,0:T(8,128)(2,1)S(1)}, bf16[1024,384]{1,0:T(8,128)(2,1)}, u32[]{:S(2)}) copy-start(bf16[1024,384]{1,0:T(8,128)(2,1)} %copy-done.11) | copy-start | bytes 2359300
  147.5 26.4 %collective-permute-start.10 = (bf16[128,1152]{1,0:T(8,128)(2,1)S(1)}, bf16[128,1152]{1,0:T(8,128)(2,1)S(1)}, u32[]{:S(2)}, u32[]{:S(2)}) collective-permute-start(bf16[128,1152]{1,0:T(8,128)(2,1)S(1)} %get-tuple-element.29), channel_id=1, source_target_pairs={{0,256},{64,320},{128,384},{192,448},{256,0},{320,64},{384,128},{4... | collective-permute-start | bytes 884744 | tf_op jit(solution)/shard_map/ppermute | solution.py:63
  158.3 34.8 %collective-permute-start.11 = (bf16[128,1152]{1,0:T(8,128)(2,1)S(1)}, bf16[128,1152]{1,0:T(8,128)(2,1)S(1)}, u32[]{:S(2)}, u32[]{:S(2)}) collective-permute-start(bf16[128,1152]{1,0:T(8,128)(2,1)S(1)} %get-tuple-element.28), channel_id=1, source_target_pairs={{0,320},{64,384},{128,448},{192,0},{256,64},{320,128},{384,192},{4... | collective-permute-start | bytes 884744 | tf_op jit(solution)/shard_map/ppermute | solution.py:63
  160.2 44.1 %collective-permute-start.12 = (bf16[128,1152]{1,0:T(8,128)(2,1)}, bf16[128,1152]{1,0:T(8,128)(2,1)}, u32[]{:S(2)}, u32[]{:S(2)}) collective-permute-start(bf16[128,1152]{1,0:T(8,128)(2,1)} %get-tuple-element.27), channel_id=1, source_target_pairs={{0,384},{64,448},{128,0},{192,64},{256,128},{320,192},{384,256},{4... | collective-permute-start | bytes 884744 | tf_op jit(solution)/shard_map/ppermute | solution.py:63
  168.1 43.1 %collective-permute-start.13 = (bf16[128,1152]{1,0:T(8,128)(2,1)}, bf16[128,1152]{1,0:T(8,128)(2,1)}, u32[]{:S(2)}, u32[]{:S(2)}) collective-permute-start(bf16[128,1152]{1,0:T(8,128)(2,1)} %get-tuple-element.26), channel_id=1, source_target_pairs={{0,448},{64,0},{128,64},{192,128},{256,192},{320,256},{384,320},{4... | collective-permute-start | bytes 884744 | tf_op jit(solution)/shard_map/ppermute | solution.py:63
  170.5 40.6 %collective-permute-start.7 = (bf16[128,1152]{1,0:T(8,128)(2,1)}, bf16[128,1152]{1,0:T(8,128)(2,1)}, u32[]{:S(2)}, u32[]{:S(2)}) collective-permute-start(bf16[128,1152]{1,0:T(8,128)(2,1)} %get-tuple-element.25), channel_id=1, source_target_pairs={{0,64},{64,128},{128,192},{192,256},{256,320},{320,384},{384,448},... | collective-permute-start | bytes 884744 | tf_op jit(solution)/shard_map/ppermute | solution.py:63
  173.9 19.1 %copy-start.1 = (bf16[128,1152]{1,0:T(8,128)(2,1)}, bf16[128,1152]{1,0:T(8,128)(2,1)S(1)}, u32[]{:S(2)}) copy-start(bf16[128,1152]{1,0:T(8,128)(2,1)S(1)} %collective-permute-done.10) | copy-start | bytes 884740
  173.9 37.2 %collective-permute-start.8 = (bf16[128,1152]{1,0:T(8,128)(2,1)}, bf16[128,1152]{1,0:T(8,128)(2,1)}, u32[]{:S(2)}, u32[]{:S(2)}) collective-permute-start(bf16[128,1152]{1,0:T(8,128)(2,1)} %get-tuple-element.31), channel_id=1, source_target_pairs={{0,128},{64,192},{128,256},{192,320},{256,384},{320,448},{384,0},{... | collective-permute-start | bytes 884744 | tf_op jit(solution)/shard_map/ppermute | solution.py:63
  193.0 0.7 copy-start.2
  193.7 25.9 %collective-permute-start.9 = (bf16[128,1152]{1,0:T(8,128)(2,1)S(1)}, bf16[128,1152]{1,0:T(8,128)(2,1)}, u32[]{:S(2)}, u32[]{:S(2)}) collective-permute-start(bf16[128,1152]{1,0:T(8,128)(2,1)S(1)} %get-tuple-element.30), channel_id=1, source_target_pairs={{0,192},{64,256},{128,320},{192,384},{256,448},{320,0},{384,64},{4... | collective-permute-start | bytes 884744 | tf_op jit(solution)/shard_map/ppermute | solution.py:63
  219.6 11.9 %copy-start.3 = (bf16[1024,128]{1,0:T(8,128)(2,1)S(1)}, bf16[1024,128]{1,0:T(8,128)(2,1)}, u32[]{:S(2)}) copy-start(bf16[1024,128]{1,0:T(8,128)(2,1)} %get-tuple-element.32) | copy-start | bytes 786436
  219.6 11.9 %copy-start.4 = (bf16[1024,128]{1,0:T(8,128)(2,1)S(1)}, bf16[1024,128]{1,0:T(8,128)(2,1)}, u32[]{:S(2)}) copy-start(bf16[1024,128]{1,0:T(8,128)(2,1)} %get-tuple-element.33) | copy-start | bytes 786436
  231.6 6.4 %copy-start.6 = (bf16[128,1024]{1,0:T(8,128)(2,1)S(1)}, bf16[128,1024]{1,0:T(8,128)(2,1)}, u32[]{:S(2)}) copy-start(bf16[128,1024]{1,0:T(8,128)(2,1)} %param.11) | copy-start | bytes 786436

commit v6 on v5

--- a/solution.py
+++ b/solution.py
@@ -1,41 +1,63 @@
+import functools
+
 import jax
 import jax.numpy as jnp
 from jax import lax
-from jax.experimental.layout import Layout, with_layout_constraint
+from jax.experimental import pallas as pl
 from jax.sharding import PartitionSpec as P
 
 
-def row_major(x):
-    return with_layout_constraint(x, Layout(major_to_minor=tuple(range(x.ndim))))
+def expert_kernel(recv_ref, w_ref, out_ref, hid_ref, dp_ref, *, width, gate_width, hidden_width):
+    contract_last = (((1,), (1,)), ((), ()))
+    rows = recv_ref[:, :width]
+    grads = recv_ref[:, width:]
+    w_in = w_ref[:, :gate_width]
+    w_out_t = w_ref[:, gate_width:]
+    pre = jnp.dot(rows, w_in, preferred_element_type=jnp.float32)
+    pre_gate = pre[:, :hidden_width]
+    up = pre[:, hidden_width:]
+    sig = 1.0 / (1.0 + jnp.exp(-pre_gate))
+    act = pre_gate * sig
+    hid = (act * up).astype(jnp.bfloat16)
+    q = jnp.dot(grads, w_out_t, preferred_element_type=jnp.float32)
+    grad_gate = q * up * sig * (1.0 + pre_gate * (1.0 - sig))
+    grad_up = q * act
+    dp = jnp.concatenate([grad_gate, grad_up], axis=1).astype(jnp.bfloat16)
+    out_ref[:, :width] = lax.dot_general(
+        hid, w_out_t, contract_last, preferred_element_type=jnp.float32
+    ).astype(jnp.bfloat16)
+    out_ref[:, width:] = lax.dot_general(
+        dp, w_in, contract_last, preferred_element_type=jnp.float32
+    ).astype(jnp.bfloat16)
+    hid_ref[...] = hid
+    dp_ref[...] = dp
 
 
-def expert_rows(rows_in, grad_rows, weight_in, weight_out_t):
-    hidden_width = weight_out_t.shape[1]
-    contract_last = (((1,), (1,)), ((), ()))
-    contract_first = (((0,), (0,)), ((), ()))
-    pre_act = row_major(jnp.dot(rows_in, weight_in, preferred_element_type=jnp.float32))
-    pre_gate = pre_act[:, :hidden_width]
-    up_value = pre_act[:, hidden_width:]
-    act = jax.nn.silu(pre_gate)
-    hidden = (act * up_value).astype(jnp.bfloat16)
-    expert_out = lax.dot_general(
-        hidden, weight_out_t, contract_last, preferred_element_type=jnp.float32
-    ).astype(jnp.bfloat16)
-    grad_hidden = jnp.dot(grad_rows, weight_out_t, preferred_element_type=jnp.float32)
-    sigmoid_value = jax.nn.sigmoid(pre_gate)
-    grad_gate = grad_hidden * up_value * sigmoid_value * (1.0 + pre_gate * (1.0 - sigmoid_value))
-    grad_up = grad_hidden * act
-    grad_pre = jnp.concatenate([grad_gate, grad_up], axis=1).astype(jnp.bfloat16)
-    grad_in = lax.dot_general(
-        grad_pre, weight_in, contract_last, preferred_element_type=jnp.float32
-    ).astype(jnp.bfloat16)
-    weight_in_grad = lax.dot_general(
-        rows_in, grad_pre, contract_first, preferred_element_type=jnp.float32
-    ).astype(jnp.bfloat16)
-    weight_out_grad_t = lax.dot_general(
-        grad_rows, hidden, contract_first, preferred_element_type=jnp.float32
-    ).astype(jnp.bfloat16)
-    return expert_out, grad_in, weight_in_grad, weight_out_grad_t
+def expert_call(recv, weights, gate_width, block=256):
+    slots, both = recv.shape
+    width = both // 2
+    hidden_width = weights.shape[1] - gate_width
+    kernel = functools.partial(
+        expert_kernel, width=width, gate_width=gate_width, hidden_width=hidden_width
+    )
+    return pl.pallas_call(
+        kernel,
+        grid=(slots // block,),
+        in_specs=[
+            pl.BlockSpec((block, both), lambda i: (i, 0)),
+            pl.BlockSpec(weights.shape, lambda i: (0, 0)),
+        ],
+        out_specs=[
+            pl.BlockSpec((block, both), lambda i: (i, 0)),
+            pl.BlockSpec((block, hidden_width), lambda i: (i, 0)),
+            pl.BlockSpec((block, gate_width), lambda i: (i, 0)),
+        ],
+        out_shape=[
+            jax.ShapeDtypeStruct((slots, both), jnp.bfloat16),
+            jax.ShapeDtypeStruct((slots, hidden_width), jnp.bfloat16),
+            jax.ShapeDtypeStruct((slots, gate_width), jnp.bfloat16),
+        ],
+    )(recv, weights)
 
 
 def gather_dp(block):
@@ -74,8 +96,6 @@
     gate_width = gate_up.shape[2]
 
     weights = gather_dp(jnp.concatenate([gate_up[0], down_proj[0].T], axis=1))
-    weight_in = weights[:, :gate_width]
-    weight_out_t = weights[:, gate_width:]
 
     flat_ids = expert_ids.reshape(route_count)
     onehot = (flat_ids[:, None] == jnp.arange(expert_count, dtype=jnp.int32)[None, :]).astype(
@@ -96,18 +116,15 @@
     send = (gathered * jnp.where(column < width, 1.0, slot_probs[:, None])).astype(jnp.bfloat16)
 
     recv = lax.all_to_all(send, "expert", split_axis=0, concat_axis=0, tiled=True)
-    rows_in = recv[:, :width]
-    grad_rows = recv[:, width:]
-    expert_out, grad_in, weight_in_grad, weight_out_grad_t = expert_rows(
-        rows_in, grad_rows, weight_in, weight_out_t
-    )
-    back = lax.all_to_all(
-        jnp.concatenate([row_major(expert_out), row_major(grad_in)], axis=1),
-        "expert",
-        split_axis=0,
-        concat_axis=0,
-        tiled=True,
-    )
+    payload, hidden, grad_pre = expert_call(recv, weights, gate_width)
+    back = lax.all_to_all(payload, "expert", split_axis=0, concat_axis=0, tiled=True)
+    contract_first = (((0,), (0,)), ((), ()))
+    weight_in_grad = lax.dot_general(
+        recv[:, :width], grad_pre, contract_first, preferred_element_type=jnp.float32
+    ).astype(jnp.bfloat16)
+    weight_out_grad_t = lax.dot_general(
+        recv[:, width:], hidden, contract_first, preferred_element_type=jnp.float32
+    ).astype(jnp.bfloat16)
     grads = scatter_dp(jnp.concatenate([weight_in_grad, weight_out_grad_t], axis=1))
     sum_in = grads[None, :, :gate_width]
     sum_out = grads[:, gate_width:].T[None]

time: 242 us -> 239 us (0.988)
  matrix products: 27.5 us -> 17.6 us
  Pallas kernels: 0 us -> 9.47 us
    dot_general x6 -> x2, matrix products: 16.1 us -> 6.18 us  [the longest x1 3.46 us: local(): lax.dot_general(recv[:, :width], grad_pre, contract_first, preferred_elem...]
    pallas_call x0 -> x1, Pallas kernels: none -> 9.47 us  [expert_call(): pl.pallas_call(kernel, grid=(slots // block,), in_specs=[pl.BlockSpec((bl...]
  transfers between devices with their start and end apart: 16 -> 16, of which waited for: 11 -> 11; matrix products, arithmetic and copies ran while one was open for 7% -> 8% of each run, Pallas kernels for 0% -> 0%
where the time goes in v6:
time: 239 us; the launch traced here: 238 us
  waiting for transfers between devices  106 us (44%)
  starting transfers between devices  83.1 us (35%)
  matrix products  17.6 us (7%)
  local copies, waits for them, and re-layouts  10.8 us (5%)
  other arithmetic  10.4 us (4%)
  Pallas kernels  9.47 us (4%)
    ppermute x7, waiting for transfers between devices, gather_dp(): pieces.append(lax.ppermute(block, 'dp', pairs))  43.5 us
    ppermute x7, starting transfers between devices, scatter_dp(): total = total + lax.ppermute(part, 'dp', pairs).astype(jnp.float32)  36 us
    ppermute x7, waiting for transfers between devices, scatter_dp(): total = total + lax.ppermute(part, 'dp', pairs).astype(jnp.float32)  33.6 us
    ppermute x7, starting transfers between devices, gather_dp(): pieces.append(lax.ppermute(block, 'dp', pairs))  30.3 us
    all_to_all x1, waiting for transfers between devices, local(): lax.all_to_all(send, 'expert', split_axis=0, concat_axis=0, tiled=True)  20 us
    all_to_all x1, starting transfers between devices, local(): lax.all_to_all(send, 'expert', split_axis=0, concat_axis=0, tiled=True)  11 us
    pallas_call x1, Pallas kernels, expert_call(): pl.pallas_call(kernel, grid=(slots // block,), in_specs=[pl.BlockSpec((bl...  9.47 us
    all_to_all x1, waiting for transfers between devices, local(): lax.all_to_all(payload, 'expert', split_axis=0, concat_axis=0, tiled=True)  8.51 us
  transfers between devices with their start and end apart: 16, of which 11 were waited for; matrix products, arithmetic and copies ran while one was open for 8% of the time, Pallas kernels for 0%

profile of v6, /device:TPU:6, one launch (start us, length us, event | category | flops | bytes accessed | tf_op | source)
XLA Modules:
  0.0 238.1 jit_solution(10996551296930796865)
XLA Ops:
  0.6 0.8 copy.47
  1.4 0.1 eq.50
  1.5 0.1 eq.46
  1.7 1.2 reduce-window.6
  2.9 0.2 slice_reduce_fusion
  3.1 0.1 fusion.34
  3.3 0.1 reduce_sum.39
  3.4 0.1 copy.50
  3.5 0.7 multiply_add_fusion
  4.2 0.4 fusion.6
  4.5 1.0 select_reduce_fusion.1
  5.5 4.3 %multiply_convert_fusion = bf16[1024,2048]{1,0:T(8,128)(2,1)} fusion(pred[1024,128]{1,0:T(8,128)(4,1)S(1)} %fusion.6, f32[1024]{0:T(1024)S(1)} %get-tuple-element.27, pred[2048]{0:T(1024)(128)(4,1)S(1)} %iota_compare_fusion.3, bf16[128,1024]{1,0:T(8,128)(2,1)} %param.11, bf16[128,1024]{1,0:T(8,128)(2,1)} %param.6), kind=kOutput, calls=%fused_computation | convolution fusion | flops 544210944 | bytes 4855808 | tf_op jit(solution)/shard_map/dot_general | solution.py:114
  9.9 11.0 %all-to-all-start = ((bf16[64,16,2048]{2,1,0:T(8,128)(2,1)}), bf16[64,16,2048]{2,1,0:T(8,128)(2,1)}, u32[]{:S(2)}, u32[]{:S(2)}) async-start(bf16[64,16,2048]{2,1,0:T(8,128)(2,1)} %bitcast.85), calls=%async_computation | async-start | bytes 8388608 | tf_op jit(solution)/shard_map/all_to_all | solution.py:118
  20.9 0.0 copy-done.5
  20.9 0.1 copy.51
  21.0 10.9 %collective-permute-start = (bf16[128,1152]{1,0:T(8,128)(2,1)S(1)}, bf16[128,1152]{1,0:T(8,128)(2,1)S(1)}, u32[]{:S(2)}, u32[]{:S(2)}) collective-permute-start(bf16[128,1152]{1,0:T(8,128)(2,1)S(1)} %pad_maximum_fusion.1), channel_id=1, source_target_pairs={{0,448},{64,0},{128,64},{192,128},{256,192},{320,256},{384,320},{4... | collective-permute-start | bytes 884744 | tf_op jit(solution)/shard_map/ppermute | solution.py:69
  31.9 2.5 %collective-permute-start.1 = (bf16[128,1152]{1,0:T(8,128)(2,1)S(1)}, bf16[128,1152]{1,0:T(8,128)(2,1)S(1)}, u32[]{:S(2)}, u32[]{:S(2)}) collective-permute-start(bf16[128,1152]{1,0:T(8,128)(2,1)S(1)} %pad_maximum_fusion.1), channel_id=1, source_target_pairs={{0,384},{64,448},{128,0},{192,64},{256,128},{320,192},{384,256},{4... | collective-permute-start | bytes 884744 | tf_op jit(solution)/shard_map/ppermute | solution.py:69
  34.4 1.9 collective-permute-start.2
  36.3 7.8 %collective-permute-start.3 = (bf16[128,1152]{1,0:T(8,128)(2,1)S(1)}, bf16[128,1152]{1,0:T(8,128)(2,1)S(1)}, u32[]{:S(2)}, u32[]{:S(2)}) collective-permute-start(bf16[128,1152]{1,0:T(8,128)(2,1)S(1)} %pad_maximum_fusion.1), channel_id=1, source_target_pairs={{0,256},{64,320},{128,384},{192,448},{256,0},{320,64},{384,128},{4... | collective-permute-start | bytes 884744 | tf_op jit(solution)/shard_map/ppermute | solution.py:69
  44.1 1.9 collective-permute-start.4
  46.1 0.0 collective-permute-done
  46.1 3.4 %collective-permute-start.5 = (bf16[128,1152]{1,0:T(8,128)(2,1)S(1)}, bf16[128,1152]{1,0:T(8,128)(2,1)S(1)}, u32[]{:S(2)}, u32[]{:S(2)}) collective-permute-start(bf16[128,1152]{1,0:T(8,128)(2,1)S(1)} %pad_maximum_fusion.1), channel_id=1, source_target_pairs={{0,128},{64,192},{128,256},{192,320},{256,384},{320,448},{384,0},{... | collective-permute-start | bytes 884744 | tf_op jit(solution)/shard_map/ppermute | solution.py:69
  49.5 5.6 %collective-permute-done.1 = bf16[128,1152]{1,0:T(8,128)(2,1)S(1)} collective-permute-done((bf16[128,1152]{1,0:T(8,128)(2,1)S(1)}, bf16[128,1152]{1,0:T(8,128)(2,1)S(1)}, u32[]{:S(2)}, u32[]{:S(2)}) %collective-permute-start.1) | collective-permute-done | bytes 294944 | tf_op jit(solution)/shard_map/ppermute | solution.py:69
  55.1 1.9 collective-permute-start.6
  57.1 25.6 %collective-permute-done.2 = bf16[128,1152]{1,0:T(8,128)(2,1)S(1)} collective-permute-done((bf16[128,1152]{1,0:T(8,128)(2,1)S(1)}, bf16[128,1152]{1,0:T(8,128)(2,1)S(1)}, u32[]{:S(2)}, u32[]{:S(2)}) %collective-permute-start.2) | collective-permute-done | bytes 294944 | tf_op jit(solution)/shard_map/ppermute | solution.py:69
  82.7 0.0 collective-permute-done.3
  82.8 0.7 collective-permute-done.4
  83.5 4.6 %collective-permute-done.5 = bf16[128,1152]{1,0:T(8,128)(2,1)S(1)} collective-permute-done((bf16[128,1152]{1,0:T(8,128)(2,1)S(1)}, bf16[128,1152]{1,0:T(8,128)(2,1)S(1)}, u32[]{:S(2)}, u32[]{:S(2)}) %collective-permute-start.5) | collective-permute-done | bytes 294944 | tf_op jit(solution)/shard_map/ppermute | solution.py:69
  88.1 7.0 %collective-permute-done.6 = bf16[128,1152]{1,0:T(8,128)(2,1)S(1)} collective-permute-done((bf16[128,1152]{1,0:T(8,128)(2,1)S(1)}, bf16[128,1152]{1,0:T(8,128)(2,1)S(1)}, u32[]{:S(2)}, u32[]{:S(2)}) %collective-permute-start.6) | collective-permute-done | bytes 294944 | tf_op jit(solution)/shard_map/ppermute | solution.py:69
  95.5 1.6 constant_dynamic-slice_fusion
  97.1 20.0 %all-to-all-done = bf16[64,16,2048]{2,1,0:T(8,128)(2,1)} async-done(((bf16[64,16,2048]{2,1,0:T(8,128)(2,1)}), bf16[64,16,2048]{2,1,0:T(8,128)(2,1)}, u32[]{:S(2)}, u32[]{:S(2)}) %all-to-all-start) | async-done | bytes 4194336 | tf_op jit(solution)/shard_map/all_to_all | solution.py:118
  117.1 9.5 %shard_map.101 = (bf16[1024,2048]{1,0:T(8,128)(2,1)}, bf16[1024,384]{1,0:T(8,128)(2,1)}, bf16[1024,768]{1,0:T(8,128)(2,1)}) custom-call(bf16[1024,2048]{1,0:T(8,128)(2,1)} %bitcast.2.recv_ref, bf16[1024,1152]{1,0:T(8,128)(2,1)} %bitcast.81), custom_call_target="tpu_custom_call" | custom-call | tf_op jit(solution)/shard_map/pallas_call | solution.py:43
  126.5 5.8 %all-to-all-start.1 = ((bf16[64,16,2048]{2,1,0:T(8,128)(2,1)}), bf16[64,16,2048]{2,1,0:T(8,128)(2,1)}, u32[]{:S(2)}, u32[]{:S(2)}) async-start(bf16[64,16,2048]{2,1,0:T(8,128)(2,1)} %bitcast.84), calls=%async_computation.1 | async-start | bytes 8388608 | tf_op jit(solution)/shard_map/all_to_all | solution.py:120
  132.5 2.7 %fusion.10 = bf16[1024,384]{0,1:T(8,128)(2,1)S(1)} fusion(bf16[1024,384]{1,0:T(8,128)(2,1)S(1)} %copy-done.7, bf16[1024,2048]{1,0:T(8,128)(2,1)} %bitcast.2.recv_ref), kind=kOutput, calls=%fused_computation.14 | convolution fusion | flops 805699584 | bytes 3670016 | tf_op jit(solution)/shard_map/dot_general | solution.py:125
  135.2 3.5 %fusion.7 = bf16[1024,768]{0,1:T(8,128)(2,1)S(1)} fusion(bf16[1024,768]{1,0:T(8,128)(2,1)S(1)} %copy-done.6, bf16[1024,2048]{1,0:T(8,128)(2,1)} %bitcast.2.recv_ref), kind=kOutput, calls=%fused_computation.13 | convolution fusion | flops 1611399168 | bytes 5242880 | tf_op jit(solution)/shard_map/dot_general | solution.py:122
  138.7 1.7 pad_maximum_fusion
  140.4 3.0 %copy.61 = bf16[1024,1152]{1,0:T(8,128)(2,1)S(1)} copy(bf16[1024,1152]{0,1:T(8,128)(2,1)} %pad_maximum_fusion) | data formatting | bytes 4718592 | tf_op jit(solution)/shard_map/reshape | solution.py:80
  143.4 1.1 dynamic-slice_bitcast_fusion.6
  144.5 10.7 %collective-permute-start.10 = (bf16[128,1152]{1,0:T(8,128)(2,1)S(1)}, bf16[128,1152]{1,0:T(8,128)(2,1)S(1)}, u32[]{:S(2)}, u32[]{:S(2)}) collective-permute-start(bf16[128,1152]{1,0:T(8,128)(2,1)S(1)} %get-tuple-element.32), channel_id=1, source_target_pairs={{0,256},{64,320},{128,384},{192,448},{256,0},{320,64},{384,128},{4... | collective-permute-start | bytes 884744 | tf_op jit(solution)/shard_map/ppermute | solution.py:85
  155.2 1.9 collective-permute-start.11
  157.2 7.9 %collective-permute-start.12 = (bf16[128,1152]{1,0:T(8,128)(2,1)}, bf16[128,1152]{1,0:T(8,128)(2,1)}, u32[]{:S(2)}, u32[]{:S(2)}) collective-permute-start(bf16[128,1152]{1,0:T(8,128)(2,1)} %get-tuple-element.30), channel_id=1, source_target_pairs={{0,384},{64,448},{128,0},{192,64},{256,128},{320,192},{384,256},{4... | collective-permute-start | bytes 884744 | tf_op jit(solution)/shard_map/ppermute | solution.py:85
  165.1 2.5 %collective-permute-start.13 = (bf16[128,1152]{1,0:T(8,128)(2,1)}, bf16[128,1152]{1,0:T(8,128)(2,1)}, u32[]{:S(2)}, u32[]{:S(2)}) collective-permute-start(bf16[128,1152]{1,0:T(8,128)(2,1)} %get-tuple-element.29), channel_id=1, source_target_pairs={{0,448},{64,0},{128,64},{192,128},{256,192},{320,256},{384,320},{4... | collective-permute-start | bytes 884744 | tf_op jit(solution)/shard_map/ppermute | solution.py:85
  167.5 3.4 %collective-permute-start.7 = (bf16[128,1152]{1,0:T(8,128)(2,1)}, bf16[128,1152]{1,0:T(8,128)(2,1)}, u32[]{:S(2)}, u32[]{:S(2)}) collective-permute-start(bf16[128,1152]{1,0:T(8,128)(2,1)} %get-tuple-element.28), channel_id=1, source_target_pairs={{0,64},{64,128},{128,192},{192,256},{256,320},{320,384},{384,448},... | collective-permute-start | bytes 884744 | tf_op jit(solution)/shard_map/ppermute | solution.py:85
  170.9 0.0 collective-permute-done.10
  170.9 2.3 collective-permute-start.8
  173.2 16.8 %collective-permute-done.11 = bf16[128,1152]{1,0:T(8,128)(2,1)S(1)} collective-permute-done((bf16[128,1152]{1,0:T(8,128)(2,1)S(1)}, bf16[128,1152]{1,0:T(8,128)(2,1)S(1)}, u32[]{:S(2)}, u32[]{:S(2)}) %collective-permute-start.11) | collective-permute-done | bytes 294944 | tf_op jit(solution)/shard_map/ppermute | solution.py:85
  190.0 0.7 copy-done.2
  190.7 7.3 %collective-permute-start.9 = (bf16[128,1152]{1,0:T(8,128)(2,1)S(1)}, bf16[128,1152]{1,0:T(8,128)(2,1)}, u32[]{:S(2)}, u32[]{:S(2)}) collective-permute-start(bf16[128,1152]{1,0:T(8,128)(2,1)S(1)} %get-tuple-element.33), channel_id=1, source_target_pairs={{0,192},{64,256},{128,320},{192,384},{256,448},{320,0},{384,64},{4... | collective-permute-start | bytes 884744 | tf_op jit(solution)/shard_map/ppermute | solution.py:85
  198.0 0.8 convert_element_type.64
  198.8 1.0 reduce-precision_convert_fusion.1
  199.8 1.5 collective-permute-done.12
  201.3 6.9 %collective-permute-done.13 = bf16[128,1152]{1,0:T(8,128)(2,1)} collective-permute-done((bf16[128,1152]{1,0:T(8,128)(2,1)}, bf16[128,1152]{1,0:T(8,128)(2,1)}, u32[]{:S(2)}, u32[]{:S(2)}) %collective-permute-start.13) | collective-permute-done | bytes 294944 | tf_op jit(solution)/shard_map/ppermute | solution.py:85
  208.1 0.0 collective-permute-done.7
  208.1 0.0 collective-permute-done.8
  208.1 8.5 %collective-permute-done.9 = bf16[128,1152]{1,0:T(8,128)(2,1)} collective-permute-done((bf16[128,1152]{1,0:T(8,128)(2,1)S(1)}, bf16[128,1152]{1,0:T(8,128)(2,1)}, u32[]{:S(2)}, u32[]{:S(2)}) %collective-permute-start.9) | collective-permute-done | bytes 294944 | tf_op jit(solution)/shard_map/ppermute | solution.py:85
  216.6 1.8 fusion.26
  218.5 0.8 copy.60
  219.3 0.8 slice_bitcast_fusion
  220.1 8.5 %all-to-all-done.1 = bf16[64,16,2048]{2,1,0:T(8,128)(2,1)} async-done(((bf16[64,16,2048]{2,1,0:T(8,128)(2,1)}), bf16[64,16,2048]{2,1,0:T(8,128)(2,1)}, u32[]{:S(2)}, u32[]{:S(2)}) %all-to-all-start.1) | async-done | bytes 4194336 | tf_op jit(solution)/shard_map/all_to_all | solution.py:120
  228.6 4.8 %fusion.13 = f32[512,2048]{1,0:T(8,128)S(1)} fusion(bf16[1024,2048]{1,0:T(8,128)(2,1)} %bitcast.16, bf16[1024,128]{1,0:T(8,128)(2,1)} %convert_element_type.64, bf16[1024,128]{1,0:T(8,128)(2,1)S(1)} %copy-done.4, bf16[1024,128]{1,0:T(8,128)(2,1)} %get-tuple-element.37, bf16[1024,128]{1,0:T(8,128)(2,1)S(1)} %copy-done.3), kind=kOutput, calls=%fused_computation.15 | convolution fusion | flops 2151677952 | bytes 9437184 | tf_op jit(solution)/shard_map/dot_general | solution.py:138
  233.4 0.8 fusion.28
  234.2 0.7 slice.76
  235.0 2.3 fusion.4
  237.3 0.8 select_reduce_fusion.2
  (38 shorter events, 0.6 us)
Async XLA Ops:
  9.8 11.0 %copy-start.5 = (bf16[1,384,128]{2,1,0:T(8,128)(2,1)S(1)}, bf16[1,384,128]{2,1,0:T(8,128)(2,1)}, u32[]{:S(2)}) copy-start(bf16[1,384,128]{2,1,0:T(8,128)(2,1)} %param.10) | copy-start | bytes 294916
  9.9 11.2 %copy-start = (bf16[1,128,768]{2,1,0:T(8,128)(2,1)S(1)}, bf16[1,128,768]{2,1,0:T(8,128)(2,1)}, u32[]{:S(2)}) copy-start(bf16[1,128,768]{2,1,0:T(8,128)(2,1)} %param.9) | copy-start | bytes 589828
  9.9 107.2 %all-to-all-start = ((bf16[64,16,2048]{2,1,0:T(8,128)(2,1)}), bf16[64,16,2048]{2,1,0:T(8,128)(2,1)}, u32[]{:S(2)}, u32[]{:S(2)}) async-start(bf16[64,16,2048]{2,1,0:T(8,128)(2,1)} %bitcast.85), calls=%async_computation | async-start | bytes 8388608 | tf_op jit(solution)/shard_map/all_to_all | solution.py:118
  21.0 25.0 %collective-permute-start = (bf16[128,1152]{1,0:T(8,128)(2,1)S(1)}, bf16[128,1152]{1,0:T(8,128)(2,1)S(1)}, u32[]{:S(2)}, u32[]{:S(2)}) collective-permute-start(bf16[128,1152]{1,0:T(8,128)(2,1)S(1)} %pad_maximum_fusion.1), channel_id=1, source_target_pairs={{0,448},{64,0},{128,64},{192,128},{256,192},{320,256},{384,320},{4... | collective-permute-start | bytes 884744 | tf_op jit(solution)/shard_map/ppermute | solution.py:69
  31.9 23.2 %collective-permute-start.1 = (bf16[128,1152]{1,0:T(8,128)(2,1)S(1)}, bf16[128,1152]{1,0:T(8,128)(2,1)S(1)}, u32[]{:S(2)}, u32[]{:S(2)}) collective-permute-start(bf16[128,1152]{1,0:T(8,128)(2,1)S(1)} %pad_maximum_fusion.1), channel_id=1, source_target_pairs={{0,384},{64,448},{128,0},{192,64},{256,128},{320,192},{384,256},{4... | collective-permute-start | bytes 884744 | tf_op jit(solution)/shard_map/ppermute | solution.py:69
  34.4 48.3 %collective-permute-start.2 = (bf16[128,1152]{1,0:T(8,128)(2,1)S(1)}, bf16[128,1152]{1,0:T(8,128)(2,1)S(1)}, u32[]{:S(2)}, u32[]{:S(2)}) collective-permute-start(bf16[128,1152]{1,0:T(8,128)(2,1)S(1)} %pad_maximum_fusion.1), channel_id=1, source_target_pairs={{0,320},{64,384},{128,448},{192,0},{256,64},{320,128},{384,192},{4... | collective-permute-start | bytes 884744 | tf_op jit(solution)/shard_map/ppermute | solution.py:69
  36.3 46.4 %collective-permute-start.3 = (bf16[128,1152]{1,0:T(8,128)(2,1)S(1)}, bf16[128,1152]{1,0:T(8,128)(2,1)S(1)}, u32[]{:S(2)}, u32[]{:S(2)}) collective-permute-start(bf16[128,1152]{1,0:T(8,128)(2,1)S(1)} %pad_maximum_fusion.1), channel_id=1, source_target_pairs={{0,256},{64,320},{128,384},{192,448},{256,0},{320,64},{384,128},{4... | collective-permute-start | bytes 884744 | tf_op jit(solution)/shard_map/ppermute | solution.py:69
  44.1 39.3 %collective-permute-start.4 = (bf16[128,1152]{1,0:T(8,128)(2,1)S(1)}, bf16[128,1152]{1,0:T(8,128)(2,1)S(1)}, u32[]{:S(2)}, u32[]{:S(2)}) collective-permute-start(bf16[128,1152]{1,0:T(8,128)(2,1)S(1)} %pad_maximum_fusion.1), channel_id=1, source_target_pairs={{0,192},{64,256},{128,320},{192,384},{256,448},{320,0},{384,64},{4... | collective-permute-start | bytes 884744 | tf_op jit(solution)/shard_map/ppermute | solution.py:69
  46.1 42.0 %collective-permute-start.5 = (bf16[128,1152]{1,0:T(8,128)(2,1)S(1)}, bf16[128,1152]{1,0:T(8,128)(2,1)S(1)}, u32[]{:S(2)}, u32[]{:S(2)}) collective-permute-start(bf16[128,1152]{1,0:T(8,128)(2,1)S(1)} %pad_maximum_fusion.1), channel_id=1, source_target_pairs={{0,128},{64,192},{128,256},{192,320},{256,384},{320,448},{384,0},{... | collective-permute-start | bytes 884744 | tf_op jit(solution)/shard_map/ppermute | solution.py:69
  55.1 40.0 %collective-permute-start.6 = (bf16[128,1152]{1,0:T(8,128)(2,1)S(1)}, bf16[128,1152]{1,0:T(8,128)(2,1)S(1)}, u32[]{:S(2)}, u32[]{:S(2)}) collective-permute-start(bf16[128,1152]{1,0:T(8,128)(2,1)S(1)} %pad_maximum_fusion.1), channel_id=1, source_target_pairs={{0,64},{64,128},{128,192},{192,256},{256,320},{320,384},{384,448},... | collective-permute-start | bytes 884744 | tf_op jit(solution)/shard_map/ppermute | solution.py:69
  126.5 5.9 %copy-start.7 = (bf16[1024,384]{1,0:T(8,128)(2,1)S(1)}, bf16[1024,384]{1,0:T(8,128)(2,1)}, u32[]{:S(2)}) copy-start(bf16[1024,384]{1,0:T(8,128)(2,1)} %get-tuple-element.10) | copy-start | bytes 2359300
  126.5 102.0 %all-to-all-start.1 = ((bf16[64,16,2048]{2,1,0:T(8,128)(2,1)}), bf16[64,16,2048]{2,1,0:T(8,128)(2,1)}, u32[]{:S(2)}, u32[]{:S(2)}) async-start(bf16[64,16,2048]{2,1,0:T(8,128)(2,1)} %bitcast.84), calls=%async_computation.1 | async-start | bytes 8388608 | tf_op jit(solution)/shard_map/all_to_all | solution.py:120
  132.5 2.7 %copy-start.6 = (bf16[1024,768]{1,0:T(8,128)(2,1)S(1)}, bf16[1024,768]{1,0:T(8,128)(2,1)}, u32[]{:S(2)}) copy-start(bf16[1024,768]{1,0:T(8,128)(2,1)} %get-tuple-element.9) | copy-start | bytes 4718596
  144.5 26.4 %collective-permute-start.10 = (bf16[128,1152]{1,0:T(8,128)(2,1)S(1)}, bf16[128,1152]{1,0:T(8,128)(2,1)S(1)}, u32[]{:S(2)}, u32[]{:S(2)}) collective-permute-start(bf16[128,1152]{1,0:T(8,128)(2,1)S(1)} %get-tuple-element.32), channel_id=1, source_target_pairs={{0,256},{64,320},{128,384},{192,448},{256,0},{320,64},{384,128},{4... | collective-permute-start | bytes 884744 | tf_op jit(solution)/shard_map/ppermute | solution.py:85
  155.2 34.8 %collective-permute-start.11 = (bf16[128,1152]{1,0:T(8,128)(2,1)S(1)}, bf16[128,1152]{1,0:T(8,128)(2,1)S(1)}, u32[]{:S(2)}, u32[]{:S(2)}) collective-permute-start(bf16[128,1152]{1,0:T(8,128)(2,1)S(1)} %get-tuple-element.31), channel_id=1, source_target_pairs={{0,320},{64,384},{128,448},{192,0},{256,64},{320,128},{384,192},{4... | collective-permute-start | bytes 884744 | tf_op jit(solution)/shard_map/ppermute | solution.py:85
  157.2 44.1 %collective-permute-start.12 = (bf16[128,1152]{1,0:T(8,128)(2,1)}, bf16[128,1152]{1,0:T(8,128)(2,1)}, u32[]{:S(2)}, u32[]{:S(2)}) collective-permute-start(bf16[128,1152]{1,0:T(8,128)(2,1)} %get-tuple-element.30), channel_id=1, source_target_pairs={{0,384},{64,448},{128,0},{192,64},{256,128},{320,192},{384,256},{4... | collective-permute-start | bytes 884744 | tf_op jit(solution)/shard_map/ppermute | solution.py:85
  165.1 43.1 %collective-permute-start.13 = (bf16[128,1152]{1,0:T(8,128)(2,1)}, bf16[128,1152]{1,0:T(8,128)(2,1)}, u32[]{:S(2)}, u32[]{:S(2)}) collective-permute-start(bf16[128,1152]{1,0:T(8,128)(2,1)} %get-tuple-element.29), channel_id=1, source_target_pairs={{0,448},{64,0},{128,64},{192,128},{256,192},{320,256},{384,320},{4... | collective-permute-start | bytes 884744 | tf_op jit(solution)/shard_map/ppermute | solution.py:85
  167.5 40.6 %collective-permute-start.7 = (bf16[128,1152]{1,0:T(8,128)(2,1)}, bf16[128,1152]{1,0:T(8,128)(2,1)}, u32[]{:S(2)}, u32[]{:S(2)}) collective-permute-start(bf16[128,1152]{1,0:T(8,128)(2,1)} %get-tuple-element.28), channel_id=1, source_target_pairs={{0,64},{64,128},{128,192},{192,256},{256,320},{320,384},{384,448},... | collective-permute-start | bytes 884744 | tf_op jit(solution)/shard_map/ppermute | solution.py:85
  170.9 19.1 %copy-start.1 = (bf16[128,1152]{1,0:T(8,128)(2,1)}, bf16[128,1152]{1,0:T(8,128)(2,1)S(1)}, u32[]{:S(2)}) copy-start(bf16[128,1152]{1,0:T(8,128)(2,1)S(1)} %collective-permute-done.10) | copy-start | bytes 884740
  170.9 37.2 %collective-permute-start.8 = (bf16[128,1152]{1,0:T(8,128)(2,1)}, bf16[128,1152]{1,0:T(8,128)(2,1)}, u32[]{:S(2)}, u32[]{:S(2)}) collective-permute-start(bf16[128,1152]{1,0:T(8,128)(2,1)} %get-tuple-element.34), channel_id=1, source_target_pairs={{0,128},{64,192},{128,256},{192,320},{256,384},{320,448},{384,0},{... | collective-permute-start | bytes 884744 | tf_op jit(solution)/shard_map/ppermute | solution.py:85
  190.0 0.7 copy-start.2
  190.7 25.9 %collective-permute-start.9 = (bf16[128,1152]{1,0:T(8,128)(2,1)S(1)}, bf16[128,1152]{1,0:T(8,128)(2,1)}, u32[]{:S(2)}, u32[]{:S(2)}) collective-permute-start(bf16[128,1152]{1,0:T(8,128)(2,1)S(1)} %get-tuple-element.33), channel_id=1, source_target_pairs={{0,192},{64,256},{128,320},{192,384},{256,448},{320,0},{384,64},{4... | collective-permute-start | bytes 884744 | tf_op jit(solution)/shard_map/ppermute | solution.py:85
  216.6 12.0 %copy-start.3 = (bf16[1024,128]{1,0:T(8,128)(2,1)S(1)}, bf16[1024,128]{1,0:T(8,128)(2,1)}, u32[]{:S(2)}) copy-start(bf16[1024,128]{1,0:T(8,128)(2,1)} %get-tuple-element.35) | copy-start | bytes 786436
  216.6 12.0 %copy-start.4 = (bf16[1024,128]{1,0:T(8,128)(2,1)S(1)}, bf16[1024,128]{1,0:T(8,128)(2,1)}, u32[]{:S(2)}) copy-start(bf16[1024,128]{1,0:T(8,128)(2,1)} %get-tuple-element.36) | copy-start | bytes 786436
  228.6 6.4 %copy-start.8 = (bf16[128,1024]{1,0:T(8,128)(2,1)S(1)}, bf16[128,1024]{1,0:T(8,128)(2,1)}, u32[]{:S(2)}) copy-start(bf16[128,1024]{1,0:T(8,128)(2,1)} %param.11) | copy-start | bytes 786436

commit v7 on v6

--- a/solution.py
+++ b/solution.py
@@ -58,6 +58,35 @@
             jax.ShapeDtypeStruct((slots, gate_width), jnp.bfloat16),
         ],
     )(recv, weights)
+
+
+def combine_kernel(comb_ref, back_ref, cot_ref, moe_ref, tgrad_ref, gate_ref, *, width, tokens):
+    contract_last = (((1,), (1,)), ((), ()))
+    out_rows = back_ref[:, :width]
+    weighted = jnp.dot(comb_ref[: 3 * tokens, :], out_rows, preferred_element_type=jnp.float32)
+    moe_ref[...] = (
+        weighted[:tokens] + weighted[tokens : 2 * tokens] + weighted[2 * tokens :]
+    ).astype(moe_ref.dtype)
+    tgrad_ref[...] = jnp.dot(
+        comb_ref[3 * tokens :, :], back_ref[:, width:], preferred_element_type=jnp.float32
+    ).astype(tgrad_ref.dtype)
+    gate_ref[...] = lax.dot_general(
+        cot_ref[...], out_rows, contract_last, preferred_element_type=jnp.float32
+    )
+
+
+def combine_call(comb_t, back, cotangent):
+    tokens, width = cotangent.shape
+    slots = back.shape[0]
+    kernel = functools.partial(combine_kernel, width=width, tokens=tokens)
+    return pl.pallas_call(
+        kernel,
+        out_shape=[
+            jax.ShapeDtypeStruct((tokens, width), jnp.bfloat16),
+            jax.ShapeDtypeStruct((tokens, width), jnp.bfloat16),
+            jax.ShapeDtypeStruct((tokens, slots), jnp.float32),
+        ],
+    )(comb_t, back, cotangent)
 
 
 def gather_dp(block):
@@ -135,18 +164,7 @@
     low = rest - middle
     parts = [part.astype(jnp.bfloat16) for part in (high, middle, low)]
     combine = jnp.concatenate(parts + [select_rows], axis=1)
-    summed = lax.dot_general(
-        combine, back, (((0,), (0,)), ((), ())), preferred_element_type=jnp.float32
-    )
-    moe_out = (
-        summed[:token_count, :width]
-        + summed[token_count : 2 * token_count, :width]
-        + summed[2 * token_count : 3 * token_count, :width]
-    ).astype(jnp.bfloat16)
-    token_grads = summed[3 * token_count :, width:].astype(jnp.bfloat16)
-    token_slot = lax.dot_general(
-        cotangent, back[:, :width], (((1,), (1,)), ((), ())), preferred_element_type=jnp.float32
-    )
+    moe_out, token_grads, token_slot = combine_call(combine.T, back, cotangent)
     gate_grads = jnp.sum(jnp.where(hits, token_slot.T[:, :, None], 0.0), axis=0)
     return (moe_out, token_grads, gate_grads, sum_in, sum_out)
 

time: 239 us -> 237 us (level)
  matrix products: 17.6 us -> 10.5 us
  Pallas kernels: 9.47 us -> 14.7 us
    dot_general x2 -> x0, matrix products: 7.13 us -> none  [the longest x1 4.84 us: local(): lax.dot_general(combine, back, (((0,), (0,)), ((), ())), preferred_elemen...]
    pallas_call x0 -> x1, Pallas kernels: none -> 5.23 us  [combine_call(): pl.pallas_call(kernel, out_shape=[jax.ShapeDtypeStruct((tokens, width), j...]
  transfers between devices with their start and end apart: 16 -> 16, of which waited for: 11 -> 11; matrix products, arithmetic and copies ran while one was open for 8% -> 9% of each run, Pallas kernels for 0% -> 0%
where the time goes in v7:
time: 237 us; the launch traced here: 236 us
  waiting for transfers between devices  106 us (45%)
  starting transfers between devices  82.5 us (35%)
  Pallas kernels  14.7 us (6%)
  local copies, waits for them, and re-layouts  11.2 us (5%)
  matrix products  10.5 us (4%)
  other arithmetic  10.3 us (4%)
    ppermute x7, waiting for transfers between devices, gather_dp(): pieces.append(lax.ppermute(block, 'dp', pairs))  43.5 us
    ppermute x7, starting transfers between devices, scatter_dp(): total = total + lax.ppermute(part, 'dp', pairs).astype(jnp.float32)  35.4 us
    ppermute x7, waiting for transfers between devices, scatter_dp(): total = total + lax.ppermute(part, 'dp', pairs).astype(jnp.float32)  32.9 us
    ppermute x7, starting transfers between devices, gather_dp(): pieces.append(lax.ppermute(block, 'dp', pairs))  30.3 us
    all_to_all x1, waiting for transfers between devices, local(): lax.all_to_all(send, 'expert', split_axis=0, concat_axis=0, tiled=True)  20 us
    all_to_all x1, starting transfers between devices, local(): lax.all_to_all(send, 'expert', split_axis=0, concat_axis=0, tiled=True)  11 us
    pallas_call x1, Pallas kernels, expert_call(): pl.pallas_call(kernel, grid=(slots // block,), in_specs=[pl.BlockSpec((bl...  9.46 us
    all_to_all x1, waiting for transfers between devices, local(): lax.all_to_all(payload, 'expert', split_axis=0, concat_axis=0, tiled=True)  9.24 us
  transfers between devices with their start and end apart: 16, of which 11 were waited for; matrix products, arithmetic and copies ran while one was open for 9% of the time, Pallas kernels for 0%

profile of v7, /device:TPU:6, one launch (start us, length us, event | category | flops | bytes accessed | tf_op | source)
XLA Modules:
  0.0 235.9 jit_solution(9664007328396789521)
XLA Ops:
  0.6 0.8 copy.53
  1.4 0.1 eq.50
  1.5 0.1 eq.46
  1.7 1.2 reduce-window.6
  2.9 0.2 slice_reduce_fusion
  3.1 0.1 fusion.23
  3.3 0.1 reduce_sum.39
  3.4 0.1 copy.56
  3.5 0.7 multiply_add_fusion
  4.2 0.4 fusion.4
  4.5 1.0 select_reduce_fusion
  5.5 4.3 %multiply_convert_fusion = bf16[1024,2048]{1,0:T(8,128)(2,1)} fusion(pred[1024,128]{1,0:T(8,128)(4,1)S(1)} %fusion.4, f32[1024]{0:T(1024)S(1)} %get-tuple-element.32, pred[2048]{0:T(1024)(128)(4,1)S(1)} %iota_compare_fusion.3, bf16[128,1024]{1,0:T(8,128)(2,1)} %cot_ref.1, bf16[128,1024]{1,0:T(8,128)(2,1)} %param.6), kind=kOutput, calls=%fused_computation | convolution fusion | flops 544210944 | bytes 4855808 | tf_op jit(solution)/shard_map/dot_general | solution.py:143
  9.9 11.0 %all-to-all-start = ((bf16[64,16,2048]{2,1,0:T(8,128)(2,1)}), bf16[64,16,2048]{2,1,0:T(8,128)(2,1)}, u32[]{:S(2)}, u32[]{:S(2)}) async-start(bf16[64,16,2048]{2,1,0:T(8,128)(2,1)} %bitcast.86), calls=%async_computation | async-start | bytes 8388608 | tf_op jit(solution)/shard_map/all_to_all | solution.py:147
  20.9 0.1 copy.60
  21.0 0.0 copy-done
  21.1 10.9 %collective-permute-start = (bf16[128,1152]{1,0:T(8,128)(2,1)S(1)}, bf16[128,1152]{1,0:T(8,128)(2,1)S(1)}, u32[]{:S(2)}, u32[]{:S(2)}) collective-permute-start(bf16[128,1152]{1,0:T(8,128)(2,1)S(1)} %pad_maximum_fusion.1), channel_id=1, source_target_pairs={{0,448},{64,0},{128,64},{192,128},{256,192},{320,256},{384,320},{4... | collective-permute-start | bytes 884744 | tf_op jit(solution)/shard_map/ppermute | solution.py:98
  31.9 2.5 %collective-permute-start.1 = (bf16[128,1152]{1,0:T(8,128)(2,1)S(1)}, bf16[128,1152]{1,0:T(8,128)(2,1)S(1)}, u32[]{:S(2)}, u32[]{:S(2)}) collective-permute-start(bf16[128,1152]{1,0:T(8,128)(2,1)S(1)} %pad_maximum_fusion.1), channel_id=1, source_target_pairs={{0,384},{64,448},{128,0},{192,64},{256,128},{320,192},{384,256},{4... | collective-permute-start | bytes 884744 | tf_op jit(solution)/shard_map/ppermute | solution.py:98
  34.4 1.9 collective-permute-start.2
  36.3 7.8 %collective-permute-start.3 = (bf16[128,1152]{1,0:T(8,128)(2,1)S(1)}, bf16[128,1152]{1,0:T(8,128)(2,1)S(1)}, u32[]{:S(2)}, u32[]{:S(2)}) collective-permute-start(bf16[128,1152]{1,0:T(8,128)(2,1)S(1)} %pad_maximum_fusion.1), channel_id=1, source_target_pairs={{0,256},{64,320},{128,384},{192,448},{256,0},{320,64},{384,128},{4... | collective-permute-start | bytes 884744 | tf_op jit(solution)/shard_map/ppermute | solution.py:98
  44.2 1.9 collective-permute-start.4
  46.1 0.0 collective-permute-done
  46.1 3.4 %collective-permute-start.5 = (bf16[128,1152]{1,0:T(8,128)(2,1)S(1)}, bf16[128,1152]{1,0:T(8,128)(2,1)S(1)}, u32[]{:S(2)}, u32[]{:S(2)}) collective-permute-start(bf16[128,1152]{1,0:T(8,128)(2,1)S(1)} %pad_maximum_fusion.1), channel_id=1, source_target_pairs={{0,128},{64,192},{128,256},{192,320},{256,384},{320,448},{384,0},{... | collective-permute-start | bytes 884744 | tf_op jit(solution)/shard_map/ppermute | solution.py:98
  49.5 5.6 %collective-permute-done.1 = bf16[128,1152]{1,0:T(8,128)(2,1)S(1)} collective-permute-done((bf16[128,1152]{1,0:T(8,128)(2,1)S(1)}, bf16[128,1152]{1,0:T(8,128)(2,1)S(1)}, u32[]{:S(2)}, u32[]{:S(2)}) %collective-permute-start.1) | collective-permute-done | bytes 294944 | tf_op jit(solution)/shard_map/ppermute | solution.py:98
  55.2 1.9 collective-permute-start.6
  57.1 25.6 %collective-permute-done.2 = bf16[128,1152]{1,0:T(8,128)(2,1)S(1)} collective-permute-done((bf16[128,1152]{1,0:T(8,128)(2,1)S(1)}, bf16[128,1152]{1,0:T(8,128)(2,1)S(1)}, u32[]{:S(2)}, u32[]{:S(2)}) %collective-permute-start.2) | collective-permute-done | bytes 294944 | tf_op jit(solution)/shard_map/ppermute | solution.py:98
  82.7 0.0 collective-permute-done.3
  82.8 0.7 collective-permute-done.4
  83.5 4.6 %collective-permute-done.5 = bf16[128,1152]{1,0:T(8,128)(2,1)S(1)} collective-permute-done((bf16[128,1152]{1,0:T(8,128)(2,1)S(1)}, bf16[128,1152]{1,0:T(8,128)(2,1)S(1)}, u32[]{:S(2)}, u32[]{:S(2)}) %collective-permute-start.5) | collective-permute-done | bytes 294944 | tf_op jit(solution)/shard_map/ppermute | solution.py:98
  88.1 7.0 %collective-permute-done.6 = bf16[128,1152]{1,0:T(8,128)(2,1)S(1)} collective-permute-done((bf16[128,1152]{1,0:T(8,128)(2,1)S(1)}, bf16[128,1152]{1,0:T(8,128)(2,1)S(1)}, u32[]{:S(2)}, u32[]{:S(2)}) %collective-permute-start.6) | collective-permute-done | bytes 294944 | tf_op jit(solution)/shard_map/ppermute | solution.py:98
  95.5 1.6 constant_dynamic-slice_fusion
  97.1 20.0 %all-to-all-done = bf16[64,16,2048]{2,1,0:T(8,128)(2,1)} async-done(((bf16[64,16,2048]{2,1,0:T(8,128)(2,1)}), bf16[64,16,2048]{2,1,0:T(8,128)(2,1)}, u32[]{:S(2)}, u32[]{:S(2)}) %all-to-all-start) | async-done | bytes 4194336 | tf_op jit(solution)/shard_map/all_to_all | solution.py:147
  117.1 9.5 %shard_map.101 = (bf16[1024,2048]{1,0:T(8,128)(2,1)}, bf16[1024,384]{1,0:T(8,128)(2,1)}, bf16[1024,768]{1,0:T(8,128)(2,1)}) custom-call(bf16[1024,2048]{1,0:T(8,128)(2,1)} %bitcast.3.recv_ref, bf16[1024,1152]{1,0:T(8,128)(2,1)} %bitcast.82), custom_call_target="tpu_custom_call" | custom-call | tf_op jit(solution)/shard_map/pallas_call | solution.py:43
  126.6 5.8 %all-to-all-start.1 = ((bf16[64,16,2048]{2,1,0:T(8,128)(2,1)}), bf16[64,16,2048]{2,1,0:T(8,128)(2,1)}, u32[]{:S(2)}, u32[]{:S(2)}) async-start(bf16[64,16,2048]{2,1,0:T(8,128)(2,1)} %bitcast.85), calls=%async_computation.1 | async-start | bytes 8388608 | tf_op jit(solution)/shard_map/all_to_all | solution.py:149
  132.5 2.7 %fusion.8 = bf16[1024,384]{0,1:T(8,128)(2,1)S(1)} fusion(bf16[1024,384]{1,0:T(8,128)(2,1)S(1)} %copy-done.3, bf16[1024,2048]{1,0:T(8,128)(2,1)} %bitcast.3.recv_ref), kind=kOutput, calls=%fused_computation.12 | convolution fusion | flops 805699584 | bytes 3670016 | tf_op jit(solution)/shard_map/dot_general | solution.py:154
  135.2 3.4 %fusion.5 = bf16[1024,768]{0,1:T(8,128)(2,1)S(1)} fusion(bf16[1024,768]{1,0:T(8,128)(2,1)S(1)} %copy-done.2, bf16[1024,2048]{1,0:T(8,128)(2,1)} %bitcast.3.recv_ref), kind=kOutput, calls=%fused_computation.11 | convolution fusion | flops 1611399168 | bytes 5242880 | tf_op jit(solution)/shard_map/dot_general | solution.py:151
  138.7 1.7 pad_maximum_fusion
  140.4 3.0 %copy.71 = bf16[1024,1152]{1,0:T(8,128)(2,1)S(1)} copy(bf16[1024,1152]{0,1:T(8,128)(2,1)} %pad_maximum_fusion) | data formatting | bytes 4718592 | tf_op jit(solution)/shard_map/reshape | solution.py:109
  143.4 1.3 dynamic-slice_bitcast_fusion.6
  144.7 10.7 %collective-permute-start.10 = (bf16[128,1152]{1,0:T(8,128)(2,1)}, bf16[128,1152]{1,0:T(8,128)(2,1)}, u32[]{:S(2)}, u32[]{:S(2)}) collective-permute-start(bf16[128,1152]{1,0:T(8,128)(2,1)} %get-tuple-element.38), channel_id=1, source_target_pairs={{0,256},{64,320},{128,384},{192,448},{256,0},{320,64},{384,128},{4... | collective-permute-start | bytes 884744 | tf_op jit(solution)/shard_map/ppermute | solution.py:114
  155.5 1.9 collective-permute-start.11
  157.4 0.2 copy.59
  157.6 0.2 copy.57
  157.9 0.7 convert_element_type.60
  158.6 7.8 %collective-permute-start.12 = (bf16[128,1152]{1,0:T(8,128)(2,1)}, bf16[128,1152]{1,0:T(8,128)(2,1)S(1)}, u32[]{:S(2)}, u32[]{:S(2)}) collective-permute-start(bf16[128,1152]{1,0:T(8,128)(2,1)} %get-tuple-element.36), channel_id=1, source_target_pairs={{0,384},{64,448},{128,0},{192,64},{256,128},{320,192},{384,256},{4... | collective-permute-start | bytes 884744 | tf_op jit(solution)/shard_map/ppermute | solution.py:114
  166.4 2.5 %collective-permute-start.13 = (bf16[128,1152]{1,0:T(8,128)(2,1)}, bf16[128,1152]{1,0:T(8,128)(2,1)S(1)}, u32[]{:S(2)}, u32[]{:S(2)}) collective-permute-start(bf16[128,1152]{1,0:T(8,128)(2,1)} %get-tuple-element.35), channel_id=1, source_target_pairs={{0,448},{64,0},{128,64},{192,128},{256,192},{320,256},{384,320},{4... | collective-permute-start | bytes 884744 | tf_op jit(solution)/shard_map/ppermute | solution.py:114
  168.9 3.4 %collective-permute-start.7 = (bf16[128,1152]{1,0:T(8,128)(2,1)}, bf16[128,1152]{1,0:T(8,128)(2,1)S(1)}, u32[]{:S(2)}, u32[]{:S(2)}) collective-permute-start(bf16[128,1152]{1,0:T(8,128)(2,1)} %get-tuple-element.34), channel_id=1, source_target_pairs={{0,64},{64,128},{128,192},{192,256},{256,320},{320,384},{384,448},... | collective-permute-start | bytes 884744 | tf_op jit(solution)/shard_map/ppermute | solution.py:114
  172.3 0.0 collective-permute-done.10
  172.3 1.9 collective-permute-start.8
  174.2 16.3 %collective-permute-done.11 = bf16[128,1152]{1,0:T(8,128)(2,1)} collective-permute-done((bf16[128,1152]{1,0:T(8,128)(2,1)}, bf16[128,1152]{1,0:T(8,128)(2,1)}, u32[]{:S(2)}, u32[]{:S(2)}) %collective-permute-start.11) | collective-permute-done | bytes 294944 | tf_op jit(solution)/shard_map/ppermute | solution.py:114
  190.5 7.1 %collective-permute-start.9 = (bf16[128,1152]{1,0:T(8,128)(2,1)}, bf16[128,1152]{1,0:T(8,128)(2,1)S(1)}, u32[]{:S(2)}, u32[]{:S(2)}) collective-permute-start(bf16[128,1152]{1,0:T(8,128)(2,1)} %get-tuple-element.39), channel_id=1, source_target_pairs={{0,192},{64,256},{128,320},{192,384},{256,448},{320,0},{384,64},{4... | collective-permute-start | bytes 884744 | tf_op jit(solution)/shard_map/ppermute | solution.py:114
  197.7 0.1 reduce-precision_convert_fusion.1
  197.8 2.1 maximum_bitcast_fusion.comb_ref
  199.8 1.7 collective-permute-done.12
  201.6 6.9 %collective-permute-done.13 = bf16[128,1152]{1,0:T(8,128)(2,1)S(1)} collective-permute-done((bf16[128,1152]{1,0:T(8,128)(2,1)}, bf16[128,1152]{1,0:T(8,128)(2,1)S(1)}, u32[]{:S(2)}, u32[]{:S(2)}) %collective-permute-start.13) | collective-permute-done | bytes 294944 | tf_op jit(solution)/shard_map/ppermute | solution.py:114
  208.4 0.0 collective-permute-done.7
  208.4 0.0 collective-permute-done.8
  208.4 8.0 %collective-permute-done.9 = bf16[128,1152]{1,0:T(8,128)(2,1)S(1)} collective-permute-done((bf16[128,1152]{1,0:T(8,128)(2,1)}, bf16[128,1152]{1,0:T(8,128)(2,1)S(1)}, u32[]{:S(2)}, u32[]{:S(2)}) %collective-permute-start.9) | collective-permute-done | bytes 294944 | tf_op jit(solution)/shard_map/ppermute | solution.py:114
  216.4 1.3 fusion.16
  217.8 0.8 copy.70
  218.6 0.8 slice_bitcast_fusion
  219.4 9.2 %all-to-all-done.1 = bf16[64,16,2048]{2,1,0:T(8,128)(2,1)} async-done(((bf16[64,16,2048]{2,1,0:T(8,128)(2,1)}), bf16[64,16,2048]{2,1,0:T(8,128)(2,1)}, u32[]{:S(2)}, u32[]{:S(2)}) %all-to-all-start.1) | async-done | bytes 4194336 | tf_op jit(solution)/shard_map/all_to_all | solution.py:149
  228.6 5.2 %shard_map.102 = (bf16[128,1024]{1,0:T(8,128)(2,1)}, bf16[128,1024]{1,0:T(8,128)(2,1)}, f32[128,1024]{1,0:T(8,128)}) custom-call(bf16[512,1024]{1,0:T(8,128)(2,1)} %maximum_bitcast_fusion.comb_ref, bf16[1024,2048]{1,0:T(8,128)(2,1)} %bitcast.17.back_ref, bf16[128,1024]{1,0:T(8,128)(2,1)} %cot_ref.1), custom_call_target="tpu_custom_call" | custom-call | tf_op jit(solution)/shard_map/pallas_call | solution.py:82
  233.8 1.2 copy.61
  235.1 0.8 select_reduce_fusion.2
  (29 shorter events, 0.6 us)
Async XLA Ops:
  9.9 11.0 %copy-start.1 = (bf16[1,384,128]{2,1,0:T(8,128)(2,1)S(1)}, bf16[1,384,128]{2,1,0:T(8,128)(2,1)}, u32[]{:S(2)}) copy-start(bf16[1,384,128]{2,1,0:T(8,128)(2,1)} %param.10) | copy-start | bytes 294916
  9.9 11.2 %copy-start = (bf16[1,128,768]{2,1,0:T(8,128)(2,1)S(1)}, bf16[1,128,768]{2,1,0:T(8,128)(2,1)}, u32[]{:S(2)}) copy-start(bf16[1,128,768]{2,1,0:T(8,128)(2,1)} %param.9) | copy-start | bytes 589828
  9.9 107.2 %all-to-all-start = ((bf16[64,16,2048]{2,1,0:T(8,128)(2,1)}), bf16[64,16,2048]{2,1,0:T(8,128)(2,1)}, u32[]{:S(2)}, u32[]{:S(2)}) async-start(bf16[64,16,2048]{2,1,0:T(8,128)(2,1)} %bitcast.86), calls=%async_computation | async-start | bytes 8388608 | tf_op jit(solution)/shard_map/all_to_all | solution.py:147
  21.1 25.0 %collective-permute-start = (bf16[128,1152]{1,0:T(8,128)(2,1)S(1)}, bf16[128,1152]{1,0:T(8,128)(2,1)S(1)}, u32[]{:S(2)}, u32[]{:S(2)}) collective-permute-start(bf16[128,1152]{1,0:T(8,128)(2,1)S(1)} %pad_maximum_fusion.1), channel_id=1, source_target_pairs={{0,448},{64,0},{128,64},{192,128},{256,192},{320,256},{384,320},{4... | collective-permute-start | bytes 884744 | tf_op jit(solution)/shard_map/ppermute | solution.py:98
  31.9 23.2 %collective-permute-start.1 = (bf16[128,1152]{1,0:T(8,128)(2,1)S(1)}, bf16[128,1152]{1,0:T(8,128)(2,1)S(1)}, u32[]{:S(2)}, u32[]{:S(2)}) collective-permute-start(bf16[128,1152]{1,0:T(8,128)(2,1)S(1)} %pad_maximum_fusion.1), channel_id=1, source_target_pairs={{0,384},{64,448},{128,0},{192,64},{256,128},{320,192},{384,256},{4... | collective-permute-start | bytes 884744 | tf_op jit(solution)/shard_map/ppermute | solution.py:98
  34.4 48.3 %collective-permute-start.2 = (bf16[128,1152]{1,0:T(8,128)(2,1)S(1)}, bf16[128,1152]{1,0:T(8,128)(2,1)S(1)}, u32[]{:S(2)}, u32[]{:S(2)}) collective-permute-start(bf16[128,1152]{1,0:T(8,128)(2,1)S(1)} %pad_maximum_fusion.1), channel_id=1, source_target_pairs={{0,320},{64,384},{128,448},{192,0},{256,64},{320,128},{384,192},{4... | collective-permute-start | bytes 884744 | tf_op jit(solution)/shard_map/ppermute | solution.py:98
  36.3 46.4 %collective-permute-start.3 = (bf16[128,1152]{1,0:T(8,128)(2,1)S(1)}, bf16[128,1152]{1,0:T(8,128)(2,1)S(1)}, u32[]{:S(2)}, u32[]{:S(2)}) collective-permute-start(bf16[128,1152]{1,0:T(8,128)(2,1)S(1)} %pad_maximum_fusion.1), channel_id=1, source_target_pairs={{0,256},{64,320},{128,384},{192,448},{256,0},{320,64},{384,128},{4... | collective-permute-start | bytes 884744 | tf_op jit(solution)/shard_map/ppermute | solution.py:98
  44.2 39.3 %collective-permute-start.4 = (bf16[128,1152]{1,0:T(8,128)(2,1)S(1)}, bf16[128,1152]{1,0:T(8,128)(2,1)S(1)}, u32[]{:S(2)}, u32[]{:S(2)}) collective-permute-start(bf16[128,1152]{1,0:T(8,128)(2,1)S(1)} %pad_maximum_fusion.1), channel_id=1, source_target_pairs={{0,192},{64,256},{128,320},{192,384},{256,448},{320,0},{384,64},{4... | collective-permute-start | bytes 884744 | tf_op jit(solution)/shard_map/ppermute | solution.py:98
  46.1 42.0 %collective-permute-start.5 = (bf16[128,1152]{1,0:T(8,128)(2,1)S(1)}, bf16[128,1152]{1,0:T(8,128)(2,1)S(1)}, u32[]{:S(2)}, u32[]{:S(2)}) collective-permute-start(bf16[128,1152]{1,0:T(8,128)(2,1)S(1)} %pad_maximum_fusion.1), channel_id=1, source_target_pairs={{0,128},{64,192},{128,256},{192,320},{256,384},{320,448},{384,0},{... | collective-permute-start | bytes 884744 | tf_op jit(solution)/shard_map/ppermute | solution.py:98
  55.2 39.9 %collective-permute-start.6 = (bf16[128,1152]{1,0:T(8,128)(2,1)S(1)}, bf16[128,1152]{1,0:T(8,128)(2,1)S(1)}, u32[]{:S(2)}, u32[]{:S(2)}) collective-permute-start(bf16[128,1152]{1,0:T(8,128)(2,1)S(1)} %pad_maximum_fusion.1), channel_id=1, source_target_pairs={{0,64},{64,128},{128,192},{192,256},{256,320},{320,384},{384,448},... | collective-permute-start | bytes 884744 | tf_op jit(solution)/shard_map/ppermute | solution.py:98
  126.6 6.0 %copy-start.3 = (bf16[1024,384]{1,0:T(8,128)(2,1)S(1)}, bf16[1024,384]{1,0:T(8,128)(2,1)}, u32[]{:S(2)}) copy-start(bf16[1024,384]{1,0:T(8,128)(2,1)} %get-tuple-element.16) | copy-start | bytes 2359300
  126.6 102.0 %all-to-all-start.1 = ((bf16[64,16,2048]{2,1,0:T(8,128)(2,1)}), bf16[64,16,2048]{2,1,0:T(8,128)(2,1)}, u32[]{:S(2)}, u32[]{:S(2)}) async-start(bf16[64,16,2048]{2,1,0:T(8,128)(2,1)} %bitcast.85), calls=%async_computation.1 | async-start | bytes 8388608 | tf_op jit(solution)/shard_map/all_to_all | solution.py:149
  132.4 2.8 %copy-start.2 = (bf16[1024,768]{1,0:T(8,128)(2,1)S(1)}, bf16[1024,768]{1,0:T(8,128)(2,1)}, u32[]{:S(2)}) copy-start(bf16[1024,768]{1,0:T(8,128)(2,1)} %get-tuple-element.15) | copy-start | bytes 4718596
  144.7 27.6 %collective-permute-start.10 = (bf16[128,1152]{1,0:T(8,128)(2,1)}, bf16[128,1152]{1,0:T(8,128)(2,1)}, u32[]{:S(2)}, u32[]{:S(2)}) collective-permute-start(bf16[128,1152]{1,0:T(8,128)(2,1)} %get-tuple-element.38), channel_id=1, source_target_pairs={{0,256},{64,320},{128,384},{192,448},{256,0},{320,64},{384,128},{4... | collective-permute-start | bytes 884744 | tf_op jit(solution)/shard_map/ppermute | solution.py:114
  155.5 35.1 %collective-permute-start.11 = (bf16[128,1152]{1,0:T(8,128)(2,1)}, bf16[128,1152]{1,0:T(8,128)(2,1)}, u32[]{:S(2)}, u32[]{:S(2)}) collective-permute-start(bf16[128,1152]{1,0:T(8,128)(2,1)} %get-tuple-element.37), channel_id=1, source_target_pairs={{0,320},{64,384},{128,448},{192,0},{256,64},{320,128},{384,192},{4... | collective-permute-start | bytes 884744 | tf_op jit(solution)/shard_map/ppermute | solution.py:114
  158.6 43.0 %collective-permute-start.12 = (bf16[128,1152]{1,0:T(8,128)(2,1)}, bf16[128,1152]{1,0:T(8,128)(2,1)S(1)}, u32[]{:S(2)}, u32[]{:S(2)}) collective-permute-start(bf16[128,1152]{1,0:T(8,128)(2,1)} %get-tuple-element.36), channel_id=1, source_target_pairs={{0,384},{64,448},{128,0},{192,64},{256,128},{320,192},{384,256},{4... | collective-permute-start | bytes 884744 | tf_op jit(solution)/shard_map/ppermute | solution.py:114
  166.4 42.0 %collective-permute-start.13 = (bf16[128,1152]{1,0:T(8,128)(2,1)}, bf16[128,1152]{1,0:T(8,128)(2,1)S(1)}, u32[]{:S(2)}, u32[]{:S(2)}) collective-permute-start(bf16[128,1152]{1,0:T(8,128)(2,1)} %get-tuple-element.35), channel_id=1, source_target_pairs={{0,448},{64,0},{128,64},{192,128},{256,192},{320,256},{384,320},{4... | collective-permute-start | bytes 884744 | tf_op jit(solution)/shard_map/ppermute | solution.py:114
  168.9 39.6 %collective-permute-start.7 = (bf16[128,1152]{1,0:T(8,128)(2,1)}, bf16[128,1152]{1,0:T(8,128)(2,1)S(1)}, u32[]{:S(2)}, u32[]{:S(2)}) collective-permute-start(bf16[128,1152]{1,0:T(8,128)(2,1)} %get-tuple-element.34), channel_id=1, source_target_pairs={{0,64},{64,128},{128,192},{192,256},{256,320},{320,384},{384,448},... | collective-permute-start | bytes 884744 | tf_op jit(solution)/shard_map/ppermute | solution.py:114
  172.3 36.2 %collective-permute-start.8 = (bf16[128,1152]{1,0:T(8,128)(2,1)}, bf16[128,1152]{1,0:T(8,128)(2,1)S(1)}, u32[]{:S(2)}, u32[]{:S(2)}) collective-permute-start(bf16[128,1152]{1,0:T(8,128)(2,1)} %get-tuple-element.40), channel_id=1, source_target_pairs={{0,128},{64,192},{128,256},{192,320},{256,384},{320,448},{384,0},{... | collective-permute-start | bytes 884744 | tf_op jit(solution)/shard_map/ppermute | solution.py:114
  190.5 25.9 %collective-permute-start.9 = (bf16[128,1152]{1,0:T(8,128)(2,1)}, bf16[128,1152]{1,0:T(8,128)(2,1)S(1)}, u32[]{:S(2)}, u32[]{:S(2)}) collective-permute-start(bf16[128,1152]{1,0:T(8,128)(2,1)} %get-tuple-element.39), channel_id=1, source_target_pairs={{0,192},{64,256},{128,320},{192,384},{256,448},{320,0},{384,64},{4... | collective-permute-start | bytes 884744 | tf_op jit(solution)/shard_map/ppermute | solution.py:114

commit v8 on v7

--- a/solution.py
+++ b/solution.py
@@ -89,6 +89,29 @@
     )(comb_t, back, cotangent)
 
 
+def dispatch_kernel(sel_ref, both_ref, prob_ref, send_ref, *, width):
+    gathered = jnp.dot(sel_ref[...], both_ref[...], preferred_element_type=jnp.float32)
+    send_ref[:, :width] = gathered[:, :width].astype(send_ref.dtype)
+    send_ref[:, width:] = (gathered[:, width:] * prob_ref[...]).astype(send_ref.dtype)
+
+
+def dispatch_call(select_rows, both, slot_probs, block=256):
+    slots, tokens = select_rows.shape
+    columns = both.shape[1]
+    kernel = functools.partial(dispatch_kernel, width=columns // 2)
+    return pl.pallas_call(
+        kernel,
+        grid=(slots // block,),
+        in_specs=[
+            pl.BlockSpec((block, tokens), lambda i: (i, 0)),
+            pl.BlockSpec((tokens, columns), lambda i: (0, 0)),
+            pl.BlockSpec((block, 1), lambda i: (i, 0)),
+        ],
+        out_specs=pl.BlockSpec((block, columns), lambda i: (i, 0)),
+        out_shape=jax.ShapeDtypeStruct((slots, columns), jnp.bfloat16),
+    )(select_rows, both, slot_probs[:, None])
+
+
 def gather_dp(block):
     size = lax.axis_size("dp")
     me = lax.axis_index("dp")
@@ -140,10 +163,7 @@
     select_rows = select.astype(jnp.bfloat16)
 
     both = jnp.concatenate([tokens, cotangent], axis=1)
-    gathered = jnp.dot(select_rows, both, preferred_element_type=jnp.float32)
-    column = lax.broadcasted_iota(jnp.int32, gathered.shape, 1)
-    send = (gathered * jnp.where(column < width, 1.0, slot_probs[:, None])).astype(jnp.bfloat16)
-
+    send = dispatch_call(select_rows, both, slot_probs)
     recv = lax.all_to_all(send, "expert", split_axis=0, concat_axis=0, tiled=True)
     payload, hidden, grad_pre = expert_call(recv, weights, gate_width)
     back = lax.all_to_all(payload, "expert", split_axis=0, concat_axis=0, tiled=True)

time: 237 us -> 242 us (1.021)
  Pallas kernels: 14.7 us -> 19.6 us
  matrix products: 10.5 us -> 6.14 us
  local copies, waits for them, and re-layouts: 11.2 us -> 13.9 us
    pallas_call x0 -> x1, Pallas kernels: none -> 4.9 us  [dispatch_call(): pl.pallas_call(kernel, grid=(slots // block,), in_specs=[pl.BlockSpec((bl...]
    dot_general x1 -> x0, matrix products: 4.33 us -> none  [local(): gathered = jnp.dot(select_rows, both, preferred_element_type=jnp.float32)]
where the time goes in v8:
time: 242 us; the launch traced here: 240 us
  waiting for transfers between devices  106 us (44%)
  starting transfers between devices  82.5 us (34%)
  Pallas kernels  19.6 us (8%)
  local copies, waits for them, and re-layouts  13.9 us (6%)
  other arithmetic  11.6 us (5%)
  matrix products  6.14 us (3%)
    ppermute x7, waiting for transfers between devices, gather_dp(): pieces.append(lax.ppermute(block, 'dp', pairs))  43.5 us
    ppermute x7, starting transfers between devices, scatter_dp(): total = total + lax.ppermute(part, 'dp', pairs).astype(jnp.float32)  35.4 us
    ppermute x7, waiting for transfers between devices, scatter_dp(): total = total + lax.ppermute(part, 'dp', pairs).astype(jnp.float32)  32.7 us
    ppermute x7, starting transfers between devices, gather_dp(): pieces.append(lax.ppermute(block, 'dp', pairs))  30.3 us
    all_to_all x1, waiting for transfers between devices, local(): lax.all_to_all(send, 'expert', split_axis=0, concat_axis=0, tiled=True)  19.9 us
    all_to_all x1, starting transfers between devices, local(): lax.all_to_all(send, 'expert', split_axis=0, concat_axis=0, tiled=True)  11 us
    all_to_all x1, waiting for transfers between devices, local(): lax.all_to_all(payload, 'expert', split_axis=0, concat_axis=0, tiled=True)  9.56 us
    pallas_call x1, Pallas kernels, expert_call(): pl.pallas_call(kernel, grid=(slots // block,), in_specs=[pl.BlockSpec((bl...  9.46 us
  transfers between devices with their start and end apart: 16, of which 11 were waited for; matrix products, arithmetic and copies ran while one was open for 9% of the time, Pallas kernels for 0%

profile of v8, /device:TPU:6, one launch (start us, length us, event | category | flops | bytes accessed | tf_op | source)
XLA Modules:
  0.0 240.5 jit_solution(10896933971324508996)
XLA Ops:
  0.6 0.8 copy.58
  1.4 0.1 eq.50
  1.5 0.1 eq.46
  1.7 1.2 reduce-window.6
  2.9 0.2 slice_reduce_fusion
  3.1 0.1 fusion.20
  3.3 0.1 reduce_sum.39
  3.4 0.1 copy.61
  3.4 0.7 multiply_add_fusion
  4.1 0.4 fusion.4
  4.5 1.0 select_reduce_fusion
  5.5 1.1 copy.66.prob_ref
  6.6 0.2 copy.64
  6.9 0.8 copy.65.sel_ref
  7.7 1.9 pad_maximum_fusion.1.both_ref
  9.6 4.9 %shard_map.101 = bf16[1024,2048]{1,0:T(8,128)(2,1)} custom-call(bf16[1024,128]{1,0:T(8,128)(2,1)} %copy.65.sel_ref, bf16[128,2048]{1,0:T(8,128)(2,1)} %pad_maximum_fusion.1.both_ref, f32[1024,1]{1,0:T(8,128)} %copy.66.prob_ref), custom_call_target="tpu_custom_call" | custom-call | tf_op jit(solution)/shard_map/pallas_call | solution.py:102
  14.5 11.0 %all-to-all-start = ((bf16[64,16,2048]{2,1,0:T(8,128)(2,1)}), bf16[64,16,2048]{2,1,0:T(8,128)(2,1)}, u32[]{:S(2)}, u32[]{:S(2)}) async-start(bf16[64,16,2048]{2,1,0:T(8,128)(2,1)} %bitcast.82), calls=%async_computation | async-start | bytes 8388608 | tf_op jit(solution)/shard_map/all_to_all | solution.py:167
  25.5 0.1 copy.67
  25.7 10.9 %collective-permute-start = (bf16[128,1152]{1,0:T(8,128)(2,1)S(1)}, bf16[128,1152]{1,0:T(8,128)(2,1)S(1)}, u32[]{:S(2)}, u32[]{:S(2)}) collective-permute-start(bf16[128,1152]{1,0:T(8,128)(2,1)S(1)} %pad_maximum_fusion.2), channel_id=1, source_target_pairs={{0,448},{64,0},{128,64},{192,128},{256,192},{320,256},{384,320},{4... | collective-permute-start | bytes 884744 | tf_op jit(solution)/shard_map/ppermute | solution.py:121
  36.5 2.5 %collective-permute-start.1 = (bf16[128,1152]{1,0:T(8,128)(2,1)S(1)}, bf16[128,1152]{1,0:T(8,128)(2,1)S(1)}, u32[]{:S(2)}, u32[]{:S(2)}) collective-permute-start(bf16[128,1152]{1,0:T(8,128)(2,1)S(1)} %pad_maximum_fusion.2), channel_id=1, source_target_pairs={{0,384},{64,448},{128,0},{192,64},{256,128},{320,192},{384,256},{4... | collective-permute-start | bytes 884744 | tf_op jit(solution)/shard_map/ppermute | solution.py:121
  39.0 1.9 collective-permute-start.2
  40.9 7.8 %collective-permute-start.3 = (bf16[128,1152]{1,0:T(8,128)(2,1)S(1)}, bf16[128,1152]{1,0:T(8,128)(2,1)S(1)}, u32[]{:S(2)}, u32[]{:S(2)}) collective-permute-start(bf16[128,1152]{1,0:T(8,128)(2,1)S(1)} %pad_maximum_fusion.2), channel_id=1, source_target_pairs={{0,256},{64,320},{128,384},{192,448},{256,0},{320,64},{384,128},{4... | collective-permute-start | bytes 884744 | tf_op jit(solution)/shard_map/ppermute | solution.py:121
  48.8 1.9 collective-permute-start.4
  50.7 0.0 collective-permute-done
  50.7 3.4 %collective-permute-start.5 = (bf16[128,1152]{1,0:T(8,128)(2,1)S(1)}, bf16[128,1152]{1,0:T(8,128)(2,1)S(1)}, u32[]{:S(2)}, u32[]{:S(2)}) collective-permute-start(bf16[128,1152]{1,0:T(8,128)(2,1)S(1)} %pad_maximum_fusion.2), channel_id=1, source_target_pairs={{0,128},{64,192},{128,256},{192,320},{256,384},{320,448},{384,0},{... | collective-permute-start | bytes 884744 | tf_op jit(solution)/shard_map/ppermute | solution.py:121
  54.1 5.6 %collective-permute-done.1 = bf16[128,1152]{1,0:T(8,128)(2,1)S(1)} collective-permute-done((bf16[128,1152]{1,0:T(8,128)(2,1)S(1)}, bf16[128,1152]{1,0:T(8,128)(2,1)S(1)}, u32[]{:S(2)}, u32[]{:S(2)}) %collective-permute-start.1) | collective-permute-done | bytes 294944 | tf_op jit(solution)/shard_map/ppermute | solution.py:121
  59.7 1.9 collective-permute-start.6
  61.7 25.6 %collective-permute-done.2 = bf16[128,1152]{1,0:T(8,128)(2,1)S(1)} collective-permute-done((bf16[128,1152]{1,0:T(8,128)(2,1)S(1)}, bf16[128,1152]{1,0:T(8,128)(2,1)S(1)}, u32[]{:S(2)}, u32[]{:S(2)}) %collective-permute-start.2) | collective-permute-done | bytes 294944 | tf_op jit(solution)/shard_map/ppermute | solution.py:121
  87.4 0.7 collective-permute-done.4
  88.1 4.6 %collective-permute-done.5 = bf16[128,1152]{1,0:T(8,128)(2,1)S(1)} collective-permute-done((bf16[128,1152]{1,0:T(8,128)(2,1)S(1)}, bf16[128,1152]{1,0:T(8,128)(2,1)S(1)}, u32[]{:S(2)}, u32[]{:S(2)}) %collective-permute-start.5) | collective-permute-done | bytes 294944 | tf_op jit(solution)/shard_map/ppermute | solution.py:121
  92.8 7.0 %collective-permute-done.6 = bf16[128,1152]{1,0:T(8,128)(2,1)S(1)} collective-permute-done((bf16[128,1152]{1,0:T(8,128)(2,1)S(1)}, bf16[128,1152]{1,0:T(8,128)(2,1)S(1)}, u32[]{:S(2)}, u32[]{:S(2)}) %collective-permute-start.6) | collective-permute-done | bytes 294944 | tf_op jit(solution)/shard_map/ppermute | solution.py:121
  100.1 1.7 constant_dynamic-slice_fusion
  101.8 19.9 %all-to-all-done = bf16[64,16,2048]{2,1,0:T(8,128)(2,1)} async-done(((bf16[64,16,2048]{2,1,0:T(8,128)(2,1)}), bf16[64,16,2048]{2,1,0:T(8,128)(2,1)}, u32[]{:S(2)}, u32[]{:S(2)}) %all-to-all-start) | async-done | bytes 4194336 | tf_op jit(solution)/shard_map/all_to_all | solution.py:167
  121.7 9.5 %shard_map.102 = (bf16[1024,2048]{1,0:T(8,128)(2,1)}, bf16[1024,384]{1,0:T(8,128)(2,1)}, bf16[1024,768]{1,0:T(8,128)(2,1)}) custom-call(bf16[1024,2048]{1,0:T(8,128)(2,1)} %bitcast.4.recv_ref, bf16[1024,1152]{1,0:T(8,128)(2,1)} %bitcast.83), custom_call_target="tpu_custom_call" | custom-call | tf_op jit(solution)/shard_map/pallas_call | solution.py:43
  131.2 5.8 %all-to-all-start.1 = ((bf16[64,16,2048]{2,1,0:T(8,128)(2,1)}), bf16[64,16,2048]{2,1,0:T(8,128)(2,1)}, u32[]{:S(2)}, u32[]{:S(2)}) async-start(bf16[64,16,2048]{2,1,0:T(8,128)(2,1)} %bitcast.86), calls=%async_computation.1 | async-start | bytes 8388608 | tf_op jit(solution)/shard_map/all_to_all | solution.py:169
  137.1 2.7 %fusion.8 = bf16[1024,384]{0,1:T(8,128)(2,1)S(1)} fusion(bf16[1024,384]{1,0:T(8,128)(2,1)S(1)} %copy-done.3, bf16[1024,2048]{1,0:T(8,128)(2,1)} %bitcast.4.recv_ref), kind=kOutput, calls=%fused_computation.11 | convolution fusion | flops 805699584 | bytes 3670016 | tf_op jit(solution)/shard_map/dot_general | solution.py:174
  139.8 3.4 %fusion.5 = bf16[1024,768]{0,1:T(8,128)(2,1)S(1)} fusion(bf16[1024,768]{1,0:T(8,128)(2,1)S(1)} %copy-done.2, bf16[1024,2048]{1,0:T(8,128)(2,1)} %bitcast.4.recv_ref), kind=kOutput, calls=%fused_computation.10 | convolution fusion | flops 1611399168 | bytes 5242880 | tf_op jit(solution)/shard_map/dot_general | solution.py:171
  143.3 1.7 pad_maximum_fusion
  145.0 3.0 %copy.78 = bf16[1024,1152]{1,0:T(8,128)(2,1)S(1)} copy(bf16[1024,1152]{0,1:T(8,128)(2,1)} %pad_maximum_fusion) | data formatting | bytes 4718592 | tf_op jit(solution)/shard_map/reshape | solution.py:132
  148.0 1.2 dynamic-slice_bitcast_fusion.6
  149.2 10.7 %collective-permute-start.10 = (bf16[128,1152]{1,0:T(8,128)(2,1)}, bf16[128,1152]{1,0:T(8,128)(2,1)}, u32[]{:S(2)}, u32[]{:S(2)}) collective-permute-start(bf16[128,1152]{1,0:T(8,128)(2,1)} %get-tuple-element.38), channel_id=1, source_target_pairs={{0,256},{64,320},{128,384},{192,448},{256,0},{320,64},{384,128},{4... | collective-permute-start | bytes 884744 | tf_op jit(solution)/shard_map/ppermute | solution.py:137
  160.0 1.9 collective-permute-start.11
  161.9 1.0 copy.62
  162.9 7.8 %collective-permute-start.12 = (bf16[128,1152]{1,0:T(8,128)(2,1)}, bf16[128,1152]{1,0:T(8,128)(2,1)S(1)}, u32[]{:S(2)}, u32[]{:S(2)}) collective-permute-start(bf16[128,1152]{1,0:T(8,128)(2,1)} %get-tuple-element.36), channel_id=1, source_target_pairs={{0,384},{64,448},{128,0},{192,64},{256,128},{320,192},{384,256},{4... | collective-permute-start | bytes 884744 | tf_op jit(solution)/shard_map/ppermute | solution.py:137
  170.8 2.5 %collective-permute-start.13 = (bf16[128,1152]{1,0:T(8,128)(2,1)}, bf16[128,1152]{1,0:T(8,128)(2,1)S(1)}, u32[]{:S(2)}, u32[]{:S(2)}) collective-permute-start(bf16[128,1152]{1,0:T(8,128)(2,1)} %get-tuple-element.35), channel_id=1, source_target_pairs={{0,448},{64,0},{128,64},{192,128},{256,192},{320,256},{384,320},{4... | collective-permute-start | bytes 884744 | tf_op jit(solution)/shard_map/ppermute | solution.py:137
  173.2 3.4 %collective-permute-start.7 = (bf16[128,1152]{1,0:T(8,128)(2,1)}, bf16[128,1152]{1,0:T(8,128)(2,1)S(1)}, u32[]{:S(2)}, u32[]{:S(2)}) collective-permute-start(bf16[128,1152]{1,0:T(8,128)(2,1)} %get-tuple-element.34), channel_id=1, source_target_pairs={{0,64},{64,128},{128,192},{192,256},{256,320},{320,384},{384,448},... | collective-permute-start | bytes 884744 | tf_op jit(solution)/shard_map/ppermute | solution.py:137
  176.6 0.0 collective-permute-done.10
  176.6 1.9 collective-permute-start.8
  178.6 16.4 %collective-permute-done.11 = bf16[128,1152]{1,0:T(8,128)(2,1)} collective-permute-done((bf16[128,1152]{1,0:T(8,128)(2,1)}, bf16[128,1152]{1,0:T(8,128)(2,1)}, u32[]{:S(2)}, u32[]{:S(2)}) %collective-permute-start.11) | collective-permute-done | bytes 294944 | tf_op jit(solution)/shard_map/ppermute | solution.py:137
  195.0 7.1 %collective-permute-start.9 = (bf16[128,1152]{1,0:T(8,128)(2,1)S(1)}, bf16[128,1152]{1,0:T(8,128)(2,1)S(1)}, u32[]{:S(2)}, u32[]{:S(2)}) collective-permute-start(bf16[128,1152]{1,0:T(8,128)(2,1)S(1)} %get-tuple-element.39), channel_id=1, source_target_pairs={{0,192},{64,256},{128,320},{192,384},{256,448},{320,0},{384,64},{4... | collective-permute-start | bytes 884744 | tf_op jit(solution)/shard_map/ppermute | solution.py:137
  202.1 1.2 reduce-precision_convert_fusion.1
  203.3 1.1 maximum_bitcast_fusion.comb_ref
  204.4 1.6 collective-permute-done.12
  206.1 6.9 %collective-permute-done.13 = bf16[128,1152]{1,0:T(8,128)(2,1)S(1)} collective-permute-done((bf16[128,1152]{1,0:T(8,128)(2,1)}, bf16[128,1152]{1,0:T(8,128)(2,1)S(1)}, u32[]{:S(2)}, u32[]{:S(2)}) %collective-permute-start.13) | collective-permute-done | bytes 294944 | tf_op jit(solution)/shard_map/ppermute | solution.py:137
  212.9 0.0 collective-permute-done.7
  212.9 0.0 collective-permute-done.8
  212.9 7.7 %collective-permute-done.9 = bf16[128,1152]{1,0:T(8,128)(2,1)S(1)} collective-permute-done((bf16[128,1152]{1,0:T(8,128)(2,1)S(1)}, bf16[128,1152]{1,0:T(8,128)(2,1)S(1)}, u32[]{:S(2)}, u32[]{:S(2)}) %collective-permute-start.9) | collective-permute-done | bytes 294944 | tf_op jit(solution)/shard_map/ppermute | solution.py:137
  220.7 1.3 fusion.16
  222.1 0.8 copy.77
  222.9 0.8 slice_bitcast_fusion
  223.6 9.6 %all-to-all-done.1 = bf16[64,16,2048]{2,1,0:T(8,128)(2,1)} async-done(((bf16[64,16,2048]{2,1,0:T(8,128)(2,1)}), bf16[64,16,2048]{2,1,0:T(8,128)(2,1)}, u32[]{:S(2)}, u32[]{:S(2)}) %all-to-all-start.1) | async-done | bytes 4194336 | tf_op jit(solution)/shard_map/all_to_all | solution.py:169
  233.2 5.2 %shard_map.103 = (bf16[128,1024]{1,0:T(8,128)(2,1)}, bf16[128,1024]{1,0:T(8,128)(2,1)}, f32[128,1024]{1,0:T(8,128)}) custom-call(bf16[512,1024]{1,0:T(8,128)(2,1)} %maximum_bitcast_fusion.comb_ref, bf16[1024,2048]{1,0:T(8,128)(2,1)} %bitcast.18.back_ref, bf16[128,1024]{1,0:T(8,128)(2,1)} %cot_ref.1), custom_call_target="tpu_custom_call" | custom-call | tf_op jit(solution)/shard_map/pallas_call | solution.py:82
  238.4 1.2 copy.68
  239.7 0.8 select_reduce_fusion.2
  (31 shorter events, 0.6 us)
Async XLA Ops:
  14.5 11.0 %copy-start.1 = (bf16[1,384,128]{2,1,0:T(8,128)(2,1)S(1)}, bf16[1,384,128]{2,1,0:T(8,128)(2,1)}, u32[]{:S(2)}) copy-start(bf16[1,384,128]{2,1,0:T(8,128)(2,1)} %param.10) | copy-start | bytes 294916
  14.5 11.2 %copy-start = (bf16[1,128,768]{2,1,0:T(8,128)(2,1)S(1)}, bf16[1,128,768]{2,1,0:T(8,128)(2,1)}, u32[]{:S(2)}) copy-start(bf16[1,128,768]{2,1,0:T(8,128)(2,1)} %param.9) | copy-start | bytes 589828
  14.5 107.2 %all-to-all-start = ((bf16[64,16,2048]{2,1,0:T(8,128)(2,1)}), bf16[64,16,2048]{2,1,0:T(8,128)(2,1)}, u32[]{:S(2)}, u32[]{:S(2)}) async-start(bf16[64,16,2048]{2,1,0:T(8,128)(2,1)} %bitcast.82), calls=%async_computation | async-start | bytes 8388608 | tf_op jit(solution)/shard_map/all_to_all | solution.py:167
  25.7 25.0 %collective-permute-start = (bf16[128,1152]{1,0:T(8,128)(2,1)S(1)}, bf16[128,1152]{1,0:T(8,128)(2,1)S(1)}, u32[]{:S(2)}, u32[]{:S(2)}) collective-permute-start(bf16[128,1152]{1,0:T(8,128)(2,1)S(1)} %pad_maximum_fusion.2), channel_id=1, source_target_pairs={{0,448},{64,0},{128,64},{192,128},{256,192},{320,256},{384,320},{4... | collective-permute-start | bytes 884744 | tf_op jit(solution)/shard_map/ppermute | solution.py:121
  36.5 23.2 %collective-permute-start.1 = (bf16[128,1152]{1,0:T(8,128)(2,1)S(1)}, bf16[128,1152]{1,0:T(8,128)(2,1)S(1)}, u32[]{:S(2)}, u32[]{:S(2)}) collective-permute-start(bf16[128,1152]{1,0:T(8,128)(2,1)S(1)} %pad_maximum_fusion.2), channel_id=1, source_target_pairs={{0,384},{64,448},{128,0},{192,64},{256,128},{320,192},{384,256},{4... | collective-permute-start | bytes 884744 | tf_op jit(solution)/shard_map/ppermute | solution.py:121
  39.0 48.3 %collective-permute-start.2 = (bf16[128,1152]{1,0:T(8,128)(2,1)S(1)}, bf16[128,1152]{1,0:T(8,128)(2,1)S(1)}, u32[]{:S(2)}, u32[]{:S(2)}) collective-permute-start(bf16[128,1152]{1,0:T(8,128)(2,1)S(1)} %pad_maximum_fusion.2), channel_id=1, source_target_pairs={{0,320},{64,384},{128,448},{192,0},{256,64},{320,128},{384,192},{4... | collective-permute-start | bytes 884744 | tf_op jit(solution)/shard_map/ppermute | solution.py:121
  40.9 46.4 %collective-permute-start.3 = (bf16[128,1152]{1,0:T(8,128)(2,1)S(1)}, bf16[128,1152]{1,0:T(8,128)(2,1)S(1)}, u32[]{:S(2)}, u32[]{:S(2)}) collective-permute-start(bf16[128,1152]{1,0:T(8,128)(2,1)S(1)} %pad_maximum_fusion.2), channel_id=1, source_target_pairs={{0,256},{64,320},{128,384},{192,448},{256,0},{320,64},{384,128},{4... | collective-permute-start | bytes 884744 | tf_op jit(solution)/shard_map/ppermute | solution.py:121
  48.8 39.3 %collective-permute-start.4 = (bf16[128,1152]{1,0:T(8,128)(2,1)S(1)}, bf16[128,1152]{1,0:T(8,128)(2,1)S(1)}, u32[]{:S(2)}, u32[]{:S(2)}) collective-permute-start(bf16[128,1152]{1,0:T(8,128)(2,1)S(1)} %pad_maximum_fusion.2), channel_id=1, source_target_pairs={{0,192},{64,256},{128,320},{192,384},{256,448},{320,0},{384,64},{4... | collective-permute-start | bytes 884744 | tf_op jit(solution)/shard_map/ppermute | solution.py:121
  50.7 42.0 %collective-permute-start.5 = (bf16[128,1152]{1,0:T(8,128)(2,1)S(1)}, bf16[128,1152]{1,0:T(8,128)(2,1)S(1)}, u32[]{:S(2)}, u32[]{:S(2)}) collective-permute-start(bf16[128,1152]{1,0:T(8,128)(2,1)S(1)} %pad_maximum_fusion.2), channel_id=1, source_target_pairs={{0,128},{64,192},{128,256},{192,320},{256,384},{320,448},{384,0},{... | collective-permute-start | bytes 884744 | tf_op jit(solution)/shard_map/ppermute | solution.py:121
  59.7 40.0 %collective-permute-start.6 = (bf16[128,1152]{1,0:T(8,128)(2,1)S(1)}, bf16[128,1152]{1,0:T(8,128)(2,1)S(1)}, u32[]{:S(2)}, u32[]{:S(2)}) collective-permute-start(bf16[128,1152]{1,0:T(8,128)(2,1)S(1)} %pad_maximum_fusion.2), channel_id=1, source_target_pairs={{0,64},{64,128},{128,192},{192,256},{256,320},{320,384},{384,448},... | collective-permute-start | bytes 884744 | tf_op jit(solution)/shard_map/ppermute | solution.py:121
  131.2 6.0 %copy-start.3 = (bf16[1024,384]{1,0:T(8,128)(2,1)S(1)}, bf16[1024,384]{1,0:T(8,128)(2,1)}, u32[]{:S(2)}) copy-start(bf16[1024,384]{1,0:T(8,128)(2,1)} %get-tuple-element.16) | copy-start | bytes 2359300
  131.2 102.0 %all-to-all-start.1 = ((bf16[64,16,2048]{2,1,0:T(8,128)(2,1)}), bf16[64,16,2048]{2,1,0:T(8,128)(2,1)}, u32[]{:S(2)}, u32[]{:S(2)}) async-start(bf16[64,16,2048]{2,1,0:T(8,128)(2,1)} %bitcast.86), calls=%async_computation.1 | async-start | bytes 8388608 | tf_op jit(solution)/shard_map/all_to_all | solution.py:169
  137.0 2.8 %copy-start.2 = (bf16[1024,768]{1,0:T(8,128)(2,1)S(1)}, bf16[1024,768]{1,0:T(8,128)(2,1)}, u32[]{:S(2)}) copy-start(bf16[1024,768]{1,0:T(8,128)(2,1)} %get-tuple-element.15) | copy-start | bytes 4718596
  149.2 27.4 %collective-permute-start.10 = (bf16[128,1152]{1,0:T(8,128)(2,1)}, bf16[128,1152]{1,0:T(8,128)(2,1)}, u32[]{:S(2)}, u32[]{:S(2)}) collective-permute-start(bf16[128,1152]{1,0:T(8,128)(2,1)} %get-tuple-element.38), channel_id=1, source_target_pairs={{0,256},{64,320},{128,384},{192,448},{256,0},{320,64},{384,128},{4... | collective-permute-start | bytes 884744 | tf_op jit(solution)/shard_map/ppermute | solution.py:137
  160.0 35.1 %collective-permute-start.11 = (bf16[128,1152]{1,0:T(8,128)(2,1)}, bf16[128,1152]{1,0:T(8,128)(2,1)}, u32[]{:S(2)}, u32[]{:S(2)}) collective-permute-start(bf16[128,1152]{1,0:T(8,128)(2,1)} %get-tuple-element.37), channel_id=1, source_target_pairs={{0,320},{64,384},{128,448},{192,0},{256,64},{320,128},{384,192},{4... | collective-permute-start | bytes 884744 | tf_op jit(solution)/shard_map/ppermute | solution.py:137
  162.9 43.1 %collective-permute-start.12 = (bf16[128,1152]{1,0:T(8,128)(2,1)}, bf16[128,1152]{1,0:T(8,128)(2,1)S(1)}, u32[]{:S(2)}, u32[]{:S(2)}) collective-permute-start(bf16[128,1152]{1,0:T(8,128)(2,1)} %get-tuple-element.36), channel_id=1, source_target_pairs={{0,384},{64,448},{128,0},{192,64},{256,128},{320,192},{384,256},{4... | collective-permute-start | bytes 884744 | tf_op jit(solution)/shard_map/ppermute | solution.py:137
  170.8 42.2 %collective-permute-start.13 = (bf16[128,1152]{1,0:T(8,128)(2,1)}, bf16[128,1152]{1,0:T(8,128)(2,1)S(1)}, u32[]{:S(2)}, u32[]{:S(2)}) collective-permute-start(bf16[128,1152]{1,0:T(8,128)(2,1)} %get-tuple-element.35), channel_id=1, source_target_pairs={{0,448},{64,0},{128,64},{192,128},{256,192},{320,256},{384,320},{4... | collective-permute-start | bytes 884744 | tf_op jit(solution)/shard_map/ppermute | solution.py:137
  173.2 39.7 %collective-permute-start.7 = (bf16[128,1152]{1,0:T(8,128)(2,1)}, bf16[128,1152]{1,0:T(8,128)(2,1)S(1)}, u32[]{:S(2)}, u32[]{:S(2)}) collective-permute-start(bf16[128,1152]{1,0:T(8,128)(2,1)} %get-tuple-element.34), channel_id=1, source_target_pairs={{0,64},{64,128},{128,192},{192,256},{256,320},{320,384},{384,448},... | collective-permute-start | bytes 884744 | tf_op jit(solution)/shard_map/ppermute | solution.py:137
  176.6 36.3 %collective-permute-start.8 = (bf16[128,1152]{1,0:T(8,128)(2,1)}, bf16[128,1152]{1,0:T(8,128)(2,1)S(1)}, u32[]{:S(2)}, u32[]{:S(2)}) collective-permute-start(bf16[128,1152]{1,0:T(8,128)(2,1)} %get-tuple-element.40), channel_id=1, source_target_pairs={{0,128},{64,192},{128,256},{192,320},{256,384},{320,448},{384,0},{... | collective-permute-start | bytes 884744 | tf_op jit(solution)/shard_map/ppermute | solution.py:137
  195.0 25.7 %collective-permute-start.9 = (bf16[128,1152]{1,0:T(8,128)(2,1)S(1)}, bf16[128,1152]{1,0:T(8,128)(2,1)S(1)}, u32[]{:S(2)}, u32[]{:S(2)}) collective-permute-start(bf16[128,1152]{1,0:T(8,128)(2,1)S(1)} %get-tuple-element.39), channel_id=1, source_target_pairs={{0,192},{64,256},{128,320},{192,384},{256,448},{320,0},{384,64},{4... | collective-permute-start | bytes 884744 | tf_op jit(solution)/shard_map/ppermute | solution.py:137

commit v9 on v7

--- a/solution.py
+++ b/solution.py
@@ -33,7 +33,7 @@
     dp_ref[...] = dp
 
 
-def expert_call(recv, weights, gate_width, block=256):
+def expert_call(recv, weights, gate_width, block=512):
     slots, both = recv.shape
     width = both // 2
     hidden_width = weights.shape[1] - gate_width

time: 237 us -> 237 us (level)
  no operation moved by 1% of the time
where the time goes in v9:
time: 237 us; the launch traced here: 236 us
  waiting for transfers between devices  106 us (45%)
  starting transfers between devices  82.5 us (35%)
  Pallas kernels  14.7 us (6%)
  local copies, waits for them, and re-layouts  11.2 us (5%)
  matrix products  10.5 us (4%)
  other arithmetic  10.3 us (4%)
    ppermute x7, waiting for transfers between devices, gather_dp(): pieces.append(lax.ppermute(block, 'dp', pairs))  43.5 us
    ppermute x7, starting transfers between devices, scatter_dp(): total = total + lax.ppermute(part, 'dp', pairs).astype(jnp.float32)  35.4 us
    ppermute x7, waiting for transfers between devices, scatter_dp(): total = total + lax.ppermute(part, 'dp', pairs).astype(jnp.float32)  32.9 us
    ppermute x7, starting transfers between devices, gather_dp(): pieces.append(lax.ppermute(block, 'dp', pairs))  30.3 us
    all_to_all x1, waiting for transfers between devices, local(): lax.all_to_all(send, 'expert', split_axis=0, concat_axis=0, tiled=True)  20 us
    all_to_all x1, starting transfers between devices, local(): lax.all_to_all(send, 'expert', split_axis=0, concat_axis=0, tiled=True)  11 us
    pallas_call x1, Pallas kernels, expert_call(): pl.pallas_call(kernel, grid=(slots // block,), in_specs=[pl.BlockSpec((bl...  9.51 us
    all_to_all x1, waiting for transfers between devices, local(): lax.all_to_all(payload, 'expert', split_axis=0, concat_axis=0, tiled=True)  9.23 us
  transfers between devices with their start and end apart: 16, of which 11 were waited for; matrix products, arithmetic and copies ran while one was open for 9% of the time, Pallas kernels for 0%

profile of v9, /device:TPU:6, one launch (start us, length us, event | category | flops | bytes accessed | tf_op | source)
XLA Modules:
  0.0 235.9 jit_solution(16330449180032400231)
XLA Ops:
  0.6 0.8 copy.53
  1.4 0.1 eq.50
  1.5 0.1 eq.46
  1.7 1.2 reduce-window.6
  2.9 0.2 slice_reduce_fusion
  3.1 0.1 fusion.23
  3.3 0.1 reduce_sum.39
  3.4 0.1 copy.56
  3.5 0.7 multiply_add_fusion
  4.2 0.4 fusion.4
  4.5 1.0 select_reduce_fusion
  5.5 4.3 %multiply_convert_fusion = bf16[1024,2048]{1,0:T(8,128)(2,1)} fusion(pred[1024,128]{1,0:T(8,128)(4,1)S(1)} %fusion.4, f32[1024]{0:T(1024)S(1)} %get-tuple-element.32, pred[2048]{0:T(1024)(128)(4,1)S(1)} %iota_compare_fusion.3, bf16[128,1024]{1,0:T(8,128)(2,1)} %cot_ref.1, bf16[128,1024]{1,0:T(8,128)(2,1)} %param.6), kind=kOutput, calls=%fused_computation | convolution fusion | flops 544210944 | bytes 4855808 | tf_op jit(solution)/shard_map/dot_general | solution.py:143
  9.9 11.0 %all-to-all-start = ((bf16[64,16,2048]{2,1,0:T(8,128)(2,1)}), bf16[64,16,2048]{2,1,0:T(8,128)(2,1)}, u32[]{:S(2)}, u32[]{:S(2)}) async-start(bf16[64,16,2048]{2,1,0:T(8,128)(2,1)} %bitcast.86), calls=%async_computation | async-start | bytes 8388608 | tf_op jit(solution)/shard_map/all_to_all | solution.py:147
  20.9 0.1 copy.60
  21.0 0.0 copy-done
  21.1 10.9 %collective-permute-start = (bf16[128,1152]{1,0:T(8,128)(2,1)S(1)}, bf16[128,1152]{1,0:T(8,128)(2,1)S(1)}, u32[]{:S(2)}, u32[]{:S(2)}) collective-permute-start(bf16[128,1152]{1,0:T(8,128)(2,1)S(1)} %pad_maximum_fusion.1), channel_id=1, source_target_pairs={{0,448},{64,0},{128,64},{192,128},{256,192},{320,256},{384,320},{4... | collective-permute-start | bytes 884744 | tf_op jit(solution)/shard_map/ppermute | solution.py:98
  31.9 2.5 %collective-permute-start.1 = (bf16[128,1152]{1,0:T(8,128)(2,1)S(1)}, bf16[128,1152]{1,0:T(8,128)(2,1)S(1)}, u32[]{:S(2)}, u32[]{:S(2)}) collective-permute-start(bf16[128,1152]{1,0:T(8,128)(2,1)S(1)} %pad_maximum_fusion.1), channel_id=1, source_target_pairs={{0,384},{64,448},{128,0},{192,64},{256,128},{320,192},{384,256},{4... | collective-permute-start | bytes 884744 | tf_op jit(solution)/shard_map/ppermute | solution.py:98
  34.4 1.9 collective-permute-start.2
  36.3 7.8 %collective-permute-start.3 = (bf16[128,1152]{1,0:T(8,128)(2,1)S(1)}, bf16[128,1152]{1,0:T(8,128)(2,1)S(1)}, u32[]{:S(2)}, u32[]{:S(2)}) collective-permute-start(bf16[128,1152]{1,0:T(8,128)(2,1)S(1)} %pad_maximum_fusion.1), channel_id=1, source_target_pairs={{0,256},{64,320},{128,384},{192,448},{256,0},{320,64},{384,128},{4... | collective-permute-start | bytes 884744 | tf_op jit(solution)/shard_map/ppermute | solution.py:98
  44.2 1.9 collective-permute-start.4
  46.1 0.0 collective-permute-done
  46.1 3.4 %collective-permute-start.5 = (bf16[128,1152]{1,0:T(8,128)(2,1)S(1)}, bf16[128,1152]{1,0:T(8,128)(2,1)S(1)}, u32[]{:S(2)}, u32[]{:S(2)}) collective-permute-start(bf16[128,1152]{1,0:T(8,128)(2,1)S(1)} %pad_maximum_fusion.1), channel_id=1, source_target_pairs={{0,128},{64,192},{128,256},{192,320},{256,384},{320,448},{384,0},{... | collective-permute-start | bytes 884744 | tf_op jit(solution)/shard_map/ppermute | solution.py:98
  49.5 5.6 %collective-permute-done.1 = bf16[128,1152]{1,0:T(8,128)(2,1)S(1)} collective-permute-done((bf16[128,1152]{1,0:T(8,128)(2,1)S(1)}, bf16[128,1152]{1,0:T(8,128)(2,1)S(1)}, u32[]{:S(2)}, u32[]{:S(2)}) %collective-permute-start.1) | collective-permute-done | bytes 294944 | tf_op jit(solution)/shard_map/ppermute | solution.py:98
  55.1 1.9 collective-permute-start.6
  57.1 25.6 %collective-permute-done.2 = bf16[128,1152]{1,0:T(8,128)(2,1)S(1)} collective-permute-done((bf16[128,1152]{1,0:T(8,128)(2,1)S(1)}, bf16[128,1152]{1,0:T(8,128)(2,1)S(1)}, u32[]{:S(2)}, u32[]{:S(2)}) %collective-permute-start.2) | collective-permute-done | bytes 294944 | tf_op jit(solution)/shard_map/ppermute | solution.py:98
  82.7 0.0 collective-permute-done.3
  82.8 0.7 collective-permute-done.4
  83.5 4.6 %collective-permute-done.5 = bf16[128,1152]{1,0:T(8,128)(2,1)S(1)} collective-permute-done((bf16[128,1152]{1,0:T(8,128)(2,1)S(1)}, bf16[128,1152]{1,0:T(8,128)(2,1)S(1)}, u32[]{:S(2)}, u32[]{:S(2)}) %collective-permute-start.5) | collective-permute-done | bytes 294944 | tf_op jit(solution)/shard_map/ppermute | solution.py:98
  88.1 7.0 %collective-permute-done.6 = bf16[128,1152]{1,0:T(8,128)(2,1)S(1)} collective-permute-done((bf16[128,1152]{1,0:T(8,128)(2,1)S(1)}, bf16[128,1152]{1,0:T(8,128)(2,1)S(1)}, u32[]{:S(2)}, u32[]{:S(2)}) %collective-permute-start.6) | collective-permute-done | bytes 294944 | tf_op jit(solution)/shard_map/ppermute | solution.py:98
  95.5 1.6 constant_dynamic-slice_fusion
  97.1 20.0 %all-to-all-done = bf16[64,16,2048]{2,1,0:T(8,128)(2,1)} async-done(((bf16[64,16,2048]{2,1,0:T(8,128)(2,1)}), bf16[64,16,2048]{2,1,0:T(8,128)(2,1)}, u32[]{:S(2)}, u32[]{:S(2)}) %all-to-all-start) | async-done | bytes 4194336 | tf_op jit(solution)/shard_map/all_to_all | solution.py:147
  117.1 9.5 %shard_map.101 = (bf16[1024,2048]{1,0:T(8,128)(2,1)}, bf16[1024,384]{1,0:T(8,128)(2,1)}, bf16[1024,768]{1,0:T(8,128)(2,1)}) custom-call(bf16[1024,2048]{1,0:T(8,128)(2,1)} %bitcast.3.recv_ref, bf16[1024,1152]{1,0:T(8,128)(2,1)} %bitcast.82), custom_call_target="tpu_custom_call" | custom-call | tf_op jit(solution)/shard_map/pallas_call | solution.py:43
  126.6 5.8 %all-to-all-start.1 = ((bf16[64,16,2048]{2,1,0:T(8,128)(2,1)}), bf16[64,16,2048]{2,1,0:T(8,128)(2,1)}, u32[]{:S(2)}, u32[]{:S(2)}) async-start(bf16[64,16,2048]{2,1,0:T(8,128)(2,1)} %bitcast.85), calls=%async_computation.1 | async-start | bytes 8388608 | tf_op jit(solution)/shard_map/all_to_all | solution.py:149
  132.6 2.7 %fusion.8 = bf16[1024,384]{0,1:T(8,128)(2,1)S(1)} fusion(bf16[1024,384]{1,0:T(8,128)(2,1)S(1)} %copy-done.3, bf16[1024,2048]{1,0:T(8,128)(2,1)} %bitcast.3.recv_ref), kind=kOutput, calls=%fused_computation.12 | convolution fusion | flops 805699584 | bytes 3670016 | tf_op jit(solution)/shard_map/dot_general | solution.py:154
  135.3 3.4 %fusion.5 = bf16[1024,768]{0,1:T(8,128)(2,1)S(1)} fusion(bf16[1024,768]{1,0:T(8,128)(2,1)S(1)} %copy-done.2, bf16[1024,2048]{1,0:T(8,128)(2,1)} %bitcast.3.recv_ref), kind=kOutput, calls=%fused_computation.11 | convolution fusion | flops 1611399168 | bytes 5242880 | tf_op jit(solution)/shard_map/dot_general | solution.py:151
  138.7 1.7 pad_maximum_fusion
  140.4 3.0 %copy.71 = bf16[1024,1152]{1,0:T(8,128)(2,1)S(1)} copy(bf16[1024,1152]{0,1:T(8,128)(2,1)} %pad_maximum_fusion) | data formatting | bytes 4718592 | tf_op jit(solution)/shard_map/reshape | solution.py:109
  143.4 1.3 dynamic-slice_bitcast_fusion.6
  144.8 10.7 %collective-permute-start.10 = (bf16[128,1152]{1,0:T(8,128)(2,1)}, bf16[128,1152]{1,0:T(8,128)(2,1)}, u32[]{:S(2)}, u32[]{:S(2)}) collective-permute-start(bf16[128,1152]{1,0:T(8,128)(2,1)} %get-tuple-element.38), channel_id=1, source_target_pairs={{0,256},{64,320},{128,384},{192,448},{256,0},{320,64},{384,128},{4... | collective-permute-start | bytes 884744 | tf_op jit(solution)/shard_map/ppermute | solution.py:114
  155.5 1.9 collective-permute-start.11
  157.5 0.2 copy.59
  157.7 0.2 copy.57
  157.9 0.7 convert_element_type.60
  158.6 7.8 %collective-permute-start.12 = (bf16[128,1152]{1,0:T(8,128)(2,1)}, bf16[128,1152]{1,0:T(8,128)(2,1)S(1)}, u32[]{:S(2)}, u32[]{:S(2)}) collective-permute-start(bf16[128,1152]{1,0:T(8,128)(2,1)} %get-tuple-element.36), channel_id=1, source_target_pairs={{0,384},{64,448},{128,0},{192,64},{256,128},{320,192},{384,256},{4... | collective-permute-start | bytes 884744 | tf_op jit(solution)/shard_map/ppermute | solution.py:114
  166.5 2.5 %collective-permute-start.13 = (bf16[128,1152]{1,0:T(8,128)(2,1)}, bf16[128,1152]{1,0:T(8,128)(2,1)S(1)}, u32[]{:S(2)}, u32[]{:S(2)}) collective-permute-start(bf16[128,1152]{1,0:T(8,128)(2,1)} %get-tuple-element.35), channel_id=1, source_target_pairs={{0,448},{64,0},{128,64},{192,128},{256,192},{320,256},{384,320},{4... | collective-permute-start | bytes 884744 | tf_op jit(solution)/shard_map/ppermute | solution.py:114
  169.0 3.4 %collective-permute-start.7 = (bf16[128,1152]{1,0:T(8,128)(2,1)}, bf16[128,1152]{1,0:T(8,128)(2,1)S(1)}, u32[]{:S(2)}, u32[]{:S(2)}) collective-permute-start(bf16[128,1152]{1,0:T(8,128)(2,1)} %get-tuple-element.34), channel_id=1, source_target_pairs={{0,64},{64,128},{128,192},{192,256},{256,320},{320,384},{384,448},... | collective-permute-start | bytes 884744 | tf_op jit(solution)/shard_map/ppermute | solution.py:114
  172.3 0.0 collective-permute-done.10
  172.3 1.9 collective-permute-start.8
  174.3 16.3 %collective-permute-done.11 = bf16[128,1152]{1,0:T(8,128)(2,1)} collective-permute-done((bf16[128,1152]{1,0:T(8,128)(2,1)}, bf16[128,1152]{1,0:T(8,128)(2,1)}, u32[]{:S(2)}, u32[]{:S(2)}) %collective-permute-start.11) | collective-permute-done | bytes 294944 | tf_op jit(solution)/shard_map/ppermute | solution.py:114
  190.6 7.1 %collective-permute-start.9 = (bf16[128,1152]{1,0:T(8,128)(2,1)}, bf16[128,1152]{1,0:T(8,128)(2,1)S(1)}, u32[]{:S(2)}, u32[]{:S(2)}) collective-permute-start(bf16[128,1152]{1,0:T(8,128)(2,1)} %get-tuple-element.39), channel_id=1, source_target_pairs={{0,192},{64,256},{128,320},{192,384},{256,448},{320,0},{384,64},{4... | collective-permute-start | bytes 884744 | tf_op jit(solution)/shard_map/ppermute | solution.py:114
  197.7 0.1 reduce-precision_convert_fusion.1
  197.8 2.1 maximum_bitcast_fusion.comb_ref
  199.9 1.7 collective-permute-done.12
  201.6 6.9 %collective-permute-done.13 = bf16[128,1152]{1,0:T(8,128)(2,1)S(1)} collective-permute-done((bf16[128,1152]{1,0:T(8,128)(2,1)}, bf16[128,1152]{1,0:T(8,128)(2,1)S(1)}, u32[]{:S(2)}, u32[]{:S(2)}) %collective-permute-start.13) | collective-permute-done | bytes 294944 | tf_op jit(solution)/shard_map/ppermute | solution.py:114
  208.5 0.0 collective-permute-done.7
  208.5 0.0 collective-permute-done.8
  208.5 8.0 %collective-permute-done.9 = bf16[128,1152]{1,0:T(8,128)(2,1)S(1)} collective-permute-done((bf16[128,1152]{1,0:T(8,128)(2,1)}, bf16[128,1152]{1,0:T(8,128)(2,1)S(1)}, u32[]{:S(2)}, u32[]{:S(2)}) %collective-permute-start.9) | collective-permute-done | bytes 294944 | tf_op jit(solution)/shard_map/ppermute | solution.py:114
  216.5 1.3 fusion.16
  217.8 0.8 copy.70
  218.6 0.8 slice_bitcast_fusion
  219.4 9.2 %all-to-all-done.1 = bf16[64,16,2048]{2,1,0:T(8,128)(2,1)} async-done(((bf16[64,16,2048]{2,1,0:T(8,128)(2,1)}), bf16[64,16,2048]{2,1,0:T(8,128)(2,1)}, u32[]{:S(2)}, u32[]{:S(2)}) %all-to-all-start.1) | async-done | bytes 4194336 | tf_op jit(solution)/shard_map/all_to_all | solution.py:149
  228.6 5.2 %shard_map.102 = (bf16[128,1024]{1,0:T(8,128)(2,1)}, bf16[128,1024]{1,0:T(8,128)(2,1)}, f32[128,1024]{1,0:T(8,128)}) custom-call(bf16[512,1024]{1,0:T(8,128)(2,1)} %maximum_bitcast_fusion.comb_ref, bf16[1024,2048]{1,0:T(8,128)(2,1)} %bitcast.17.back_ref, bf16[128,1024]{1,0:T(8,128)(2,1)} %cot_ref.1), custom_call_target="tpu_custom_call" | custom-call | tf_op jit(solution)/shard_map/pallas_call | solution.py:82
  233.9 1.2 copy.61
  235.1 0.8 select_reduce_fusion.2
  (29 shorter events, 0.6 us)
Async XLA Ops:
  9.9 11.0 %copy-start.1 = (bf16[1,384,128]{2,1,0:T(8,128)(2,1)S(1)}, bf16[1,384,128]{2,1,0:T(8,128)(2,1)}, u32[]{:S(2)}) copy-start(bf16[1,384,128]{2,1,0:T(8,128)(2,1)} %param.10) | copy-start | bytes 294916
  9.9 11.2 %copy-start = (bf16[1,128,768]{2,1,0:T(8,128)(2,1)S(1)}, bf16[1,128,768]{2,1,0:T(8,128)(2,1)}, u32[]{:S(2)}) copy-start(bf16[1,128,768]{2,1,0:T(8,128)(2,1)} %param.9) | copy-start | bytes 589828
  9.9 107.2 %all-to-all-start = ((bf16[64,16,2048]{2,1,0:T(8,128)(2,1)}), bf16[64,16,2048]{2,1,0:T(8,128)(2,1)}, u32[]{:S(2)}, u32[]{:S(2)}) async-start(bf16[64,16,2048]{2,1,0:T(8,128)(2,1)} %bitcast.86), calls=%async_computation | async-start | bytes 8388608 | tf_op jit(solution)/shard_map/all_to_all | solution.py:147
  21.1 25.0 %collective-permute-start = (bf16[128,1152]{1,0:T(8,128)(2,1)S(1)}, bf16[128,1152]{1,0:T(8,128)(2,1)S(1)}, u32[]{:S(2)}, u32[]{:S(2)}) collective-permute-start(bf16[128,1152]{1,0:T(8,128)(2,1)S(1)} %pad_maximum_fusion.1), channel_id=1, source_target_pairs={{0,448},{64,0},{128,64},{192,128},{256,192},{320,256},{384,320},{4... | collective-permute-start | bytes 884744 | tf_op jit(solution)/shard_map/ppermute | solution.py:98
  31.9 23.2 %collective-permute-start.1 = (bf16[128,1152]{1,0:T(8,128)(2,1)S(1)}, bf16[128,1152]{1,0:T(8,128)(2,1)S(1)}, u32[]{:S(2)}, u32[]{:S(2)}) collective-permute-start(bf16[128,1152]{1,0:T(8,128)(2,1)S(1)} %pad_maximum_fusion.1), channel_id=1, source_target_pairs={{0,384},{64,448},{128,0},{192,64},{256,128},{320,192},{384,256},{4... | collective-permute-start | bytes 884744 | tf_op jit(solution)/shard_map/ppermute | solution.py:98
  34.4 48.3 %collective-permute-start.2 = (bf16[128,1152]{1,0:T(8,128)(2,1)S(1)}, bf16[128,1152]{1,0:T(8,128)(2,1)S(1)}, u32[]{:S(2)}, u32[]{:S(2)}) collective-permute-start(bf16[128,1152]{1,0:T(8,128)(2,1)S(1)} %pad_maximum_fusion.1), channel_id=1, source_target_pairs={{0,320},{64,384},{128,448},{192,0},{256,64},{320,128},{384,192},{4... | collective-permute-start | bytes 884744 | tf_op jit(solution)/shard_map/ppermute | solution.py:98
  36.3 46.4 %collective-permute-start.3 = (bf16[128,1152]{1,0:T(8,128)(2,1)S(1)}, bf16[128,1152]{1,0:T(8,128)(2,1)S(1)}, u32[]{:S(2)}, u32[]{:S(2)}) collective-permute-start(bf16[128,1152]{1,0:T(8,128)(2,1)S(1)} %pad_maximum_fusion.1), channel_id=1, source_target_pairs={{0,256},{64,320},{128,384},{192,448},{256,0},{320,64},{384,128},{4... | collective-permute-start | bytes 884744 | tf_op jit(solution)/shard_map/ppermute | solution.py:98
  44.2 39.3 %collective-permute-start.4 = (bf16[128,1152]{1,0:T(8,128)(2,1)S(1)}, bf16[128,1152]{1,0:T(8,128)(2,1)S(1)}, u32[]{:S(2)}, u32[]{:S(2)}) collective-permute-start(bf16[128,1152]{1,0:T(8,128)(2,1)S(1)} %pad_maximum_fusion.1), channel_id=1, source_target_pairs={{0,192},{64,256},{128,320},{192,384},{256,448},{320,0},{384,64},{4... | collective-permute-start | bytes 884744 | tf_op jit(solution)/shard_map/ppermute | solution.py:98
  46.1 42.0 %collective-permute-start.5 = (bf16[128,1152]{1,0:T(8,128)(2,1)S(1)}, bf16[128,1152]{1,0:T(8,128)(2,1)S(1)}, u32[]{:S(2)}, u32[]{:S(2)}) collective-permute-start(bf16[128,1152]{1,0:T(8,128)(2,1)S(1)} %pad_maximum_fusion.1), channel_id=1, source_target_pairs={{0,128},{64,192},{128,256},{192,320},{256,384},{320,448},{384,0},{... | collective-permute-start | bytes 884744 | tf_op jit(solution)/shard_map/ppermute | solution.py:98
  55.1 40.0 %collective-permute-start.6 = (bf16[128,1152]{1,0:T(8,128)(2,1)S(1)}, bf16[128,1152]{1,0:T(8,128)(2,1)S(1)}, u32[]{:S(2)}, u32[]{:S(2)}) collective-permute-start(bf16[128,1152]{1,0:T(8,128)(2,1)S(1)} %pad_maximum_fusion.1), channel_id=1, source_target_pairs={{0,64},{64,128},{128,192},{192,256},{256,320},{320,384},{384,448},... | collective-permute-start | bytes 884744 | tf_op jit(solution)/shard_map/ppermute | solution.py:98
  126.6 6.0 %copy-start.3 = (bf16[1024,384]{1,0:T(8,128)(2,1)S(1)}, bf16[1024,384]{1,0:T(8,128)(2,1)}, u32[]{:S(2)}) copy-start(bf16[1024,384]{1,0:T(8,128)(2,1)} %get-tuple-element.16) | copy-start | bytes 2359300
  126.6 102.0 %all-to-all-start.1 = ((bf16[64,16,2048]{2,1,0:T(8,128)(2,1)}), bf16[64,16,2048]{2,1,0:T(8,128)(2,1)}, u32[]{:S(2)}, u32[]{:S(2)}) async-start(bf16[64,16,2048]{2,1,0:T(8,128)(2,1)} %bitcast.85), calls=%async_computation.1 | async-start | bytes 8388608 | tf_op jit(solution)/shard_map/all_to_all | solution.py:149
  132.5 2.8 %copy-start.2 = (bf16[1024,768]{1,0:T(8,128)(2,1)S(1)}, bf16[1024,768]{1,0:T(8,128)(2,1)}, u32[]{:S(2)}) copy-start(bf16[1024,768]{1,0:T(8,128)(2,1)} %get-tuple-element.15) | copy-start | bytes 4718596
  144.8 27.6 %collective-permute-start.10 = (bf16[128,1152]{1,0:T(8,128)(2,1)}, bf16[128,1152]{1,0:T(8,128)(2,1)}, u32[]{:S(2)}, u32[]{:S(2)}) collective-permute-start(bf16[128,1152]{1,0:T(8,128)(2,1)} %get-tuple-element.38), channel_id=1, source_target_pairs={{0,256},{64,320},{128,384},{192,448},{256,0},{320,64},{384,128},{4... | collective-permute-start | bytes 884744 | tf_op jit(solution)/shard_map/ppermute | solution.py:114
  155.5 35.1 %collective-permute-start.11 = (bf16[128,1152]{1,0:T(8,128)(2,1)}, bf16[128,1152]{1,0:T(8,128)(2,1)}, u32[]{:S(2)}, u32[]{:S(2)}) collective-permute-start(bf16[128,1152]{1,0:T(8,128)(2,1)} %get-tuple-element.37), channel_id=1, source_target_pairs={{0,320},{64,384},{128,448},{192,0},{256,64},{320,128},{384,192},{4... | collective-permute-start | bytes 884744 | tf_op jit(solution)/shard_map/ppermute | solution.py:114
  158.6 43.0 %collective-permute-start.12 = (bf16[128,1152]{1,0:T(8,128)(2,1)}, bf16[128,1152]{1,0:T(8,128)(2,1)S(1)}, u32[]{:S(2)}, u32[]{:S(2)}) collective-permute-start(bf16[128,1152]{1,0:T(8,128)(2,1)} %get-tuple-element.36), channel_id=1, source_target_pairs={{0,384},{64,448},{128,0},{192,64},{256,128},{320,192},{384,256},{4... | collective-permute-start | bytes 884744 | tf_op jit(solution)/shard_map/ppermute | solution.py:114
  166.5 42.0 %collective-permute-start.13 = (bf16[128,1152]{1,0:T(8,128)(2,1)}, bf16[128,1152]{1,0:T(8,128)(2,1)S(1)}, u32[]{:S(2)}, u32[]{:S(2)}) collective-permute-start(bf16[128,1152]{1,0:T(8,128)(2,1)} %get-tuple-element.35), channel_id=1, source_target_pairs={{0,448},{64,0},{128,64},{192,128},{256,192},{320,256},{384,320},{4... | collective-permute-start | bytes 884744 | tf_op jit(solution)/shard_map/ppermute | solution.py:114
  169.0 39.5 %collective-permute-start.7 = (bf16[128,1152]{1,0:T(8,128)(2,1)}, bf16[128,1152]{1,0:T(8,128)(2,1)S(1)}, u32[]{:S(2)}, u32[]{:S(2)}) collective-permute-start(bf16[128,1152]{1,0:T(8,128)(2,1)} %get-tuple-element.34), channel_id=1, source_target_pairs={{0,64},{64,128},{128,192},{192,256},{256,320},{320,384},{384,448},... | collective-permute-start | bytes 884744 | tf_op jit(solution)/shard_map/ppermute | solution.py:114
  172.3 36.2 %collective-permute-start.8 = (bf16[128,1152]{1,0:T(8,128)(2,1)}, bf16[128,1152]{1,0:T(8,128)(2,1)S(1)}, u32[]{:S(2)}, u32[]{:S(2)}) collective-permute-start(bf16[128,1152]{1,0:T(8,128)(2,1)} %get-tuple-element.40), channel_id=1, source_target_pairs={{0,128},{64,192},{128,256},{192,320},{256,384},{320,448},{384,0},{... | collective-permute-start | bytes 884744 | tf_op jit(solution)/shard_map/ppermute | solution.py:114
  190.6 25.9 %collective-permute-start.9 = (bf16[128,1152]{1,0:T(8,128)(2,1)}, bf16[128,1152]{1,0:T(8,128)(2,1)S(1)}, u32[]{:S(2)}, u32[]{:S(2)}) collective-permute-start(bf16[128,1152]{1,0:T(8,128)(2,1)} %get-tuple-element.39), channel_id=1, source_target_pairs={{0,192},{64,256},{128,320},{192,384},{256,448},{320,0},{384,64},{4... | collective-permute-start | bytes 884744 | tf_op jit(solution)/shard_map/ppermute | solution.py:114

commit v10 on v9

--- a/solution.py
+++ b/solution.py
@@ -130,7 +130,13 @@
     onehot = (flat_ids[:, None] == jnp.arange(expert_count, dtype=jnp.int32)[None, :]).astype(
         jnp.int32
     )
-    slot_index = jnp.sum((jnp.cumsum(onehot, axis=0) - onehot) * onehot, axis=1)
+    earlier = lax.broadcasted_iota(jnp.int32, (route_count, route_count), 1) < lax.broadcasted_iota(
+        jnp.int32, (route_count, route_count), 0
+    )
+    before = jnp.dot(
+        earlier.astype(jnp.bfloat16), onehot.astype(jnp.bfloat16), preferred_element_type=jnp.float32
+    ).astype(jnp.int32)
+    slot_index = jnp.sum(before * onehot, axis=1)
     position = (flat_ids * capacity + slot_index).reshape(token_count, top_count)
     slot_range = jnp.arange(slot_count, dtype=jnp.int32)
     hits = position[None, :, :] == slot_range[:, None, None]

time: 237 us -> 235 us (level)
  no operation moved by 1% of the time
where the time goes in v10:
time: 235 us; the launch traced here: 234 us
  waiting for transfers between devices  105 us (45%)
  starting transfers between devices  82.7 us (35%)
  Pallas kernels  14.7 us (6%)
  local copies, waits for them, and re-layouts  10.9 us (5%)
  matrix products  10.7 us (5%)
  other arithmetic  8.95 us (4%)
    ppermute x7, waiting for transfers between devices, gather_dp(): pieces.append(lax.ppermute(block, 'dp', pairs))  43.5 us
    ppermute x7, starting transfers between devices, scatter_dp(): total = total + lax.ppermute(part, 'dp', pairs).astype(jnp.float32)  35.5 us
    ppermute x7, waiting for transfers between devices, scatter_dp(): total = total + lax.ppermute(part, 'dp', pairs).astype(jnp.float32)  32.7 us
    ppermute x7, starting transfers between devices, gather_dp(): pieces.append(lax.ppermute(block, 'dp', pairs))  30.3 us
    all_to_all x1, waiting for transfers between devices, local(): lax.all_to_all(send, 'expert', split_axis=0, concat_axis=0, tiled=True)  20 us
    all_to_all x1, starting transfers between devices, local(): lax.all_to_all(send, 'expert', split_axis=0, concat_axis=0, tiled=True)  11 us
    pallas_call x1, Pallas kernels, expert_call(): pl.pallas_call(kernel, grid=(slots // block,), in_specs=[pl.BlockSpec((bl...  9.5 us
    all_to_all x1, waiting for transfers between devices, local(): lax.all_to_all(payload, 'expert', split_axis=0, concat_axis=0, tiled=True)  9.22 us
  transfers between devices with their start and end apart: 16, of which 11 were waited for; matrix products, arithmetic and copies ran while one was open for 9% of the time, Pallas kernels for 0%

profile of v10, /device:TPU:6, one launch (start us, length us, event | category | flops | bytes accessed | tf_op | source)
XLA Modules:
  0.0 234.5 jit_solution(13445727568127941832)
XLA Ops:
  0.6 0.8 copy.49
  1.4 0.1 eq.36
  1.5 0.3 fusion.12
  1.8 0.1 reduce_sum.39
  2.0 0.1 copy.50
  2.0 0.7 multiply_add_fusion
  2.7 0.4 fusion.4
  3.1 1.0 select_reduce_fusion
  4.1 4.3 %multiply_convert_fusion = bf16[1024,2048]{1,0:T(8,128)(2,1)} fusion(pred[1024,128]{1,0:T(8,128)(4,1)S(1)} %fusion.4, f32[1024]{0:T(1024)S(1)} %get-tuple-element.32, pred[2048]{0:T(1024)(128)(4,1)S(1)} %iota_compare_fusion.4, bf16[128,1024]{1,0:T(8,128)(2,1)} %cot_ref.1, bf16[128,1024]{1,0:T(8,128)(2,1)} %param.6), kind=kOutput, calls=%fused_computation | convolution fusion | flops 544210944 | bytes 4855808 | tf_op jit(solution)/shard_map/dot_general | solution.py:149
  8.4 11.0 %all-to-all-start = ((bf16[64,16,2048]{2,1,0:T(8,128)(2,1)}), bf16[64,16,2048]{2,1,0:T(8,128)(2,1)}, u32[]{:S(2)}, u32[]{:S(2)}) async-start(bf16[64,16,2048]{2,1,0:T(8,128)(2,1)} %bitcast.67), calls=%async_computation | async-start | bytes 8388608 | tf_op jit(solution)/shard_map/all_to_all | solution.py:153
  19.4 0.0 copy-done.1
  19.4 0.1 copy.54
  19.6 0.0 copy-done
  19.6 10.8 %collective-permute-start = (bf16[128,1152]{1,0:T(8,128)(2,1)S(1)}, bf16[128,1152]{1,0:T(8,128)(2,1)S(1)}, u32[]{:S(2)}, u32[]{:S(2)}) collective-permute-start(bf16[128,1152]{1,0:T(8,128)(2,1)S(1)} %pad_maximum_fusion.1), channel_id=1, source_target_pairs={{0,448},{64,0},{128,64},{192,128},{256,192},{320,256},{384,320},{4... | collective-permute-start | bytes 884744 | tf_op jit(solution)/shard_map/ppermute | solution.py:98
  30.5 2.5 %collective-permute-start.1 = (bf16[128,1152]{1,0:T(8,128)(2,1)S(1)}, bf16[128,1152]{1,0:T(8,128)(2,1)S(1)}, u32[]{:S(2)}, u32[]{:S(2)}) collective-permute-start(bf16[128,1152]{1,0:T(8,128)(2,1)S(1)} %pad_maximum_fusion.1), channel_id=1, source_target_pairs={{0,384},{64,448},{128,0},{192,64},{256,128},{320,192},{384,256},{4... | collective-permute-start | bytes 884744 | tf_op jit(solution)/shard_map/ppermute | solution.py:98
  32.9 1.9 collective-permute-start.2
  34.9 7.8 %collective-permute-start.3 = (bf16[128,1152]{1,0:T(8,128)(2,1)S(1)}, bf16[128,1152]{1,0:T(8,128)(2,1)S(1)}, u32[]{:S(2)}, u32[]{:S(2)}) collective-permute-start(bf16[128,1152]{1,0:T(8,128)(2,1)S(1)} %pad_maximum_fusion.1), channel_id=1, source_target_pairs={{0,256},{64,320},{128,384},{192,448},{256,0},{320,64},{384,128},{4... | collective-permute-start | bytes 884744 | tf_op jit(solution)/shard_map/ppermute | solution.py:98
  42.7 1.9 collective-permute-start.4
  44.6 0.0 collective-permute-done
  44.6 3.4 %collective-permute-start.5 = (bf16[128,1152]{1,0:T(8,128)(2,1)S(1)}, bf16[128,1152]{1,0:T(8,128)(2,1)S(1)}, u32[]{:S(2)}, u32[]{:S(2)}) collective-permute-start(bf16[128,1152]{1,0:T(8,128)(2,1)S(1)} %pad_maximum_fusion.1), channel_id=1, source_target_pairs={{0,128},{64,192},{128,256},{192,320},{256,384},{320,448},{384,0},{... | collective-permute-start | bytes 884744 | tf_op jit(solution)/shard_map/ppermute | solution.py:98
  48.1 5.6 %collective-permute-done.1 = bf16[128,1152]{1,0:T(8,128)(2,1)S(1)} collective-permute-done((bf16[128,1152]{1,0:T(8,128)(2,1)S(1)}, bf16[128,1152]{1,0:T(8,128)(2,1)S(1)}, u32[]{:S(2)}, u32[]{:S(2)}) %collective-permute-start.1) | collective-permute-done | bytes 294944 | tf_op jit(solution)/shard_map/ppermute | solution.py:98
  53.7 1.9 collective-permute-start.6
  55.6 25.6 %collective-permute-done.2 = bf16[128,1152]{1,0:T(8,128)(2,1)S(1)} collective-permute-done((bf16[128,1152]{1,0:T(8,128)(2,1)S(1)}, bf16[128,1152]{1,0:T(8,128)(2,1)S(1)}, u32[]{:S(2)}, u32[]{:S(2)}) %collective-permute-start.2) | collective-permute-done | bytes 294944 | tf_op jit(solution)/shard_map/ppermute | solution.py:98
  81.3 0.0 collective-permute-done.3
  81.3 0.7 collective-permute-done.4
  82.0 4.6 %collective-permute-done.5 = bf16[128,1152]{1,0:T(8,128)(2,1)S(1)} collective-permute-done((bf16[128,1152]{1,0:T(8,128)(2,1)S(1)}, bf16[128,1152]{1,0:T(8,128)(2,1)S(1)}, u32[]{:S(2)}, u32[]{:S(2)}) %collective-permute-start.5) | collective-permute-done | bytes 294944 | tf_op jit(solution)/shard_map/ppermute | solution.py:98
  86.6 7.0 %collective-permute-done.6 = bf16[128,1152]{1,0:T(8,128)(2,1)S(1)} collective-permute-done((bf16[128,1152]{1,0:T(8,128)(2,1)S(1)}, bf16[128,1152]{1,0:T(8,128)(2,1)S(1)}, u32[]{:S(2)}, u32[]{:S(2)}) %collective-permute-start.6) | collective-permute-done | bytes 294944 | tf_op jit(solution)/shard_map/ppermute | solution.py:98
  94.0 1.6 constant_dynamic-slice_fusion
  95.7 20.0 %all-to-all-done = bf16[64,16,2048]{2,1,0:T(8,128)(2,1)} async-done(((bf16[64,16,2048]{2,1,0:T(8,128)(2,1)}), bf16[64,16,2048]{2,1,0:T(8,128)(2,1)}, u32[]{:S(2)}, u32[]{:S(2)}) %all-to-all-start) | async-done | bytes 4194336 | tf_op jit(solution)/shard_map/all_to_all | solution.py:153
  115.6 9.5 %shard_map.101 = (bf16[1024,2048]{1,0:T(8,128)(2,1)}, bf16[1024,384]{1,0:T(8,128)(2,1)}, bf16[1024,768]{1,0:T(8,128)(2,1)}) custom-call(bf16[1024,2048]{1,0:T(8,128)(2,1)} %bitcast.2.recv_ref, bf16[1024,1152]{1,0:T(8,128)(2,1)} %bitcast.63), custom_call_target="tpu_custom_call" | custom-call | tf_op jit(solution)/shard_map/pallas_call | solution.py:43
  125.1 5.9 %all-to-all-start.1 = ((bf16[64,16,2048]{2,1,0:T(8,128)(2,1)}), bf16[64,16,2048]{2,1,0:T(8,128)(2,1)}, u32[]{:S(2)}, u32[]{:S(2)}) async-start(bf16[64,16,2048]{2,1,0:T(8,128)(2,1)} %bitcast.66), calls=%async_computation.1 | async-start | bytes 8388608 | tf_op jit(solution)/shard_map/all_to_all | solution.py:155
  131.0 0.0 copy-start.2
  131.1 2.7 %fusion.8 = bf16[1024,384]{0,1:T(8,128)(2,1)S(1)} fusion(bf16[1024,384]{1,0:T(8,128)(2,1)S(1)} %copy-done.3, bf16[1024,2048]{1,0:T(8,128)(2,1)} %bitcast.2.recv_ref), kind=kOutput, calls=%fused_computation.12 | convolution fusion | flops 805699584 | bytes 3670016 | tf_op jit(solution)/shard_map/dot_general | solution.py:160
  133.8 0.0 copy-done.2
  133.8 3.4 %fusion.5 = bf16[1024,768]{0,1:T(8,128)(2,1)S(1)} fusion(bf16[1024,768]{1,0:T(8,128)(2,1)S(1)} %copy-done.2, bf16[1024,2048]{1,0:T(8,128)(2,1)} %bitcast.2.recv_ref), kind=kOutput, calls=%fused_computation.11 | convolution fusion | flops 1611399168 | bytes 5242880 | tf_op jit(solution)/shard_map/dot_general | solution.py:157
  137.3 1.7 pad_maximum_fusion
  139.0 3.0 %copy.65 = bf16[1024,1152]{1,0:T(8,128)(2,1)S(1)} copy(bf16[1024,1152]{0,1:T(8,128)(2,1)} %pad_maximum_fusion) | data formatting | bytes 4718592 | tf_op jit(solution)/shard_map/reshape | solution.py:109
  142.0 1.4 dynamic-slice_bitcast_fusion.6
  143.3 10.7 %collective-permute-start.10 = (bf16[128,1152]{1,0:T(8,128)(2,1)}, bf16[128,1152]{1,0:T(8,128)(2,1)}, u32[]{:S(2)}, u32[]{:S(2)}) collective-permute-start(bf16[128,1152]{1,0:T(8,128)(2,1)} %get-tuple-element.38), channel_id=1, source_target_pairs={{0,256},{64,320},{128,384},{192,448},{256,0},{320,64},{384,128},{4... | collective-permute-start | bytes 884744 | tf_op jit(solution)/shard_map/ppermute | solution.py:114
  154.1 2.1 collective-permute-start.11
  156.2 0.2 copy.53
  156.4 0.2 copy.51
  156.6 0.7 convert_element_type.64
  157.4 7.8 %collective-permute-start.12 = (bf16[128,1152]{1,0:T(8,128)(2,1)}, bf16[128,1152]{1,0:T(8,128)(2,1)S(1)}, u32[]{:S(2)}, u32[]{:S(2)}) collective-permute-start(bf16[128,1152]{1,0:T(8,128)(2,1)} %get-tuple-element.36), channel_id=1, source_target_pairs={{0,384},{64,448},{128,0},{192,64},{256,128},{320,192},{384,256},{4... | collective-permute-start | bytes 884744 | tf_op jit(solution)/shard_map/ppermute | solution.py:114
  165.2 2.5 %collective-permute-start.13 = (bf16[128,1152]{1,0:T(8,128)(2,1)}, bf16[128,1152]{1,0:T(8,128)(2,1)S(1)}, u32[]{:S(2)}, u32[]{:S(2)}) collective-permute-start(bf16[128,1152]{1,0:T(8,128)(2,1)} %get-tuple-element.35), channel_id=1, source_target_pairs={{0,448},{64,0},{128,64},{192,128},{256,192},{320,256},{384,320},{4... | collective-permute-start | bytes 884744 | tf_op jit(solution)/shard_map/ppermute | solution.py:114
  167.7 3.4 %collective-permute-start.7 = (bf16[128,1152]{1,0:T(8,128)(2,1)}, bf16[128,1152]{1,0:T(8,128)(2,1)S(1)}, u32[]{:S(2)}, u32[]{:S(2)}) collective-permute-start(bf16[128,1152]{1,0:T(8,128)(2,1)} %get-tuple-element.34), channel_id=1, source_target_pairs={{0,64},{64,128},{128,192},{192,256},{256,320},{320,384},{384,448},... | collective-permute-start | bytes 884744 | tf_op jit(solution)/shard_map/ppermute | solution.py:114
  171.1 0.0 collective-permute-done.10
  171.1 1.9 collective-permute-start.8
  173.0 16.1 %collective-permute-done.11 = bf16[128,1152]{1,0:T(8,128)(2,1)} collective-permute-done((bf16[128,1152]{1,0:T(8,128)(2,1)}, bf16[128,1152]{1,0:T(8,128)(2,1)}, u32[]{:S(2)}, u32[]{:S(2)}) %collective-permute-start.11) | collective-permute-done | bytes 294944 | tf_op jit(solution)/shard_map/ppermute | solution.py:114
  189.1 7.1 %collective-permute-start.9 = (bf16[128,1152]{1,0:T(8,128)(2,1)}, bf16[128,1152]{1,0:T(8,128)(2,1)S(1)}, u32[]{:S(2)}, u32[]{:S(2)}) collective-permute-start(bf16[128,1152]{1,0:T(8,128)(2,1)} %get-tuple-element.39), channel_id=1, source_target_pairs={{0,192},{64,256},{128,320},{192,384},{256,448},{320,0},{384,64},{4... | collective-permute-start | bytes 884744 | tf_op jit(solution)/shard_map/ppermute | solution.py:114
  196.3 0.1 reduce-precision_convert_fusion.1
  196.4 2.1 maximum_bitcast_fusion.comb_ref
  198.5 1.7 collective-permute-done.12
  200.2 6.9 %collective-permute-done.13 = bf16[128,1152]{1,0:T(8,128)(2,1)S(1)} collective-permute-done((bf16[128,1152]{1,0:T(8,128)(2,1)}, bf16[128,1152]{1,0:T(8,128)(2,1)S(1)}, u32[]{:S(2)}, u32[]{:S(2)}) %collective-permute-start.13) | collective-permute-done | bytes 294944 | tf_op jit(solution)/shard_map/ppermute | solution.py:114
  207.0 0.0 collective-permute-done.7
  207.0 0.0 collective-permute-done.8
  207.1 8.0 %collective-permute-done.9 = bf16[128,1152]{1,0:T(8,128)(2,1)S(1)} collective-permute-done((bf16[128,1152]{1,0:T(8,128)(2,1)}, bf16[128,1152]{1,0:T(8,128)(2,1)S(1)}, u32[]{:S(2)}, u32[]{:S(2)}) %collective-permute-start.9) | collective-permute-done | bytes 294944 | tf_op jit(solution)/shard_map/ppermute | solution.py:114
  215.0 1.3 fusion.18
  216.4 0.8 copy.64
  217.2 0.8 slice_bitcast_fusion
  218.0 9.2 %all-to-all-done.1 = bf16[64,16,2048]{2,1,0:T(8,128)(2,1)} async-done(((bf16[64,16,2048]{2,1,0:T(8,128)(2,1)}), bf16[64,16,2048]{2,1,0:T(8,128)(2,1)}, u32[]{:S(2)}, u32[]{:S(2)}) %all-to-all-start.1) | async-done | bytes 4194336 | tf_op jit(solution)/shard_map/all_to_all | solution.py:155
  227.2 5.2 %shard_map.102 = (bf16[128,1024]{1,0:T(8,128)(2,1)}, bf16[128,1024]{1,0:T(8,128)(2,1)}, f32[128,1024]{1,0:T(8,128)}) custom-call(bf16[512,1024]{1,0:T(8,128)(2,1)} %maximum_bitcast_fusion.comb_ref, bf16[1024,2048]{1,0:T(8,128)(2,1)} %bitcast.16.back_ref, bf16[128,1024]{1,0:T(8,128)(2,1)} %cot_ref.1), custom_call_target="tpu_custom_call" | custom-call | tf_op jit(solution)/shard_map/pallas_call | solution.py:82
  232.4 1.2 copy.55
  233.7 0.8 select_reduce_fusion.2
  (23 shorter events, 0.5 us)
Async XLA Ops:
  8.4 11.0 %copy-start.1 = (bf16[1,384,128]{2,1,0:T(8,128)(2,1)S(1)}, bf16[1,384,128]{2,1,0:T(8,128)(2,1)}, u32[]{:S(2)}) copy-start(bf16[1,384,128]{2,1,0:T(8,128)(2,1)} %param.10) | copy-start | bytes 294916
  8.4 11.2 %copy-start = (bf16[1,128,768]{2,1,0:T(8,128)(2,1)S(1)}, bf16[1,128,768]{2,1,0:T(8,128)(2,1)}, u32[]{:S(2)}) copy-start(bf16[1,128,768]{2,1,0:T(8,128)(2,1)} %param.9) | copy-start | bytes 589828
  8.4 107.2 %all-to-all-start = ((bf16[64,16,2048]{2,1,0:T(8,128)(2,1)}), bf16[64,16,2048]{2,1,0:T(8,128)(2,1)}, u32[]{:S(2)}, u32[]{:S(2)}) async-start(bf16[64,16,2048]{2,1,0:T(8,128)(2,1)} %bitcast.67), calls=%async_computation | async-start | bytes 8388608 | tf_op jit(solution)/shard_map/all_to_all | solution.py:153
  19.6 25.0 %collective-permute-start = (bf16[128,1152]{1,0:T(8,128)(2,1)S(1)}, bf16[128,1152]{1,0:T(8,128)(2,1)S(1)}, u32[]{:S(2)}, u32[]{:S(2)}) collective-permute-start(bf16[128,1152]{1,0:T(8,128)(2,1)S(1)} %pad_maximum_fusion.1), channel_id=1, source_target_pairs={{0,448},{64,0},{128,64},{192,128},{256,192},{320,256},{384,320},{4... | collective-permute-start | bytes 884744 | tf_op jit(solution)/shard_map/ppermute | solution.py:98
  30.5 23.2 %collective-permute-start.1 = (bf16[128,1152]{1,0:T(8,128)(2,1)S(1)}, bf16[128,1152]{1,0:T(8,128)(2,1)S(1)}, u32[]{:S(2)}, u32[]{:S(2)}) collective-permute-start(bf16[128,1152]{1,0:T(8,128)(2,1)S(1)} %pad_maximum_fusion.1), channel_id=1, source_target_pairs={{0,384},{64,448},{128,0},{192,64},{256,128},{320,192},{384,256},{4... | collective-permute-start | bytes 884744 | tf_op jit(solution)/shard_map/ppermute | solution.py:98
  32.9 48.3 %collective-permute-start.2 = (bf16[128,1152]{1,0:T(8,128)(2,1)S(1)}, bf16[128,1152]{1,0:T(8,128)(2,1)S(1)}, u32[]{:S(2)}, u32[]{:S(2)}) collective-permute-start(bf16[128,1152]{1,0:T(8,128)(2,1)S(1)} %pad_maximum_fusion.1), channel_id=1, source_target_pairs={{0,320},{64,384},{128,448},{192,0},{256,64},{320,128},{384,192},{4... | collective-permute-start | bytes 884744 | tf_op jit(solution)/shard_map/ppermute | solution.py:98
  34.9 46.4 %collective-permute-start.3 = (bf16[128,1152]{1,0:T(8,128)(2,1)S(1)}, bf16[128,1152]{1,0:T(8,128)(2,1)S(1)}, u32[]{:S(2)}, u32[]{:S(2)}) collective-permute-start(bf16[128,1152]{1,0:T(8,128)(2,1)S(1)} %pad_maximum_fusion.1), channel_id=1, source_target_pairs={{0,256},{64,320},{128,384},{192,448},{256,0},{320,64},{384,128},{4... | collective-permute-start | bytes 884744 | tf_op jit(solution)/shard_map/ppermute | solution.py:98
  42.7 39.3 %collective-permute-start.4 = (bf16[128,1152]{1,0:T(8,128)(2,1)S(1)}, bf16[128,1152]{1,0:T(8,128)(2,1)S(1)}, u32[]{:S(2)}, u32[]{:S(2)}) collective-permute-start(bf16[128,1152]{1,0:T(8,128)(2,1)S(1)} %pad_maximum_fusion.1), channel_id=1, source_target_pairs={{0,192},{64,256},{128,320},{192,384},{256,448},{320,0},{384,64},{4... | collective-permute-start | bytes 884744 | tf_op jit(solution)/shard_map/ppermute | solution.py:98
  44.6 42.0 %collective-permute-start.5 = (bf16[128,1152]{1,0:T(8,128)(2,1)S(1)}, bf16[128,1152]{1,0:T(8,128)(2,1)S(1)}, u32[]{:S(2)}, u32[]{:S(2)}) collective-permute-start(bf16[128,1152]{1,0:T(8,128)(2,1)S(1)} %pad_maximum_fusion.1), channel_id=1, source_target_pairs={{0,128},{64,192},{128,256},{192,320},{256,384},{320,448},{384,0},{... | collective-permute-start | bytes 884744 | tf_op jit(solution)/shard_map/ppermute | solution.py:98
  53.7 40.0 %collective-permute-start.6 = (bf16[128,1152]{1,0:T(8,128)(2,1)S(1)}, bf16[128,1152]{1,0:T(8,128)(2,1)S(1)}, u32[]{:S(2)}, u32[]{:S(2)}) collective-permute-start(bf16[128,1152]{1,0:T(8,128)(2,1)S(1)} %pad_maximum_fusion.1), channel_id=1, source_target_pairs={{0,64},{64,128},{128,192},{192,256},{256,320},{320,384},{384,448},... | collective-permute-start | bytes 884744 | tf_op jit(solution)/shard_map/ppermute | solution.py:98
  125.1 6.0 %copy-start.3 = (bf16[1024,384]{1,0:T(8,128)(2,1)S(1)}, bf16[1024,384]{1,0:T(8,128)(2,1)}, u32[]{:S(2)}) copy-start(bf16[1024,384]{1,0:T(8,128)(2,1)} %get-tuple-element.16) | copy-start | bytes 2359300
  125.1 102.1 %all-to-all-start.1 = ((bf16[64,16,2048]{2,1,0:T(8,128)(2,1)}), bf16[64,16,2048]{2,1,0:T(8,128)(2,1)}, u32[]{:S(2)}, u32[]{:S(2)}) async-start(bf16[64,16,2048]{2,1,0:T(8,128)(2,1)} %bitcast.66), calls=%async_computation.1 | async-start | bytes 8388608 | tf_op jit(solution)/shard_map/all_to_all | solution.py:155
  131.0 2.8 %copy-start.2 = (bf16[1024,768]{1,0:T(8,128)(2,1)S(1)}, bf16[1024,768]{1,0:T(8,128)(2,1)}, u32[]{:S(2)}) copy-start(bf16[1024,768]{1,0:T(8,128)(2,1)} %get-tuple-element.15) | copy-start | bytes 4718596
  143.3 27.7 %collective-permute-start.10 = (bf16[128,1152]{1,0:T(8,128)(2,1)}, bf16[128,1152]{1,0:T(8,128)(2,1)}, u32[]{:S(2)}, u32[]{:S(2)}) collective-permute-start(bf16[128,1152]{1,0:T(8,128)(2,1)} %get-tuple-element.38), channel_id=1, source_target_pairs={{0,256},{64,320},{128,384},{192,448},{256,0},{320,64},{384,128},{4... | collective-permute-start | bytes 884744 | tf_op jit(solution)/shard_map/ppermute | solution.py:114
  154.1 35.1 %collective-permute-start.11 = (bf16[128,1152]{1,0:T(8,128)(2,1)}, bf16[128,1152]{1,0:T(8,128)(2,1)}, u32[]{:S(2)}, u32[]{:S(2)}) collective-permute-start(bf16[128,1152]{1,0:T(8,128)(2,1)} %get-tuple-element.37), channel_id=1, source_target_pairs={{0,320},{64,384},{128,448},{192,0},{256,64},{320,128},{384,192},{4... | collective-permute-start | bytes 884744 | tf_op jit(solution)/shard_map/ppermute | solution.py:114
  157.4 42.8 %collective-permute-start.12 = (bf16[128,1152]{1,0:T(8,128)(2,1)}, bf16[128,1152]{1,0:T(8,128)(2,1)S(1)}, u32[]{:S(2)}, u32[]{:S(2)}) collective-permute-start(bf16[128,1152]{1,0:T(8,128)(2,1)} %get-tuple-element.36), channel_id=1, source_target_pairs={{0,384},{64,448},{128,0},{192,64},{256,128},{320,192},{384,256},{4... | collective-permute-start | bytes 884744 | tf_op jit(solution)/shard_map/ppermute | solution.py:114
  165.2 41.8 %collective-permute-start.13 = (bf16[128,1152]{1,0:T(8,128)(2,1)}, bf16[128,1152]{1,0:T(8,128)(2,1)S(1)}, u32[]{:S(2)}, u32[]{:S(2)}) collective-permute-start(bf16[128,1152]{1,0:T(8,128)(2,1)} %get-tuple-element.35), channel_id=1, source_target_pairs={{0,448},{64,0},{128,64},{192,128},{256,192},{320,256},{384,320},{4... | collective-permute-start | bytes 884744 | tf_op jit(solution)/shard_map/ppermute | solution.py:114
  167.7 39.4 %collective-permute-start.7 = (bf16[128,1152]{1,0:T(8,128)(2,1)}, bf16[128,1152]{1,0:T(8,128)(2,1)S(1)}, u32[]{:S(2)}, u32[]{:S(2)}) collective-permute-start(bf16[128,1152]{1,0:T(8,128)(2,1)} %get-tuple-element.34), channel_id=1, source_target_pairs={{0,64},{64,128},{128,192},{192,256},{256,320},{320,384},{384,448},... | collective-permute-start | bytes 884744 | tf_op jit(solution)/shard_map/ppermute | solution.py:114
  171.1 36.0 %collective-permute-start.8 = (bf16[128,1152]{1,0:T(8,128)(2,1)}, bf16[128,1152]{1,0:T(8,128)(2,1)S(1)}, u32[]{:S(2)}, u32[]{:S(2)}) collective-permute-start(bf16[128,1152]{1,0:T(8,128)(2,1)} %get-tuple-element.40), channel_id=1, source_target_pairs={{0,128},{64,192},{128,256},{192,320},{256,384},{320,448},{384,0},{... | collective-permute-start | bytes 884744 | tf_op jit(solution)/shard_map/ppermute | solution.py:114
  189.1 25.9 %collective-permute-start.9 = (bf16[128,1152]{1,0:T(8,128)(2,1)}, bf16[128,1152]{1,0:T(8,128)(2,1)S(1)}, u32[]{:S(2)}, u32[]{:S(2)}) collective-permute-start(bf16[128,1152]{1,0:T(8,128)(2,1)} %get-tuple-element.39), channel_id=1, source_target_pairs={{0,192},{64,256},{128,320},{192,384},{256,448},{320,0},{384,64},{4... | collective-permute-start | bytes 884744 | tf_op jit(solution)/shard_map/ppermute | solution.py:114
